TPU v7x, 32 devices: a whole 2x2x4 slice. The times are simulated.
32 devices in a mesh: uv: 8 (over z, y), rep: 4 (over x, core).
Axes of the slice: x: 2, y: 2, z: 4, core: 2. Of those that a mesh axis runs over, the one named last changes fastest.
Arguments:
- visibilities: float32 [2, 32, 8, 16, 12], P(None, ('uv', 'rep')), may hold values from -6 to 6
- tile_counts: int32 [32, 8, 16], P(('uv', 'rep')), may hold values from 2 to 12, as said below
- w_plane: int32 [32, 8, 16, 12], P(('uv', 'rep')), may hold values from 0 to 63
- u_offset: int32 [32, 8, 16, 12], P(('uv', 'rep')), may hold values from 0 to 120
- v_offset: int32 [32, 8, 16, 12], P(('uv', 'rep')), may hold values from 0 to 120
- kernels: float32 [64, 128], replicated, may hold values from -2.5 to 2.5
Outputs:
- spectrum: float32 [2048, 2, 1024], P(('uv', 'rep'))
Inputs may be any that keep to these rules, and one draw needn't show every extreme that they name: `tile_counts`: every source device's list for tile 16//2 of destination column 4 holds 12 visibilities; tiles near the grid's centre are fuller than others.
All inputs are finite; a program needn't handle non-finite values.
Results may differ from a plain program's by a relative error of at most 0.0029.
Values may be sent and summed in bfloat16 or wider, within the bound.
No kernel may reach another device: no remote copies, remote signals or barrier semaphores. Data moves between devices by JAX's collectives and lax.ppermute only.
A program may use at most 192 MiB of HBM per device.

v0:
```python
import math

import jax
import jax.numpy as jnp
from jax import lax
from jax.sharding import PartitionSpec as P

TILE = 128
SUPPORT = 8


def weigh(vis_re, vis_im, planes, kernels):
    nplanes = kernels.shape[0]
    width = kernels.shape[1]
    half = width // 2
    onehot = (
        planes[..., None] == lax.broadcasted_iota(jnp.int32, planes.shape + (nplanes,), planes.ndim)
    ).astype(jnp.float32)
    kern = jnp.dot(
        onehot.reshape(-1, nplanes),
        kernels,
        precision=lax.Precision.HIGHEST,
        preferred_element_type=jnp.float32,
    )
    kern = kern.reshape(planes.shape + (width,))
    kern_re = kern[..., :half]
    kern_im = kern[..., half:]
    part_re = vis_re[..., None] * kern_re - vis_im[..., None] * kern_im
    part_im = vis_re[..., None] * kern_im + vis_im[..., None] * kern_re
    return jnp.concatenate([part_re, part_im], axis=-1).astype(jnp.bfloat16)


def grid_tiles(weighted, row_start, col_start):
    senders = weighted.shape[0]
    ntiles = weighted.shape[1]
    slots = weighted.shape[2]
    count = senders * slots
    per_tile = jnp.moveaxis(weighted, 1, 0).reshape(ntiles, count, 2, SUPPORT, SUPPORT)
    rows_all = jnp.moveaxis(row_start, 1, 0).reshape(ntiles, count)
    cols_all = jnp.moveaxis(col_start, 1, 0).reshape(ntiles, count)
    lanes = lax.broadcasted_iota(jnp.int32, (1, SUPPORT, TILE), 2)
    taps = lax.broadcasted_iota(jnp.int32, (1, SUPPORT, TILE), 1)
    cells = lax.broadcasted_iota(jnp.int32, (TILE, 1, SUPPORT), 0)
    taps_row = lax.broadcasted_iota(jnp.int32, (TILE, 1, SUPPORT), 2)

    def one_tile(operands):
        values, row_first, col_first = operands
        place = (lanes == col_first[:, None, None] + taps).astype(jnp.bfloat16)
        spread = jnp.einsum("ncij,njb->nicb", values, place)
        spread = spread.reshape(count * SUPPORT, 2 * TILE)
        pick = (cells == row_first[None, :, None] + taps_row).astype(jnp.bfloat16)
        pick = pick.reshape(TILE, count * SUPPORT)
        summed = jnp.dot(pick, spread, preferred_element_type=jnp.float32)
        return summed.reshape(TILE, 2, TILE)

    return lax.map(one_tile, (per_tile, rows_all, cols_all))


def make_table(first, second, length):
    index_a = lax.broadcasted_iota(jnp.int32, (first, second), 0)
    index_b = lax.broadcasted_iota(jnp.int32, (first, second), 1)
    angle = 2.0 * math.pi / length * (index_a * index_b % length).astype(jnp.float32)
    return (jnp.cos(angle), jnp.sin(angle))


def transform(pencil):
    nrows = pencil.shape[0]
    groups = lax.axis_size("uv")
    total = pencil.shape[2]
    width = total // groups
    highest = lax.Precision.HIGHEST
    cos_a, sin_a = make_table(groups, groups, groups)
    cos_t, sin_t = make_table(groups, width, total)
    cos_b, sin_b = make_table(width, width, width)
    field = pencil.reshape(nrows, 2, groups, width)
    real_in = field[:, 0]
    imag_in = field[:, 1]
    first_re = jnp.einsum("rpj,pk->rkj", real_in, cos_a, precision=highest) + jnp.einsum(
        "rpj,pk->rkj", imag_in, sin_a, precision=highest
    )
    first_im = jnp.einsum("rpj,pk->rkj", imag_in, cos_a, precision=highest) - jnp.einsum(
        "rpj,pk->rkj", real_in, sin_a, precision=highest
    )
    turned_re = first_re * cos_t + first_im * sin_t
    turned_im = first_im * cos_t - first_re * sin_t
    final_re = jnp.einsum("rkj,jm->rmk", turned_re, cos_b, precision=highest) + jnp.einsum(
        "rkj,jm->rmk", turned_im, sin_b, precision=highest
    )
    final_im = jnp.einsum("rkj,jm->rmk", turned_im, cos_b, precision=highest) - jnp.einsum(
        "rkj,jm->rmk", turned_re, sin_b, precision=highest
    )
    scale = 1.0 / math.sqrt(total)
    return (
        jnp.stack([final_re.reshape(nrows, total), final_im.reshape(nrows, total)], axis=1) * scale
    )


def shards(visibilities, tile_counts, w_plane, u_offset, v_offset, kernels):
    dests = visibilities.shape[2]
    ntiles = visibilities.shape[3]
    slots = visibilities.shape[4]
    nuv = lax.axis_size("uv")
    nrep = lax.axis_size("rep")
    per_device = ntiles * TILE // (nuv * nrep)
    live = (
        lax.broadcasted_iota(jnp.int32, (dests, ntiles, slots), 2) < tile_counts[0][:, :, None]
    ).astype(jnp.float32)
    vis_re = visibilities[0, 0] * live
    vis_im = visibilities[1, 0] * live
    weighted = weigh(vis_re, vis_im, w_plane[0], kernels)
    slab = grid_tiles(
        lax.all_to_all(weighted, "uv", split_axis=0, concat_axis=0, tiled=True),
        lax.all_to_all(u_offset[0], "uv", split_axis=0, concat_axis=0, tiled=True),
        lax.all_to_all(v_offset[0], "uv", split_axis=0, concat_axis=0, tiled=True),
    )
    blocks = slab.reshape(nuv, nrep, per_device, 2, TILE)
    moved_rows = lax.all_to_all(blocks, "uv", split_axis=0, concat_axis=4, tiled=True)
    pencil = lax.psum_scatter(moved_rows, "rep", scatter_dimension=1, tiled=True)
    pencil = pencil.reshape(per_device, 2, nuv * TILE)
    return transform(pencil)


def solution(mesh):
    placed = (
        P(None, ("uv", "rep"), None, None, None),
        P(("uv", "rep"), None, None),
        P(("uv", "rep"), None, None, None),
        P(("uv", "rep"), None, None, None),
        P(("uv", "rep"), None, None, None),
        P(),
    )
    return jax.shard_map(
        shards, mesh=mesh, in_specs=placed, out_specs=P(("uv", "rep"), None, None), check_vma=False
    )
```

profile of v0, /device:TPU:0, one launch (start us, length us, event | category | flops | bytes accessed | tf_op | source)
XLA Modules:
  0.0 184.7 jit_solution(3883717939173195149)
XLA Ops:
  8.1 7.3 %all-to-all-start = ((s32[8,1,192]{2,1,0:T(1,128)}), s32[8,1,192]{2,1,0:T(1,128)S(1)}, u32[]{:S(2)}, u32[]{:S(2)}) async-start(s32[8,1,192]{2,1,0:T(1,128)} %reshape.171), calls=%async_computation | async-start | bytes 16384 | tf_op jit(solution)/shard_map/all_to_all | solution.py:113
  19.3 2.6 %all-to-all-done = s32[8,1,192]{2,1,0:T(1,128)S(1)} async-done(((s32[8,1,192]{2,1,0:T(1,128)}), s32[8,1,192]{2,1,0:T(1,128)S(1)}, u32[]{:S(2)}, u32[]{:S(2)}) %all-to-all-start) | async-done | bytes 6176 | tf_op jit(solution)/shard_map/all_to_all | solution.py:113
  21.8 3.4 %all-to-all-start.1 = ((s32[8,1,192]{2,1,0:T(1,128)}), s32[8,1,192]{2,1,0:T(1,128)S(1)}, u32[]{:S(2)}, u32[]{:S(2)}) async-start(s32[8,1,192]{2,1,0:T(1,128)} %reshape.173), calls=%async_computation.1 | async-start | bytes 16384 | tf_op jit(solution)/shard_map/all_to_all | solution.py:114
  26.2 5.5 %all-to-all-done.1 = s32[8,1,192]{2,1,0:T(1,128)S(1)} async-done(((s32[8,1,192]{2,1,0:T(1,128)}), s32[8,1,192]{2,1,0:T(1,128)S(1)}, u32[]{:S(2)}, u32[]{:S(2)}) %all-to-all-start.1) | async-done | bytes 6176 | tf_op jit(solution)/shard_map/all_to_all | solution.py:114
  31.8 3.5 %all-to-all-start.2 = ((bf16[8,16,12,128]{3,1,2,0:T(8,128)(2,1)}), bf16[8,16,12,128]{3,1,2,0:T(8,128)(2,1)S(1)}, u32[]{:S(2)}, u32[]{:S(2)}) async-start(bf16[8,16,12,128]{3,1,2,0:T(8,128)(2,1)} %pad_maximum_fusion), calls=%async_computation.2 | async-start | bytes 786432 | tf_op jit(solution)/shard_map/all_to_all | solution.py:112
  37.6 7.5 %all-to-all-done.2 = bf16[8,16,12,128]{3,1,2,0:T(8,128)(2,1)S(1)} async-done(((bf16[8,16,12,128]{3,1,2,0:T(8,128)(2,1)}), bf16[8,16,12,128]{3,1,2,0:T(8,128)(2,1)S(1)}, u32[]{:S(2)}, u32[]{:S(2)}) %all-to-all-start.2) | async-done | bytes 393248 | tf_op jit(solution)/shard_map/all_to_all | solution.py:112
  45.3 8.5 %reshape.170 = bf16[16,96,2,8,8]{4,3,2,1,0:T(8,128)(2,1)} reshape(bf16[16,8,12,128]{3,2,1,0:T(8,128)(2,1)S(1)} %copy.99) | data formatting | bytes 786432
  53.7 31.8 %while.13 = (s32[]{:T(128)}, f32[16,128,2,128]{3,1,0,2:T(8,128)S(1)}, s32[16,96]{1,0:T(8,128)S(1)}, s32[16,96]{1,0:T(8,128)S(1)}, bf16[16,96,2,8,8]{4,3,2,1,0:T(8,128)(2,1)}, /*index=5*/s32[]{:T(128)}) while((s32[]{:T(128)}, f32[16,128,2,128]{3,1,0,2:T(8,128)S(1)}, s32[16,96]{1,0:T(8,128)S(1)}, s32[16,96]{1,0:T(8,128)S(1)}, ...), condition=%wide.region_1.2_spmd.clone.clone, body=%wide.region_0.1_spmd.clone.clone.sunk | while | flops 53773056 | bytes 2113357 | solution.py:56
  55.7 1.3 convolution_bitcast_fusion.3
  57.7 1.3 convolution_bitcast_fusion.3
  59.7 1.3 convolution_bitcast_fusion.3
  61.7 1.3 convolution_bitcast_fusion.3
  63.7 1.3 convolution_bitcast_fusion.3
  65.7 1.3 convolution_bitcast_fusion.3
  67.7 1.3 convolution_bitcast_fusion.3
  69.6 1.3 convolution_bitcast_fusion.3
  71.6 1.3 convolution_bitcast_fusion.3
  73.6 1.3 convolution_bitcast_fusion.3
  75.6 1.3 convolution_bitcast_fusion.3
  77.6 1.3 convolution_bitcast_fusion.3
  79.6 1.3 convolution_bitcast_fusion.3
  85.8 50.9 %all_to_all.33 = f32[8,4,64,2,128]{4,2,1,3,0:T(8,128)S(1)} all-to-all(f32[8,4,64,2,128]{4,2,1,3,0:T(8,128)S(1)} %copy.83), channel_id=1, replica_groups=mesh['uv'=8,'rep'=4] {'uv'}, dimensions={0} | all-to-all | bytes 4194304 | tf_op jit(solution)/shard_map/all_to_all | solution.py:117
  137.9 2.0 %copy.85 = f32[1,4,64,2,1024]{4,2,3,0,1:T(8,128)} copy(f32[1,4,64,2,1024]{4,0,3,2,1:T(1,128)S(1)} %bitcast.143) | data formatting | bytes 4194304 | tf_op jit(solution)/shard_map/all_to_all | solution.py:117
  139.9 30.4 %reduce-scatter.2.cloned.1.call-done = f32[1,1,64,2,1024]{4,2,3,0,1:T(8,128)} async-done(((f32[1,4,64,2,1024]{4,2,3,0,1:T(8,128)}), f32[1,1,64,2,1024]{4,2,3,0,1:T(8,128)}) %reduce-scatter.2.cloned.1.call-update) | async-done | bytes 524304 | tf_op jit(solution)/shard_map/reduce_scatter | solution.py:118
  (131 shorter events, 31.8 us)
Async XLA Ops:
  6.5 10.5 %copy-start = (f32[64,128]{1,0:T(8,128)S(1)}, f32[64,128]{1,0:T(8,128)}, u32[]{:S(2)}) copy-start(f32[64,128]{1,0:T(8,128)} %param.13) | copy-start | bytes 98308
  6.5 12.0 %copy-start.1 = (s32[1,8,16,12]{2,1,3,0:T(8,128)S(1)}, s32[1,8,16,12]{2,1,3,0:T(8,128)}, u32[]{:S(2)}) copy-start(s32[1,8,16,12]{2,1,3,0:T(8,128)} %param.12) | copy-start | bytes 18436
  8.1 13.8 %all-to-all-start = ((s32[8,1,192]{2,1,0:T(1,128)}), s32[8,1,192]{2,1,0:T(1,128)S(1)}, u32[]{:S(2)}, u32[]{:S(2)}) async-start(s32[8,1,192]{2,1,0:T(1,128)} %reshape.171), calls=%async_computation | async-start | bytes 16384 | tf_op jit(solution)/shard_map/all_to_all | solution.py:113
  21.8 9.9 %all-to-all-start.1 = ((s32[8,1,192]{2,1,0:T(1,128)}), s32[8,1,192]{2,1,0:T(1,128)S(1)}, u32[]{:S(2)}, u32[]{:S(2)}) async-start(s32[8,1,192]{2,1,0:T(1,128)} %reshape.173), calls=%async_computation.1 | async-start | bytes 16384 | tf_op jit(solution)/shard_map/all_to_all | solution.py:114
  31.8 13.4 %all-to-all-start.2 = ((bf16[8,16,12,128]{3,1,2,0:T(8,128)(2,1)}), bf16[8,16,12,128]{3,1,2,0:T(8,128)(2,1)S(1)}, u32[]{:S(2)}, u32[]{:S(2)}) async-start(bf16[8,16,12,128]{3,1,2,0:T(8,128)(2,1)} %pad_maximum_fusion), calls=%async_computation.2 | async-start | bytes 786432 | tf_op jit(solution)/shard_map/all_to_all | solution.py:112
  35.2 135.1 %reduce-scatter.2.cloned.1.call-start = ((), (), s32[]{:S(2)}) async-start(), calls=%async_computation.5 | async-start | bytes 2621440 | tf_op jit(solution)/shard_map/reduce_scatter | solution.py:118
Sparse Core Ops, SparseCore 0:
  140.0 30.3 reduce-scatter.1
where the time goes:
time: 186 us; the launch traced here: 185 us
  blocking collectives  50.9 us (27%)
  waiting for transfers between devices  46.1 us (25%)
  matrix products  30.6 us (16%)
  local copies, waits for them, and re-layouts  23.5 us (13%)
  starting transfers between devices  14.2 us (8%)
  between operations  13.7 us (7%)
  other arithmetic  5.16 us (3%)
    all_to_all x1, blocking collectives, shards(): lax.all_to_all(blocks, 'uv', split_axis=0, concat_axis=4, tiled=True)  50.9 us
    reduce_scatter x1, waiting for transfers between devices, shards(): lax.psum_scatter(moved_rows, 'rep', scatter_dimension=1, tiled=True)  30.4 us
    dot_general x16, matrix products, one_tile(): spread = jnp.einsum('ncij,njb->nicb', values, place)  20.9 us
    unnamed x13, local copies, waits for them, and re-layouts  12.1 us
    all_to_all x1, waiting for transfers between devices, shards(): lax.all_to_all(weighted, 'uv', split_axis=0, concat_axis=0, tiled=True)  7.5 us
    all_to_all x1, starting transfers between devices, shards(): lax.all_to_all(u_offset[0], 'uv', split_axis=0, concat_axis=0, tiled=True)  7.28 us
    all_to_all x1, waiting for transfers between devices, shards(): lax.all_to_all(v_offset[0], 'uv', split_axis=0, concat_axis=0, tiled=True)  5.54 us
    dot_general x16, matrix products, one_tile(): summed = jnp.dot(pick, spread, preferred_element_type=jnp.float32)  4.67 us
  transfers between devices with their start and end apart: 4, of which 4 were waited for; matrix products, arithmetic and copies ran while one was open for 4% of the time, Pallas kernels for 0%

commit v1 on v0

v1 whole, which is shorter than its diff:
```python
import functools
import math

import jax
import jax.numpy as jnp
from jax import lax
from jax.experimental import pallas as pl
from jax.experimental.pallas import tpu as pltpu
from jax.sharding import PartitionSpec as P

TILE = 128
SUPPORT = 8
GROUP = 16
FIELDS = 5


def make_table(first, second, length):
    index_a = lax.broadcasted_iota(jnp.int32, (first, second), 0)
    index_b = lax.broadcasted_iota(jnp.int32, (first, second), 1)
    angle = 2.0 * math.pi / length * (index_a * index_b % length).astype(jnp.float32)
    return (jnp.cos(angle), jnp.sin(angle))


def transform(real_in, imag_in, groups):
    nrows = real_in.shape[0]
    total = real_in.shape[1]
    width = total // groups
    highest = lax.Precision.HIGHEST
    cos_a, sin_a = make_table(groups, groups, groups)
    cos_t, sin_t = make_table(groups, width, total)
    cos_b, sin_b = make_table(width, width, width)
    real_in = real_in.reshape(nrows, groups, width)
    imag_in = imag_in.reshape(nrows, groups, width)
    first_re = jnp.einsum("rpj,pk->rkj", real_in, cos_a, precision=highest) + jnp.einsum(
        "rpj,pk->rkj", imag_in, sin_a, precision=highest
    )
    first_im = jnp.einsum("rpj,pk->rkj", imag_in, cos_a, precision=highest) - jnp.einsum(
        "rpj,pk->rkj", real_in, sin_a, precision=highest
    )
    turned_re = first_re * cos_t + first_im * sin_t
    turned_im = first_im * cos_t - first_re * sin_t
    final_re = jnp.einsum("rkj,jm->rmk", turned_re, cos_b, precision=highest) + jnp.einsum(
        "rkj,jm->rmk", turned_im, sin_b, precision=highest
    )
    final_im = jnp.einsum("rkj,jm->rmk", turned_im, cos_b, precision=highest) - jnp.einsum(
        "rkj,jm->rmk", turned_re, sin_b, precision=highest
    )
    scale = 1.0 / math.sqrt(total)
    return (
        jnp.stack([final_re.reshape(nrows, total), final_im.reshape(nrows, total)], axis=1) * scale
    )


def weigh(vis_re, vis_im, planes, kernels):
    nplanes = kernels.shape[0]
    width = kernels.shape[1]
    half = width // 2
    onehot = (
        planes[..., None] == lax.broadcasted_iota(jnp.int32, planes.shape + (nplanes,), planes.ndim)
    ).astype(jnp.float32)
    kern = jnp.dot(
        onehot.reshape(-1, nplanes),
        kernels,
        precision=lax.Precision.HIGHEST,
        preferred_element_type=jnp.float32,
    )
    kern = kern.reshape(planes.shape + (width,))
    kern_re = kern[..., :half]
    kern_im = kern[..., half:]
    part_re = vis_re[..., None] * kern_re - vis_im[..., None] * kern_im
    part_im = vis_re[..., None] * kern_im + vis_im[..., None] * kern_re
    return jnp.concatenate([part_re, part_im], axis=-1).astype(jnp.bfloat16)


def grid_kernel(w_ref, vob_ref, uoa_ref, e_ref, out_ref, rep_ref):
    chunk_step = pl.program_id(1)
    chunk = w_ref.shape[1]
    rows = out_ref.shape[1]
    ngroups = chunk // GROUP
    nblocks = w_ref.shape[2] // SUPPORT

    @pl.when(chunk_step == 0)
    def _():
        out_ref[...] = jnp.zeros_like(out_ref)

    rep_ref[...] = jnp.dot(
        w_ref[0], e_ref[...], preferred_element_type=jnp.float32
    ).astype(jnp.bfloat16)
    lane = lax.broadcasted_iota(jnp.int32, (GROUP, TILE), 1)
    row = lax.broadcasted_iota(jnp.int32, (GROUP, TILE), 0)
    keep = (lane // SUPPORT) == row
    vrow = lax.broadcasted_iota(jnp.int32, (TILE, TILE), 0)
    urow = lax.broadcasted_iota(jnp.int32, (rows, TILE), 0)
    zero = jnp.zeros((GROUP, TILE), jnp.bfloat16)

    def body(g, acc):
        start = pl.multiple_of(g * GROUP, GROUP)
        blocks = [
            jnp.where(keep, rep_ref[pl.ds(start, GROUP), pl.ds(i * TILE, TILE)], zero)
            for i in range(nblocks)
        ]
        wbd = jnp.concatenate(blocks, axis=0)
        vob = vob_ref[0, pl.ds(g, 1), :]
        cst = (vrow == vob).astype(jnp.bfloat16)
        spread = lax.dot_general(
            wbd, cst, (((1,), (1,)), ((), ())), preferred_element_type=jnp.float32
        ).astype(jnp.bfloat16)
        uoa = uoa_ref[0, pl.ds(g, 1), :]
        pick = (urow == uoa).astype(jnp.bfloat16)
        half = spread.shape[0] // 2
        acc_re = acc[0] + jnp.dot(pick, spread[:half], preferred_element_type=jnp.float32)
        acc_im = acc[1] + jnp.dot(pick, spread[half:], preferred_element_type=jnp.float32)
        return (acc_re, acc_im)

    init = (jnp.zeros((rows, TILE), jnp.float32), jnp.zeros((rows, TILE), jnp.float32))
    acc_re, acc_im = lax.fori_loop(0, ngroups, body, init)
    out_ref[0] += acc_re
    out_ref[1] += acc_im


def grid_rows(weighted, vob, uoa, rows):
    dests, per_dest, width = weighted.shape
    chunk = per_dest
    for size in (384, 192, 96, 48, 16):
        if per_dest % size == 0 and size <= per_dest:
            chunk = size
            break
    steps = per_dest // chunk
    nblocks = width // SUPPORT
    lanes_in = lax.broadcasted_iota(jnp.int32, (width, nblocks * TILE), 0)
    lanes_out = lax.broadcasted_iota(jnp.int32, (width, nblocks * TILE), 1)
    expand = (
        (lanes_in // SUPPORT == lanes_out // TILE) & (lanes_in % SUPPORT == lanes_out % SUPPORT)
    ).astype(jnp.bfloat16)
    return pl.pallas_call(
        grid_kernel,
        grid=(dests, steps),
        in_specs=[
            pl.BlockSpec((1, chunk, width), lambda d, c: (d, c, 0)),
            pl.BlockSpec((1, chunk // GROUP, TILE), lambda d, c: (d, c, 0)),
            pl.BlockSpec((1, chunk // GROUP, TILE), lambda d, c: (d, c, 0)),
            pl.BlockSpec((width, nblocks * TILE), lambda d, c: (0, 0)),
        ],
        out_specs=pl.BlockSpec((2, rows, TILE), lambda d, c: (0, 0, d)),
        out_shape=jax.ShapeDtypeStruct((2, rows, dests * TILE), jnp.float32),
        scratch_shapes=[pltpu.VMEM((chunk, nblocks * TILE), jnp.bfloat16)],
        compiler_params=pltpu.CompilerParams(
            dimension_semantics=("arbitrary", "arbitrary")
        ),
    )(weighted, vob, uoa, expand)


def shards(visibilities, tile_counts, w_plane, u_offset, v_offset, kernels):
    dests = visibilities.shape[2]
    ntiles = visibilities.shape[3]
    slots = visibilities.shape[4]
    axes = ("uv", "rep")
    ndev = lax.axis_size(axes)
    rows = ntiles * TILE // ndev
    per_tile = ndev // ntiles
    me = lax.axis_index(axes)
    live = (
        lax.broadcasted_iota(jnp.int32, (dests, ntiles, slots), 2) < tile_counts[0][:, :, None]
    ).astype(jnp.float32)
    fields = jnp.stack(
        [
            visibilities[0, 0] * live,
            visibilities[1, 0] * live,
            w_plane[0].astype(jnp.float32),
            u_offset[0].astype(jnp.float32),
            v_offset[0].astype(jnp.float32),
        ]
    )
    send = jnp.repeat(fields, per_tile, axis=2)
    send = jnp.moveaxis(send, 2, 0)
    got = lax.all_to_all(send, axes, split_axis=0, concat_axis=0, tiled=True)
    got = jnp.moveaxis(got, 0, 2).reshape(FIELDS, dests, ndev * slots)
    vis_re = got[0]
    vis_im = got[1]
    planes = got[2].astype(jnp.int32)
    rows_first = got[3].astype(jnp.int32)
    cols_first = got[4].astype(jnp.int32)
    if vis_re.size <= 65536:
        weighted = weigh(vis_re, vis_im, planes, kernels)
    else:
        weighted = lax.map(lambda x: weigh(x[0], x[1], x[2], kernels), (vis_re, vis_im, planes))
    per_dest = ndev * slots
    ngroups = per_dest // GROUP
    taps = jnp.arange(SUPPORT, dtype=jnp.int32)
    vob = (cols_first.reshape(dests, ngroups, GROUP, 1) + taps).reshape(dests, ngroups, TILE)
    offset = (me % per_tile) * rows
    uoa = (rows_first.reshape(dests, ngroups, 1, GROUP) + taps[:, None] - offset).reshape(
        dests, ngroups, TILE
    )
    slab = grid_rows(weighted, vob, uoa, rows)
    return transform(slab[0], slab[1], dests)


def solution(mesh):
    placed = (
        P(None, ("uv", "rep"), None, None, None),
        P(("uv", "rep"), None, None),
        P(("uv", "rep"), None, None, None),
        P(("uv", "rep"), None, None, None),
        P(("uv", "rep"), None, None, None),
        P(),
    )
    return jax.shard_map(
        shards, mesh=mesh, in_specs=placed, out_specs=P(("uv", "rep"), None, None), check_vma=False
    )
```

time: 186 us -> 103 us (0.55)
  Pallas kernels: 0 us -> 65.5 us
  blocking collectives: 50.9 us -> 0 us
  waiting for transfers between devices: 46.1 us -> 6.04 us
  matrix products: 30.6 us -> 5.59 us
  local copies, waits for them, and re-layouts: 23.5 us -> 7.9 us
  between operations: 13.7 us -> 0.27 us
  starting transfers between devices: 14.2 us -> 7.3 us
  other arithmetic: 5.16 us -> 9.47 us
    pallas_call x0 -> x1, Pallas kernels: none -> 65.5 us  [grid_rows(): pl.pallas_call(grid_kernel, grid=(dests, steps), in_specs=[pl.BlockSpec((...]
    all_to_all x1 -> x0, blocking collectives: 50.9 us -> none  [shards(): lax.all_to_all(blocks, 'uv', split_axis=0, concat_axis=4, tiled=True)]
    reduce_scatter x1 -> x0, waiting for transfers between devices: 30.4 us -> none  [shards(): lax.psum_scatter(moved_rows, 'rep', scatter_dimension=1, tiled=True)]
    dot_general x32 -> x0, matrix products: 25.6 us -> none  [the longest x16 20.9 us: one_tile(): spread = jnp.einsum('ncij,njb->nicb', values, place)]
    all_to_all x3 -> x1, waiting for transfers between devices: 15.6 us -> 6.04 us  [shards(): got = lax.all_to_all(send, axes, split_axis=0, concat_axis=0, tiled=True)]
    unnamed x13 -> x7, local copies, waits for them, and re-layouts: 12.1 us -> 2.66 us
    all_to_all x3 -> x1, starting transfers between devices: 14.2 us -> 7.3 us  [shards(): got = lax.all_to_all(send, axes, split_axis=0, concat_axis=0, tiled=True)]
    unnamed x0 -> x4, other arithmetic: none -> 3.23 us
  transfers between devices with their start and end apart: 4 -> 1, of which waited for: 4 -> 1; matrix products, arithmetic and copies ran while one was open for 4% -> 1% of each run, Pallas kernels for 0% -> 0%
where the time goes in v1:
time: 103 us; the launch traced here: 102 us
  Pallas kernels  65.5 us (64%)
  other arithmetic  9.47 us (9%)
  local copies, waits for them, and re-layouts  7.9 us (8%)
  starting transfers between devices  7.3 us (7%)
  waiting for transfers between devices  6.04 us (6%)
  matrix products  5.59 us (5%)
    pallas_call x1, Pallas kernels, grid_rows(): pl.pallas_call(grid_kernel, grid=(dests, steps), in_specs=[pl.BlockSpec((...  65.5 us
    all_to_all x1, starting transfers between devices, shards(): got = lax.all_to_all(send, axes, split_axis=0, concat_axis=0, tiled=True)  7.3 us
    all_to_all x1, waiting for transfers between devices, shards(): got = lax.all_to_all(send, axes, split_axis=0, concat_axis=0, tiled=True)  6.04 us
    unnamed x4, other arithmetic  3.23 us
    unnamed x7, local copies, waits for them, and re-layouts  2.66 us
  transfers between devices with their start and end apart: 1, of which 1 were waited for; matrix products, arithmetic and copies ran while one was open for 1% of the time, Pallas kernels for 0%

profile of v1, /device:TPU:0, one launch (start us, length us, event | category | flops | bytes accessed | tf_op | source)
XLA Modules:
  0.0 102.1 jit_solution(8442687544806478612)
XLA Ops:
  0.0 0.8 fusion.23
  0.8 0.8 fusion.22
  1.6 0.8 convert_dynamic-update-slice_fusion.2
  2.4 0.8 convert_dynamic-update-slice_fusion.1
  3.2 0.8 convert_dynamic-update-slice_fusion
  4.4 1.3 %reshape.114 = f32[32,1,480]{2,1,0:T(1,128)} reshape(f32[32,5,8,12]{3,2,1,0:T(8,128)S(1)} %bitcast.74) | data formatting | bytes 122880
  5.7 7.3 %all-to-all-start = ((f32[32,1,480]{2,1,0:T(1,128)}), f32[32,1,480]{2,1,0:T(1,128)S(1)}, u32[]{:S(2)}, u32[]{:S(2)}) async-start(f32[32,1,480]{2,1,0:T(1,128)} %reshape.114), calls=%async_computation | async-start | bytes 131072 | tf_op jit(solution)/shard_map/all_to_all | solution.py:176
  13.0 1.1 %fusion.3.e_ref = bf16[128,2048]{1,0:T(8,128)(2,1)} fusion(s32[2048]{0:T(1024)S(1)} %get-tuple-element.16, s32[2048]{0:T(1024)S(1)} %get-tuple-element.18, s32[128]{0:T(128)S(1)} %get-tuple-element.25, s32[128]{0:T(128)S(1)} %get-tuple-element.26, s32[2048]{0:T(1024)S(1)} %get-tuple-element.17, s32[2048]{0:T(1024)S(1)} %get-tuple-element.19, ...), kind=kLoop, calls=%fused_computation.11 | loop fusion | flops 2097152 | bytes 563456 | tf_op jit(solution)/shard_map/convert_element_type | solution.py:134
  14.3 6.0 %all-to-all-done = f32[32,1,480]{2,1,0:T(1,128)S(1)} async-done(((f32[32,1,480]{2,1,0:T(1,128)}), f32[32,1,480]{2,1,0:T(1,128)S(1)}, u32[]{:S(2)}, u32[]{:S(2)}) %all-to-all-start) | async-done | bytes 61472 | tf_op jit(solution)/shard_map/all_to_all | solution.py:176
  20.4 0.5 broadcast.220
  20.9 0.8 reduce
  24.2 1.4 %fusion.4 = f32[8,384,128]{2,1,0:T(8,128)S(1)} fusion(s32[8,384]{1,0:T(8,128)S(1)} %convert_element_type.88, f32[64,128]{1,0:T(8,128)S(1)} %copy-done), kind=kOutput, calls=%fused_computation.14 | convolution fusion | flops 302186496 | bytes 1617920 | tf_op jit(solution)/shard_map/dot_general | solution.py:61
  25.6 1.4 %subtract_convert_fusion = (bf16[8,384,64]{2,1,0:T(8,128)(2,1)S(1)}, bf16[8,384,64]{2,1,0:T(8,128)(2,1)S(1)}) fusion(f32[8,384,128]{2,1,0:T(8,128)S(1)} %fusion.4, f32[8,384]{1,0:T(8,128)S(1)} %mul.174, f32[8,384]{1,0:T(8,128)S(1)} %mul.171), kind=kLoop, calls=%fused_computation.1 | loop fusion | flops 1572864 | bytes 2383872 | tf_op jit(solution)/shard_map/convert
  27.0 1.3 %pad_maximum_fusion.w_ref = bf16[8,384,128]{2,1,0:T(8,128)(2,1)} fusion(bf16[8,384,64]{2,1,0:T(8,128)(2,1)S(1)} %get-tuple-element.6, bf16[8,384,64]{2,1,0:T(8,128)(2,1)S(1)} %get-tuple-element.5), kind=kLoop, calls=%fused_computation.12 | loop fusion | flops 1572864 | bytes 1572864 | tf_op jit(solution)/shard_map/concatenate | solution.py:72
  28.4 0.7 add_subtract_fusion
  29.1 65.5 %shard_map.64 = f32[2,64,1024]{2,1,0:T(8,128)} custom-call(bf16[8,384,128]{2,1,0:T(8,128)(2,1)} %pad_maximum_fusion.w_ref, s32[8,24,128]{2,1,0:T(8,128)} %get-tuple-element.29.vob_ref, s32[8,24,128]{2,1,0:T(8,128)} %get-tuple-element.28.uoa_ref, bf16[128,2048]{1,0:T(8,128)(2,1)} %fusion.3.e_ref), custom_call_target="tpu_custom_call" | custom-call | tf_op jit(solution)/shard_map/pallas_call | solution.py:135
  94.6 1.1 %slice_bitcast_fusion = (f32[8,8,8,128]{3,1,2,0:T(8,128)S(1)}, f32[8,8,8,128]{3,1,2,0:T(8,128)S(1)}) fusion(f32[2,64,1024]{2,1,0:T(8,128)} %shard_map.64), kind=kLoop, calls=%fused_computation.17 | loop fusion | bytes 1048576
  96.2 0.4 fusion.48
  97.0 0.5 add_bitcast_fusion
  97.5 0.6 fusion.6
  98.1 0.6 fusion.10
  98.7 0.6 fusion
  99.8 0.6 fusion.1
  100.9 1.2 %copy.62 = f32[64,2,1024]{2,1,0:T(2,128)} copy(f32[64,2,1024]{2,0,1:T(8,128)S(1)} %maximum_multiply_fusion) | data formatting | bytes 1048576 | tf_op jit(solution)/shard_map/mul | solution.py:50
  (42 shorter events, 4.8 us)
Async XLA Ops:
  0.0 24.2 %copy-start = (f32[64,128]{1,0:T(8,128)S(1)}, f32[64,128]{1,0:T(8,128)}, u32[]{:S(2)}) copy-start(f32[64,128]{1,0:T(8,128)} %param.11) | copy-start | bytes 98308
  5.7 14.7 %all-to-all-start = ((f32[32,1,480]{2,1,0:T(1,128)}), f32[32,1,480]{2,1,0:T(1,128)S(1)}, u32[]{:S(2)}, u32[]{:S(2)}) async-start(f32[32,1,480]{2,1,0:T(1,128)} %reshape.114), calls=%async_computation | async-start | bytes 131072 | tf_op jit(solution)/shard_map/all_to_all | solution.py:176

commit v2 on v1

--- a/solution.py
+++ b/solution.py
@@ -72,12 +72,13 @@
     return jnp.concatenate([part_re, part_im], axis=-1).astype(jnp.bfloat16)
 
 
-def grid_kernel(w_ref, vob_ref, uoa_ref, e_ref, out_ref, rep_ref):
+def grid_kernel(w_ref, vob_ref, uoa_ref, e_ref, out_ref, rep_ref, x_ref, r_ref):
     chunk_step = pl.program_id(1)
     chunk = w_ref.shape[1]
     rows = out_ref.shape[1]
     ngroups = chunk // GROUP
     nblocks = w_ref.shape[2] // SUPPORT
+    depth = nblocks * GROUP // 2
 
     @pl.when(chunk_step == 0)
     def _():
@@ -93,7 +94,7 @@
     urow = lax.broadcasted_iota(jnp.int32, (rows, TILE), 0)
     zero = jnp.zeros((GROUP, TILE), jnp.bfloat16)
 
-    def body(g, acc):
+    def body(g, carry):
         start = pl.multiple_of(g * GROUP, GROUP)
         blocks = [
             jnp.where(keep, rep_ref[pl.ds(start, GROUP), pl.ds(i * TILE, TILE)], zero)
@@ -105,17 +106,17 @@
         spread = lax.dot_general(
             wbd, cst, (((1,), (1,)), ((), ())), preferred_element_type=jnp.float32
         ).astype(jnp.bfloat16)
+        at = pl.multiple_of(g * depth, depth)
+        x_ref[0, pl.ds(at, depth), :] = spread[:depth]
+        x_ref[1, pl.ds(at, depth), :] = spread[depth:]
         uoa = uoa_ref[0, pl.ds(g, 1), :]
-        pick = (urow == uoa).astype(jnp.bfloat16)
-        half = spread.shape[0] // 2
-        acc_re = acc[0] + jnp.dot(pick, spread[:half], preferred_element_type=jnp.float32)
-        acc_im = acc[1] + jnp.dot(pick, spread[half:], preferred_element_type=jnp.float32)
-        return (acc_re, acc_im)
-
-    init = (jnp.zeros((rows, TILE), jnp.float32), jnp.zeros((rows, TILE), jnp.float32))
-    acc_re, acc_im = lax.fori_loop(0, ngroups, body, init)
-    out_ref[0] += acc_re
-    out_ref[1] += acc_im
+        r_ref[:, pl.ds(at, TILE)] = (urow == uoa).astype(jnp.bfloat16)
+        return carry
+
+    lax.fori_loop(0, ngroups, body, 0, unroll=4)
+    pick = r_ref[...]
+    out_ref[0] += jnp.dot(pick, x_ref[0], preferred_element_type=jnp.float32)
+    out_ref[1] += jnp.dot(pick, x_ref[1], preferred_element_type=jnp.float32)
 
 
 def grid_rows(weighted, vob, uoa, rows):
@@ -143,7 +144,11 @@
         ],
         out_specs=pl.BlockSpec((2, rows, TILE), lambda d, c: (0, 0, d)),
         out_shape=jax.ShapeDtypeStruct((2, rows, dests * TILE), jnp.float32),
-        scratch_shapes=[pltpu.VMEM((chunk, nblocks * TILE), jnp.bfloat16)],
+        scratch_shapes=[
+            pltpu.VMEM((chunk, nblocks * TILE), jnp.bfloat16),
+            pltpu.VMEM((2, chunk * SUPPORT, TILE), jnp.bfloat16),
+            pltpu.VMEM((rows, chunk * SUPPORT), jnp.bfloat16),
+        ],
         compiler_params=pltpu.CompilerParams(
             dimension_semantics=("arbitrary", "arbitrary")
         ),

time: 103 us -> 58.3 us (0.57)
  Pallas kernels: 65.5 us -> 21.3 us
    pallas_call x1, Pallas kernels: 65.5 us -> 21.3 us  [grid_rows(): pl.pallas_call(grid_kernel, grid=(dests, steps), in_specs=[pl.BlockSpec((...]
  transfers between devices with their start and end apart: 1 -> 1, of which waited for: 1 -> 1; matrix products, arithmetic and copies ran while one was open for 1% -> 2% of each run, Pallas kernels for 0% -> 0%
where the time goes in v2:
time: 58.3 us; the launch traced here: 57.9 us
  Pallas kernels  21.3 us (37%)
  other arithmetic  9.47 us (16%)
  local copies, waits for them, and re-layouts  7.9 us (14%)
  starting transfers between devices  7.3 us (13%)
  waiting for transfers between devices  6.04 us (10%)
  matrix products  5.59 us (10%)
    pallas_call x1, Pallas kernels, grid_rows(): pl.pallas_call(grid_kernel, grid=(dests, steps), in_specs=[pl.BlockSpec((...  21.3 us
    all_to_all x1, starting transfers between devices, shards(): got = lax.all_to_all(send, axes, split_axis=0, concat_axis=0, tiled=True)  7.3 us
    all_to_all x1, waiting for transfers between devices, shards(): got = lax.all_to_all(send, axes, split_axis=0, concat_axis=0, tiled=True)  6.04 us
    unnamed x4, other arithmetic  3.23 us
    unnamed x7, local copies, waits for them, and re-layouts  2.66 us
    another operation x1, other arithmetic  1.44 us
    dot_general x1, matrix products, weigh(): jnp.dot(onehot.reshape(-1, nplanes), kernels, precision=lax.Precision.HIG...  1.42 us
    concatenate x1, other arithmetic, weigh(): return jnp.concatenate([part_re, part_im], axis=-1).astype(jnp.bfloat16)  1.32 us
  transfers between devices with their start and end apart: 1, of which 1 were waited for; matrix products, arithmetic and copies ran while one was open for 2% of the time, Pallas kernels for 0%

profile of v2, /device:TPU:0, one launch (start us, length us, event | category | flops | bytes accessed | tf_op | source)
XLA Modules:
  0.0 57.9 jit_solution(8380091507292874809)
XLA Ops:
  0.0 0.8 %fusion.23 = f32[5,8,16,12]{2,1,3,0:T(8,128)S(1)} fusion(f32[2,1,8,16,12]{3,2,4,1,0:T(8,128)} %param.6, s32[8,16]{1,0:T(8,128)} %bitcast.82), kind=kLoop, calls=%fused_computation.48 | loop fusion | flops 3071 | bytes 55808
  0.8 0.8 %fusion.22 = f32[5,8,16,12]{2,1,3,0:T(8,128)S(1)} fusion(f32[5,8,16,12]{2,1,3,0:T(8,128)S(1)} %fusion.23, f32[2,1,8,16,12]{3,2,4,1,0:T(8,128)} %param.6, s32[8,16]{1,0:T(8,128)} %bitcast.83), kind=kLoop, calls=%fused_computation.46 | loop fusion | flops 3072 | bytes 55808
  1.6 0.8 %convert_dynamic-update-slice_fusion.2 = f32[5,8,16,12]{2,1,3,0:T(8,128)S(1)} fusion(f32[5,8,16,12]{2,1,3,0:T(8,128)S(1)} %fusion.22, s32[1,8,16,12]{2,1,3,0:T(8,128)} %param.8), kind=kLoop, calls=%fused_computation.52 | loop fusion | flops 1536 | bytes 55296
  2.4 0.8 %convert_dynamic-update-slice_fusion.1 = f32[5,8,16,12]{2,1,3,0:T(8,128)S(1)} fusion(f32[5,8,16,12]{2,1,3,0:T(8,128)S(1)} %convert_dynamic-update-slice_fusion.2, s32[1,8,16,12]{2,1,3,0:T(8,128)} %param.9), kind=kLoop, calls=%fused_computation.51 | loop fusion | flops 1536 | bytes 55296
  3.2 0.8 %convert_dynamic-update-slice_fusion = f32[5,8,16,12]{2,1,3,0:T(8,128)S(1)} fusion(f32[5,8,16,12]{2,1,3,0:T(8,128)S(1)} %convert_dynamic-update-slice_fusion.1, s32[1,8,16,12]{2,1,3,0:T(8,128)} %param.10), kind=kLoop, calls=%fused_computation.50 | loop fusion | flops 1536 | bytes 55296 | tf_op jit(solution)/shard_map/stack | solution.py:170
  4.4 1.3 %reshape.114 = f32[32,1,480]{2,1,0:T(1,128)} reshape(f32[32,5,8,12]{3,2,1,0:T(8,128)S(1)} %bitcast.74) | data formatting | bytes 122880
  5.7 7.3 %all-to-all-start = ((f32[32,1,480]{2,1,0:T(1,128)}), f32[32,1,480]{2,1,0:T(1,128)S(1)}, u32[]{:S(2)}, u32[]{:S(2)}) async-start(f32[32,1,480]{2,1,0:T(1,128)} %reshape.114), calls=%async_computation | async-start | bytes 131072 | tf_op jit(solution)/shard_map/all_to_all | solution.py:181
  13.0 1.1 %fusion.3.e_ref = bf16[128,2048]{1,0:T(8,128)(2,1)} fusion(s32[2048]{0:T(1024)S(1)} %get-tuple-element.16, s32[2048]{0:T(1024)S(1)} %get-tuple-element.18, s32[128]{0:T(128)S(1)} %get-tuple-element.25, s32[128]{0:T(128)S(1)} %get-tuple-element.26, s32[2048]{0:T(1024)S(1)} %get-tuple-element.17, s32[2048]{0:T(1024)S(1)} %get-tuple-element.19, ...), kind=kLoop, calls=%fused_computation.11 | loop fusion | flops 2097152 | bytes 563456 | tf_op jit(solution)/shard_map/convert_element_type | solution.py:135
  14.3 6.0 %all-to-all-done = f32[32,1,480]{2,1,0:T(1,128)S(1)} async-done(((f32[32,1,480]{2,1,0:T(1,128)}), f32[32,1,480]{2,1,0:T(1,128)S(1)}, u32[]{:S(2)}, u32[]{:S(2)}) %all-to-all-start) | async-done | bytes 61472 | tf_op jit(solution)/shard_map/all_to_all | solution.py:181
  20.4 0.5 broadcast.220
  20.9 0.8 %reduce = f32[32,480]{1,0:T(8,128)S(1)} reduce(f32[32,1,480]{2,1,0:T(1,128)S(1)} %all-to-all-done, f32[]{:T(128)} %broadcast.220), dimensions={1}, to_apply=%all_to_all.3.reduce_sub_computation | reduce | bytes 122884 | tf_op jit(solution)/shard_map/all_to_all | solution.py:181
  24.2 1.4 %fusion.4 = f32[8,384,128]{2,1,0:T(8,128)S(1)} fusion(s32[8,384]{1,0:T(8,128)S(1)} %convert_element_type.88, f32[64,128]{1,0:T(8,128)S(1)} %copy-done), kind=kOutput, calls=%fused_computation.14 | convolution fusion | flops 302186496 | bytes 1617920 | tf_op jit(solution)/shard_map/dot_general | solution.py:61
  25.6 1.4 %subtract_convert_fusion = (bf16[8,384,64]{2,1,0:T(8,128)(2,1)S(1)}, bf16[8,384,64]{2,1,0:T(8,128)(2,1)S(1)}) fusion(f32[8,384,128]{2,1,0:T(8,128)S(1)} %fusion.4, f32[8,384]{1,0:T(8,128)S(1)} %mul.174, f32[8,384]{1,0:T(8,128)S(1)} %mul.171), kind=kLoop, calls=%fused_computation.1 | loop fusion | flops 1572864 | bytes 2383872 | tf_op jit(solution)/shard_map/convert
  27.0 1.3 %pad_maximum_fusion.w_ref = bf16[8,384,128]{2,1,0:T(8,128)(2,1)} fusion(bf16[8,384,64]{2,1,0:T(8,128)(2,1)S(1)} %get-tuple-element.6, bf16[8,384,64]{2,1,0:T(8,128)(2,1)S(1)} %get-tuple-element.5), kind=kLoop, calls=%fused_computation.12 | loop fusion | flops 1572864 | bytes 1572864 | tf_op jit(solution)/shard_map/concatenate | solution.py:72
  28.4 0.7 %add_subtract_fusion = (s32[8,24,128]{2,1,0:T(8,128)}, s32[8,24,128]{2,1,0:T(8,128)}) fusion(s32[8,24,128]{2,1,0:T(8,128)S(1)} %add.135, s32[]{:T(128)S(6)} %mul.180, s32[128]{0:T(128)S(1)} %add.137, s32[8,24,128]{2,1,0:T(8,128)S(1)} %copy.52, s32[128]{0:T(128)S(1)} %add.131), kind=kLoop, calls=%fused_computation.28 | loop fusion | flops 73728 | bytes 394244 | tf_op jit(solution)/shard_map/sub | solution.py:197
  29.1 21.3 %shard_map.64 = f32[2,64,1024]{2,1,0:T(8,128)} custom-call(bf16[8,384,128]{2,1,0:T(8,128)(2,1)} %pad_maximum_fusion.w_ref, s32[8,24,128]{2,1,0:T(8,128)} %get-tuple-element.29.vob_ref, s32[8,24,128]{2,1,0:T(8,128)} %get-tuple-element.28.uoa_ref, bf16[128,2048]{1,0:T(8,128)(2,1)} %fusion.3.e_ref), custom_call_target="tpu_custom_call" | custom-call | tf_op jit(solution)/shard_map/pallas_call | solution.py:136
  50.3 1.1 %slice_bitcast_fusion = (f32[8,8,8,128]{3,1,2,0:T(8,128)S(1)}, f32[8,8,8,128]{3,1,2,0:T(8,128)S(1)}) fusion(f32[2,64,1024]{2,1,0:T(8,128)} %shard_map.64), kind=kLoop, calls=%fused_computation.17 | loop fusion | bytes 1048576
  51.5 0.4 fusion.46
  52.8 0.5 add_bitcast_fusion
  53.2 0.6 %fusion.6 = f32[128,64,8]{0,1,2:T(8,128)S(1)} fusion(f32[64,8,128]{2,1,0:T(8,128)S(1)} %get-tuple-element.8), kind=kOutput, calls=%fused_computation.22 | convolution fusion | flops 100892672 | bytes 524288 | tf_op jit(solution)/shard_map/rkj,jm->rmk/dot_general | solution.py:45
  53.9 0.6 %fusion.10 = f32[128,64,8]{0,1,2:T(8,128)S(1)} fusion(f32[64,8,128]{2,1,0:T(8,128)S(1)} %get-tuple-element.7), kind=kOutput, calls=%fused_computation.26 | convolution fusion | flops 100892672 | bytes 524288 | tf_op jit(solution)/shard_map/rkj,jm->rmk/dot_general | solution.py:42
  54.5 0.6 %fusion = f32[64,128,8]{1,0,2:T(8,128)S(1)} fusion(f32[128,64,8]{0,1,2:T(8,128)S(1)} %fusion.6, f32[64,8,128]{2,1,0:T(8,128)S(1)} %get-tuple-element.7), kind=kOutput, calls=%fused_computation.3 | convolution fusion | flops 100958208 | bytes 786432 | tf_op jit(solution)/shard_map/rkj,jm->rmk/dot_general | solution.py:45
  55.5 0.6 %fusion.1 = f32[64,128,8]{1,0,2:T(8,128)S(1)} fusion(f32[128,64,8]{0,1,2:T(8,128)S(1)} %fusion.10, f32[64,8,128]{2,1,0:T(8,128)S(1)} %get-tuple-element.8), kind=kOutput, calls=%fused_computation.5 | convolution fusion | flops 100958208 | bytes 786432 | tf_op jit(solution)/shard_map/rkj,jm->rmk/dot_general | solution.py:42
  56.7 1.2 %copy.62 = f32[64,2,1024]{2,1,0:T(2,128)} copy(f32[64,2,1024]{2,0,1:T(8,128)S(1)} %maximum_multiply_fusion) | data formatting | bytes 1048576 | tf_op jit(solution)/shard_map/mul | solution.py:50
  (42 shorter events, 4.8 us)
Async XLA Ops:
  0.0 24.2 %copy-start = (f32[64,128]{1,0:T(8,128)S(1)}, f32[64,128]{1,0:T(8,128)}, u32[]{:S(2)}) copy-start(f32[64,128]{1,0:T(8,128)} %param.11) | copy-start | bytes 98308
  5.7 14.7 %all-to-all-start = ((f32[32,1,480]{2,1,0:T(1,128)}), f32[32,1,480]{2,1,0:T(1,128)S(1)}, u32[]{:S(2)}, u32[]{:S(2)}) async-start(f32[32,1,480]{2,1,0:T(1,128)} %reshape.114), calls=%async_computation | async-start | bytes 131072 | tf_op jit(solution)/shard_map/all_to_all | solution.py:181

commit v3 on v2

--- a/solution.py
+++ b/solution.py
@@ -163,7 +163,9 @@
     ndev = lax.axis_size(axes)
     rows = ntiles * TILE // ndev
     per_tile = ndev // ntiles
+    own_dests = dests // per_tile
     me = lax.axis_index(axes)
+    member = me % per_tile
     live = (
         lax.broadcasted_iota(jnp.int32, (dests, ntiles, slots), 2) < tile_counts[0][:, :, None]
     ).astype(jnp.float32)
@@ -176,10 +178,10 @@
             v_offset[0].astype(jnp.float32),
         ]
     )
-    send = jnp.repeat(fields, per_tile, axis=2)
-    send = jnp.moveaxis(send, 2, 0)
+    send = fields.reshape(FIELDS, per_tile, own_dests, ntiles, slots).transpose(3, 1, 0, 2, 4)
+    send = send.reshape(ndev, FIELDS, own_dests, slots)
     got = lax.all_to_all(send, axes, split_axis=0, concat_axis=0, tiled=True)
-    got = jnp.moveaxis(got, 0, 2).reshape(FIELDS, dests, ndev * slots)
+    got = got.transpose(1, 2, 0, 3).reshape(FIELDS, own_dests, ndev * slots)
     vis_re = got[0]
     vis_im = got[1]
     planes = got[2].astype(jnp.int32)
@@ -192,13 +194,26 @@
     per_dest = ndev * slots
     ngroups = per_dest // GROUP
     taps = jnp.arange(SUPPORT, dtype=jnp.int32)
-    vob = (cols_first.reshape(dests, ngroups, GROUP, 1) + taps).reshape(dests, ngroups, TILE)
-    offset = (me % per_tile) * rows
-    uoa = (rows_first.reshape(dests, ngroups, 1, GROUP) + taps[:, None] - offset).reshape(
-        dests, ngroups, TILE
-    )
-    slab = grid_rows(weighted, vob, uoa, rows)
-    return transform(slab[0], slab[1], dests)
+    vob = (cols_first.reshape(own_dests, ngroups, GROUP, 1) + taps).reshape(own_dests, ngroups, TILE)
+    uoa = (rows_first.reshape(own_dests, ngroups, 1, GROUP) + taps[:, None]).reshape(
+        own_dests, ngroups, TILE
+    )
+    slab = grid_rows(weighted, vob, uoa, TILE)
+    width = own_dests * TILE
+    mine = lax.dynamic_slice_in_dim(slab, member * rows, rows, axis=1)
+    full = jnp.zeros((2, rows, dests * TILE), jnp.float32)
+    full = lax.dynamic_update_slice_in_dim(full, mine, member * width, axis=2)
+    for step in range(1, per_tile):
+        target = (member + step) % per_tile
+        source = (member + per_tile - step) % per_tile
+        pairs = [
+            (k, (k // per_tile) * per_tile + (k % per_tile + step) % per_tile)
+            for k in range(ndev)
+        ]
+        piece = lax.dynamic_slice_in_dim(slab, target * rows, rows, axis=1)
+        piece = lax.ppermute(piece, axes, pairs)
+        full = lax.dynamic_update_slice_in_dim(full, piece, source * width, axis=2)
+    return transform(full[0], full[1], dests)
 
 
 def solution(mesh):

time: 58.3 us -> 48.6 us (0.83)
  Pallas kernels: 21.3 us -> 12.5 us
  other arithmetic: 9.47 us -> 4.44 us
  local copies, waits for them, and re-layouts: 7.9 us -> 11 us
  waiting for transfers between devices: 6.04 us -> 7.31 us
  matrix products: 5.59 us -> 4.98 us
    pallas_call x1, Pallas kernels: 21.3 us -> 12.5 us  [grid_rows(): pl.pallas_call(grid_kernel, grid=(dests, steps), in_specs=[pl.BlockSpec((...]
    unnamed x4 -> x2, other arithmetic: 3.23 us -> 0.29 us
    unnamed x7 -> x19, local copies, waits for them, and re-layouts: 2.66 us -> 4.79 us
    another operation x2 -> x1, other arithmetic: 2.24 us -> 0.68 us
    ppermute x0 -> x1, waiting for transfers between devices: none -> 1.37 us  [shards(): piece = lax.ppermute(piece, axes, pairs)]
    slice x0 -> x1, local copies, waits for them, and re-layouts: none -> 0.84 us  [shards(): visibilities[1, 0] * live]
    sub x1 -> x0, other arithmetic: 0.69 us -> none  [shards(): rows_first.reshape(dests, ngroups, 1, GROUP) + taps[:, None] - offset]
    add x0 -> x1, other arithmetic: none -> 0.64 us  [shards(): rows_first.reshape(own_dests, ngroups, 1, GROUP) + taps[:, None]]
  transfers between devices with their start and end apart: 1 -> 2, of which waited for: 1 -> 2; matrix products, arithmetic and copies ran while one was open for 2% -> 3% of each run, Pallas kernels for 0% -> 0%
where the time goes in v3:
time: 48.6 us; the launch traced here: 48.1 us
  Pallas kernels  12.5 us (26%)
  local copies, waits for them, and re-layouts  11 us (23%)
  starting transfers between devices  7.48 us (15%)
  waiting for transfers between devices  7.31 us (15%)
  matrix products  4.98 us (10%)
  other arithmetic  4.44 us (9%)
    pallas_call x1, Pallas kernels, grid_rows(): pl.pallas_call(grid_kernel, grid=(dests, steps), in_specs=[pl.BlockSpec((...  12.5 us
    all_to_all x1, starting transfers between devices, shards(): got = lax.all_to_all(send, axes, split_axis=0, concat_axis=0, tiled=True)  7.3 us
    all_to_all x1, waiting for transfers between devices, shards(): got = lax.all_to_all(send, axes, split_axis=0, concat_axis=0, tiled=True)  5.94 us
    unnamed x19, local copies, waits for them, and re-layouts  4.79 us
    ppermute x1, waiting for transfers between devices, shards(): piece = lax.ppermute(piece, axes, pairs)  1.37 us
    mul x1, local copies, waits for them, and re-layouts, transform(): jnp.stack([final_re.reshape(nrows, total), final_im.reshape(nrows, total)...  1.2 us
    convert_element_type x1, other arithmetic, grid_rows(): expand = ((lanes_in // SUPPORT == lanes_out // TILE) & (lanes_in % SUPPOR...  1.05 us
    concatenate x1, other arithmetic, weigh(): return jnp.concatenate([part_re, part_im], axis=-1).astype(jnp.bfloat16)  0.98 us
  transfers between devices with their start and end apart: 2, of which 2 were waited for; matrix products, arithmetic and copies ran while one was open for 3% of the time, Pallas kernels for 0%

profile of v3, /device:TPU:0, one launch (start us, length us, event | category | flops | bytes accessed | tf_op | source)
XLA Modules:
  0.0 48.1 jit_solution(11814925750206746554)
XLA Ops:
  0.0 0.8 %fusion.94 = (f32[1,1,8,16,12]{3,2,4,1,0:T(8,128)S(1)}, f32[1,1,8,16,12]{3,2,4,1,0:T(8,128)S(1)}) fusion(f32[2,1,8,16,12]{3,2,4,1,0:T(8,128)} %param.6), kind=kLoop, calls=%fused_computation.137 | loop fusion | bytes 24576 | tf_op jit(solution)/shard_map/slice | solution.py:175
  1.0 0.5 %copy-done.5 = s32[1,8,16]{2,1,0:T(8,128)S(1)} copy-done((s32[1,8,16]{2,1,0:T(8,128)S(1)}, s32[1,8,16]{2,1,0:T(8,128)}, u32[]{:S(2)}) %copy-start.5) | copy-done | bytes 536
  1.8 0.7 %copy-done.2 = s32[1,8,16,12]{2,1,3,0:T(8,128)S(1)} copy-done((s32[1,8,16,12]{2,1,3,0:T(8,128)S(1)}, s32[1,8,16,12]{2,1,3,0:T(8,128)}, u32[]{:S(2)}) %copy-start.2) | copy-done | bytes 6168
  2.6 0.7 %copy-done.3 = s32[1,8,16,12]{2,1,3,0:T(8,128)S(1)} copy-done((s32[1,8,16,12]{2,1,3,0:T(8,128)S(1)}, s32[1,8,16,12]{2,1,3,0:T(8,128)}, u32[]{:S(2)}) %copy-start.3) | copy-done | bytes 6168
  3.4 0.7 %copy-done.4 = s32[1,8,16,12]{2,1,3,0:T(8,128)S(1)} copy-done((s32[1,8,16,12]{2,1,3,0:T(8,128)S(1)}, s32[1,8,16,12]{2,1,3,0:T(8,128)}, u32[]{:S(2)}) %copy-start.4) | copy-done | bytes 6168
  4.8 0.9 %reshape.128 = f32[32,1,240]{2,1,0:T(1,128)} reshape(f32[32,5,4,12]{3,2,1,0:T(4,128)S(1)} %copy.59) | data formatting | bytes 61440
  5.6 7.3 %all-to-all-start = ((f32[32,1,240]{2,1,0:T(1,128)}), f32[32,1,240]{2,1,0:T(1,128)S(1)}, u32[]{:S(2)}, u32[]{:S(2)}) async-start(f32[32,1,240]{2,1,0:T(1,128)} %reshape.128), calls=%async_computation | async-start | bytes 65536 | tf_op jit(solution)/shard_map/all_to_all | solution.py:183
  13.0 1.1 %fusion.3.e_ref = bf16[128,2048]{1,0:T(8,128)(2,1)} fusion(s32[2048]{0:T(1024)S(1)} %get-tuple-element.22, s32[2048]{0:T(1024)S(1)} %get-tuple-element.24, s32[128]{0:T(128)S(1)} %get-tuple-element.29, s32[128]{0:T(128)S(1)} %get-tuple-element.30, s32[2048]{0:T(1024)S(1)} %get-tuple-element.23, s32[2048]{0:T(1024)S(1)} %get-tuple-element.25, ...), kind=kLoop, calls=%fused_computation.9 | loop fusion | flops 2097152 | bytes 563456 | tf_op jit(solution)/shard_map/convert_element_type | solution.py:135
  14.2 5.9 %all-to-all-done = f32[32,1,240]{2,1,0:T(1,128)S(1)} async-done(((f32[32,1,240]{2,1,0:T(1,128)}), f32[32,1,240]{2,1,0:T(1,128)S(1)}, u32[]{:S(2)}, u32[]{:S(2)}) %all-to-all-start) | async-done | bytes 30752 | tf_op jit(solution)/shard_map/all_to_all | solution.py:183
  20.2 0.5 %broadcast.233 = f32[]{:T(128)} broadcast(f32[]{:T(128)} %constant.260), dimensions={} | broadcast | bytes 8 | tf_op jit(solution)/shard_map/all_to_all | solution.py:183
  20.7 0.6 %reduce = f32[32,240]{1,0:T(8,128)S(1)} reduce(f32[32,1,240]{2,1,0:T(1,128)S(1)} %all-to-all-done, f32[]{:T(128)} %broadcast.233), dimensions={1}, to_apply=%all_to_all.3.reduce_sub_computation | reduce | bytes 61444 | tf_op jit(solution)/shard_map/all_to_all | solution.py:183
  23.2 0.8 %fusion.4 = f32[4,384,128]{2,1,0:T(8,128)S(1)} fusion(s32[4,384]{1,0:T(4,128)S(1)} %convert_element_type.88, f32[64,128]{1,0:T(8,128)S(1)} %copy-done), kind=kOutput, calls=%fused_computation.15 | convolution fusion | flops 151093248 | bytes 825344 | tf_op jit(solution)/shard_map/dot_general | solution.py:61
  24.0 0.7 %subtract_convert_fusion = (bf16[4,384,64]{2,1,0:T(8,128)(2,1)S(1)}, bf16[4,384,64]{2,1,0:T(8,128)(2,1)S(1)}) fusion(f32[4,384,128]{2,1,0:T(8,128)S(1)} %fusion.4, f32[4,384]{1,0:T(4,128)S(1)} %mul.183, f32[4,384]{1,0:T(4,128)S(1)} %mul.180), kind=kLoop, calls=%fused_computation.11 | loop fusion | flops 786432 | bytes 1191936 | tf_op jit(solution)/shard_map/convert
  24.7 1.0 %pad_maximum_fusion.w_ref = bf16[4,384,128]{2,1,0:T(8,128)(2,1)} fusion(bf16[4,384,64]{2,1,0:T(8,128)(2,1)S(1)} %get-tuple-element.6, bf16[4,384,64]{2,1,0:T(8,128)(2,1)S(1)} %get-tuple-element.5), kind=kLoop, calls=%fused_computation.13 | loop fusion | flops 786432 | bytes 786432 | tf_op jit(solution)/shard_map/concatenate | solution.py:72
  25.7 0.6 %broadcast_add_fusion = (s32[4,24,128]{2,1,0:T(8,128)}, s32[4,24,128]{2,1,0:T(8,128)}) fusion(s32[4,24,128]{2,1,0:T(8,128)S(1)} %add.158, s32[128]{0:T(128)S(1)} %add.160, s32[4,24,128]{2,1,0:T(8,128)S(1)} %copy.68, s32[128]{0:T(128)S(1)} %add.154), kind=kLoop, calls=%fused_computation.51 | loop fusion | flops 24576 | bytes 197632 | tf_op jit(solution)/shard_map/add | solution.py:198
  26.3 12.5 %shard_map.64 = f32[2,128,512]{2,1,0:T(8,128)} custom-call(bf16[4,384,128]{2,1,0:T(8,128)(2,1)} %pad_maximum_fusion.w_ref, s32[4,24,128]{2,1,0:T(8,128)} %get-tuple-element.33.vob_ref, s32[4,24,128]{2,1,0:T(8,128)} %get-tuple-element.32.uoa_ref, bf16[128,2048]{1,0:T(8,128)(2,1)} %fusion.3.e_ref), custom_call_target="tpu_custom_call" | custom-call | tf_op jit(solution)/shard_map/pallas_call | solution.py:136
  38.9 1.0 %copy-done.1 = f32[2,128,512]{2,1,0:T(8,128)S(1)} copy-done((f32[2,128,512]{2,1,0:T(8,128)S(1)}, f32[2,128,512]{2,1,0:T(8,128)}, u32[]{:S(2)}) %copy-start.1) | copy-done | bytes 524312
  40.2 1.4 %collective-permute-done = f32[2,64,512]{2,1,0:T(8,128)S(1)} collective-permute-done((f32[2,64,512]{2,1,0:T(8,128)S(1)}, f32[2,64,512]{2,1,0:T(8,128)S(1)}, u32[]{:S(2)}, u32[]{:S(2)}) %collective-permute-start) | collective-permute-done | bytes 262176 | tf_op jit(solution)/shard_map/ppermute | solution.py:214
  43.0 0.5 add_bitcast_fusion
  43.5 0.6 %fusion.9 = f32[128,64,8]{0,1,2:T(8,128)S(1)} fusion(f32[64,8,128]{2,1,0:T(8,128)S(1)} %get-tuple-element.7), kind=kOutput, calls=%fused_computation.25 | convolution fusion | flops 100892672 | bytes 524288 | tf_op jit(solution)/shard_map/rkj,jm->rmk/dot_general | solution.py:42
  44.1 0.6 %fusion.5 = f32[128,64,8]{0,1,2:T(8,128)S(1)} fusion(f32[64,8,128]{2,1,0:T(8,128)S(1)} %get-tuple-element.8), kind=kOutput, calls=%fused_computation.21 | convolution fusion | flops 100892672 | bytes 524288 | tf_op jit(solution)/shard_map/rkj,jm->rmk/dot_general | solution.py:45
  44.7 0.6 %fusion.1 = f32[64,128,8]{1,0,2:T(8,128)S(1)} fusion(f32[128,64,8]{0,1,2:T(8,128)S(1)} %fusion.9, f32[64,8,128]{2,1,0:T(8,128)S(1)} %get-tuple-element.8), kind=kOutput, calls=%fused_computation.3 | convolution fusion | flops 100958208 | bytes 786432 | tf_op jit(solution)/shard_map/rkj,jm->rmk/dot_general | solution.py:42
  45.8 0.6 %fusion = f32[64,128,8]{1,0,2:T(8,128)S(1)} fusion(f32[128,64,8]{0,1,2:T(8,128)S(1)} %fusion.5, f32[64,8,128]{2,1,0:T(8,128)S(1)} %get-tuple-element.7), kind=kOutput, calls=%fused_computation.1 | convolution fusion | flops 100958208 | bytes 786432 | tf_op jit(solution)/shard_map/rkj,jm->rmk/dot_general | solution.py:45
  46.9 1.2 %copy.78 = f32[64,2,1024]{2,1,0:T(2,128)} copy(f32[64,2,1024]{2,0,1:T(8,128)S(1)} %maximum_multiply_fusion) | data formatting | bytes 1048576 | tf_op jit(solution)/shard_map/mul | solution.py:50
  (66 shorter events, 5.9 us)
Async XLA Ops:
  0.0 23.2 %copy-start = (f32[64,128]{1,0:T(8,128)S(1)}, f32[64,128]{1,0:T(8,128)}, u32[]{:S(2)}) copy-start(f32[64,128]{1,0:T(8,128)} %param.11) | copy-start | bytes 98308
  0.8 0.7 %copy-start.5 = (s32[1,8,16]{2,1,0:T(8,128)S(1)}, s32[1,8,16]{2,1,0:T(8,128)}, u32[]{:S(2)}) copy-start(s32[1,8,16]{2,1,0:T(8,128)} %param.7) | copy-start | bytes 1540
  1.6 0.8 %copy-start.2 = (s32[1,8,16,12]{2,1,3,0:T(8,128)S(1)}, s32[1,8,16,12]{2,1,3,0:T(8,128)}, u32[]{:S(2)}) copy-start(s32[1,8,16,12]{2,1,3,0:T(8,128)} %param.8) | copy-start | bytes 18436
  2.4 0.8 %copy-start.3 = (s32[1,8,16,12]{2,1,3,0:T(8,128)S(1)}, s32[1,8,16,12]{2,1,3,0:T(8,128)}, u32[]{:S(2)}) copy-start(s32[1,8,16,12]{2,1,3,0:T(8,128)} %param.9) | copy-start | bytes 18436
  3.2 0.8 %copy-start.4 = (s32[1,8,16,12]{2,1,3,0:T(8,128)S(1)}, s32[1,8,16,12]{2,1,3,0:T(8,128)}, u32[]{:S(2)}) copy-start(s32[1,8,16,12]{2,1,3,0:T(8,128)} %param.10) | copy-start | bytes 18436
  5.6 14.6 %all-to-all-start = ((f32[32,1,240]{2,1,0:T(1,128)}), f32[32,1,240]{2,1,0:T(1,128)S(1)}, u32[]{:S(2)}, u32[]{:S(2)}) async-start(f32[32,1,240]{2,1,0:T(1,128)} %reshape.128), calls=%async_computation | async-start | bytes 65536 | tf_op jit(solution)/shard_map/all_to_all | solution.py:183
  38.9 1.0 %copy-start.1 = (f32[2,128,512]{2,1,0:T(8,128)S(1)}, f32[2,128,512]{2,1,0:T(8,128)}, u32[]{:S(2)}) copy-start(f32[2,128,512]{2,1,0:T(8,128)} %shard_map.64) | copy-start | bytes 1572868
  40.0 1.6 %collective-permute-start = (f32[2,64,512]{2,1,0:T(8,128)S(1)}, f32[2,64,512]{2,1,0:T(8,128)S(1)}, u32[]{:S(2)}, u32[]{:S(2)}) collective-permute-start(f32[2,64,512]{2,1,0:T(8,128)S(1)} %get-tuple-element.11), channel_id=1, source_target_pairs={{0,1},{1,0},{2,3},{3,2},{4,5},{5,4},{6,7},{7,6},{8,9},{9,8},{10,11... | collective-permute-start | bytes 786440 | tf_op jit(solution)/shard_map/ppermute | solution.py:214

commit v4 on v3

--- a/solution.py
+++ b/solution.py
@@ -25,7 +25,7 @@
     nrows = real_in.shape[0]
     total = real_in.shape[1]
     width = total // groups
-    highest = lax.Precision.HIGHEST
+    highest = lax.Precision.HIGH
     cos_a, sin_a = make_table(groups, groups, groups)
     cos_t, sin_t = make_table(groups, width, total)
     cos_b, sin_b = make_table(width, width, width)

time: 48.6 us -> 47.7 us (0.981)
  matrix products: 4.98 us -> 4.1 us
where the time goes in v4:
time: 47.7 us; the launch traced here: 47.2 us
  Pallas kernels  12.5 us (26%)
  local copies, waits for them, and re-layouts  11 us (23%)
  starting transfers between devices  7.48 us (16%)
  waiting for transfers between devices  7.31 us (15%)
  other arithmetic  4.44 us (9%)
  matrix products  4.1 us (9%)
    pallas_call x1, Pallas kernels, grid_rows(): pl.pallas_call(grid_kernel, grid=(dests, steps), in_specs=[pl.BlockSpec((...  12.5 us
    all_to_all x1, starting transfers between devices, shards(): got = lax.all_to_all(send, axes, split_axis=0, concat_axis=0, tiled=True)  7.3 us
    all_to_all x1, waiting for transfers between devices, shards(): got = lax.all_to_all(send, axes, split_axis=0, concat_axis=0, tiled=True)  5.94 us
    unnamed x19, local copies, waits for them, and re-layouts  4.79 us
    ppermute x1, waiting for transfers between devices, shards(): piece = lax.ppermute(piece, axes, pairs)  1.37 us
    mul x1, local copies, waits for them, and re-layouts, transform(): jnp.stack([final_re.reshape(nrows, total), final_im.reshape(nrows, total)...  1.2 us
    convert_element_type x1, other arithmetic, grid_rows(): expand = ((lanes_in // SUPPORT == lanes_out // TILE) & (lanes_in % SUPPOR...  1.05 us
    concatenate x1, other arithmetic, weigh(): return jnp.concatenate([part_re, part_im], axis=-1).astype(jnp.bfloat16)  0.98 us
  transfers between devices with their start and end apart: 2, of which 2 were waited for; matrix products, arithmetic and copies ran while one was open for 3% of the time, Pallas kernels for 0%

profile of v4, /device:TPU:0, one launch (start us, length us, event | category | flops | bytes accessed | tf_op | source)
XLA Modules:
  0.0 47.2 jit_solution(9869622671084427959)
XLA Ops:
  0.0 0.8 %fusion.94 = (f32[1,1,8,16,12]{3,2,4,1,0:T(8,128)S(1)}, f32[1,1,8,16,12]{3,2,4,1,0:T(8,128)S(1)}) fusion(f32[2,1,8,16,12]{3,2,4,1,0:T(8,128)} %param.6), kind=kLoop, calls=%fused_computation.137 | loop fusion | bytes 24576 | tf_op jit(solution)/shard_map/slice | solution.py:175
  1.0 0.5 %copy-done.5 = s32[1,8,16]{2,1,0:T(8,128)S(1)} copy-done((s32[1,8,16]{2,1,0:T(8,128)S(1)}, s32[1,8,16]{2,1,0:T(8,128)}, u32[]{:S(2)}) %copy-start.5) | copy-done | bytes 536
  1.8 0.7 %copy-done.2 = s32[1,8,16,12]{2,1,3,0:T(8,128)S(1)} copy-done((s32[1,8,16,12]{2,1,3,0:T(8,128)S(1)}, s32[1,8,16,12]{2,1,3,0:T(8,128)}, u32[]{:S(2)}) %copy-start.2) | copy-done | bytes 6168
  2.6 0.7 %copy-done.3 = s32[1,8,16,12]{2,1,3,0:T(8,128)S(1)} copy-done((s32[1,8,16,12]{2,1,3,0:T(8,128)S(1)}, s32[1,8,16,12]{2,1,3,0:T(8,128)}, u32[]{:S(2)}) %copy-start.3) | copy-done | bytes 6168
  3.4 0.7 %copy-done.4 = s32[1,8,16,12]{2,1,3,0:T(8,128)S(1)} copy-done((s32[1,8,16,12]{2,1,3,0:T(8,128)S(1)}, s32[1,8,16,12]{2,1,3,0:T(8,128)}, u32[]{:S(2)}) %copy-start.4) | copy-done | bytes 6168
  4.8 0.9 %reshape.128 = f32[32,1,240]{2,1,0:T(1,128)} reshape(f32[32,5,4,12]{3,2,1,0:T(4,128)S(1)} %copy.59) | data formatting | bytes 61440
  5.6 7.3 %all-to-all-start = ((f32[32,1,240]{2,1,0:T(1,128)}), f32[32,1,240]{2,1,0:T(1,128)S(1)}, u32[]{:S(2)}, u32[]{:S(2)}) async-start(f32[32,1,240]{2,1,0:T(1,128)} %reshape.128), calls=%async_computation | async-start | bytes 65536 | tf_op jit(solution)/shard_map/all_to_all | solution.py:183
  13.0 1.1 %fusion.3.e_ref = bf16[128,2048]{1,0:T(8,128)(2,1)} fusion(s32[2048]{0:T(1024)S(1)} %get-tuple-element.22, s32[2048]{0:T(1024)S(1)} %get-tuple-element.24, s32[128]{0:T(128)S(1)} %get-tuple-element.29, s32[128]{0:T(128)S(1)} %get-tuple-element.30, s32[2048]{0:T(1024)S(1)} %get-tuple-element.23, s32[2048]{0:T(1024)S(1)} %get-tuple-element.25, ...), kind=kLoop, calls=%fused_computation.9 | loop fusion | flops 2097152 | bytes 563456 | tf_op jit(solution)/shard_map/convert_element_type | solution.py:135
  14.2 5.9 %all-to-all-done = f32[32,1,240]{2,1,0:T(1,128)S(1)} async-done(((f32[32,1,240]{2,1,0:T(1,128)}), f32[32,1,240]{2,1,0:T(1,128)S(1)}, u32[]{:S(2)}, u32[]{:S(2)}) %all-to-all-start) | async-done | bytes 30752 | tf_op jit(solution)/shard_map/all_to_all | solution.py:183
  20.2 0.5 %broadcast.233 = f32[]{:T(128)} broadcast(f32[]{:T(128)} %constant.260), dimensions={} | broadcast | bytes 8 | tf_op jit(solution)/shard_map/all_to_all | solution.py:183
  20.7 0.6 %reduce = f32[32,240]{1,0:T(8,128)S(1)} reduce(f32[32,1,240]{2,1,0:T(1,128)S(1)} %all-to-all-done, f32[]{:T(128)} %broadcast.233), dimensions={1}, to_apply=%all_to_all.3.reduce_sub_computation | reduce | bytes 61444 | tf_op jit(solution)/shard_map/all_to_all | solution.py:183
  23.2 0.8 %fusion.4 = f32[4,384,128]{2,1,0:T(8,128)S(1)} fusion(s32[4,384]{1,0:T(4,128)S(1)} %convert_element_type.88, f32[64,128]{1,0:T(8,128)S(1)} %copy-done), kind=kOutput, calls=%fused_computation.15 | convolution fusion | flops 151093248 | bytes 825344 | tf_op jit(solution)/shard_map/dot_general | solution.py:61
  24.0 0.7 %subtract_convert_fusion = (bf16[4,384,64]{2,1,0:T(8,128)(2,1)S(1)}, bf16[4,384,64]{2,1,0:T(8,128)(2,1)S(1)}) fusion(f32[4,384,128]{2,1,0:T(8,128)S(1)} %fusion.4, f32[4,384]{1,0:T(4,128)S(1)} %mul.183, f32[4,384]{1,0:T(4,128)S(1)} %mul.180), kind=kLoop, calls=%fused_computation.11 | loop fusion | flops 786432 | bytes 1191936 | tf_op jit(solution)/shard_map/convert
  24.7 1.0 %pad_maximum_fusion.w_ref = bf16[4,384,128]{2,1,0:T(8,128)(2,1)} fusion(bf16[4,384,64]{2,1,0:T(8,128)(2,1)S(1)} %get-tuple-element.6, bf16[4,384,64]{2,1,0:T(8,128)(2,1)S(1)} %get-tuple-element.5), kind=kLoop, calls=%fused_computation.13 | loop fusion | flops 786432 | bytes 786432 | tf_op jit(solution)/shard_map/concatenate | solution.py:72
  25.7 0.6 %broadcast_add_fusion = (s32[4,24,128]{2,1,0:T(8,128)}, s32[4,24,128]{2,1,0:T(8,128)}) fusion(s32[4,24,128]{2,1,0:T(8,128)S(1)} %add.158, s32[128]{0:T(128)S(1)} %add.160, s32[4,24,128]{2,1,0:T(8,128)S(1)} %copy.68, s32[128]{0:T(128)S(1)} %add.154), kind=kLoop, calls=%fused_computation.51 | loop fusion | flops 24576 | bytes 197632 | tf_op jit(solution)/shard_map/add | solution.py:198
  26.3 12.5 %shard_map.64 = f32[2,128,512]{2,1,0:T(8,128)} custom-call(bf16[4,384,128]{2,1,0:T(8,128)(2,1)} %pad_maximum_fusion.w_ref, s32[4,24,128]{2,1,0:T(8,128)} %get-tuple-element.33.vob_ref, s32[4,24,128]{2,1,0:T(8,128)} %get-tuple-element.32.uoa_ref, bf16[128,2048]{1,0:T(8,128)(2,1)} %fusion.3.e_ref), custom_call_target="tpu_custom_call" | custom-call | tf_op jit(solution)/shard_map/pallas_call | solution.py:136
  38.9 1.0 %copy-done.1 = f32[2,128,512]{2,1,0:T(8,128)S(1)} copy-done((f32[2,128,512]{2,1,0:T(8,128)S(1)}, f32[2,128,512]{2,1,0:T(8,128)}, u32[]{:S(2)}) %copy-start.1) | copy-done | bytes 524312
  40.2 1.4 %collective-permute-done = f32[2,64,512]{2,1,0:T(8,128)S(1)} collective-permute-done((f32[2,64,512]{2,1,0:T(8,128)S(1)}, f32[2,64,512]{2,1,0:T(8,128)S(1)}, u32[]{:S(2)}, u32[]{:S(2)}) %collective-permute-start) | collective-permute-done | bytes 262176 | tf_op jit(solution)/shard_map/ppermute | solution.py:214
  42.7 0.3 add_bitcast_fusion
  43.1 0.5 %fusion.9 = f32[128,64,8]{0,1,2:T(8,128)S(1)} fusion(f32[64,8,128]{2,1,0:T(8,128)S(1)} %get-tuple-element.7), kind=kOutput, calls=%fused_computation.25 | convolution fusion | flops 50561024 | bytes 524288 | tf_op jit(solution)/shard_map/rkj,jm->rmk/dot_general | solution.py:42
  43.6 0.5 %fusion.5 = f32[128,64,8]{0,1,2:T(8,128)S(1)} fusion(f32[64,8,128]{2,1,0:T(8,128)S(1)} %get-tuple-element.8), kind=kOutput, calls=%fused_computation.21 | convolution fusion | flops 50561024 | bytes 524288 | tf_op jit(solution)/shard_map/rkj,jm->rmk/dot_general | solution.py:45
  44.1 0.5 %fusion.1 = f32[64,128,8]{1,0,2:T(8,128)S(1)} fusion(f32[128,64,8]{0,1,2:T(8,128)S(1)} %fusion.9, f32[64,8,128]{2,1,0:T(8,128)S(1)} %get-tuple-element.8), kind=kOutput, calls=%fused_computation.3 | convolution fusion | flops 50626560 | bytes 786432 | tf_op jit(solution)/shard_map/rkj,jm->rmk/dot_general | solution.py:42
  45.0 0.5 %fusion = f32[64,128,8]{1,0,2:T(8,128)S(1)} fusion(f32[128,64,8]{0,1,2:T(8,128)S(1)} %fusion.5, f32[64,8,128]{2,1,0:T(8,128)S(1)} %get-tuple-element.7), kind=kOutput, calls=%fused_computation.1 | convolution fusion | flops 50626560 | bytes 786432 | tf_op jit(solution)/shard_map/rkj,jm->rmk/dot_general | solution.py:45
  46.0 1.2 %copy.78 = f32[64,2,1024]{2,1,0:T(2,128)} copy(f32[64,2,1024]{2,0,1:T(8,128)S(1)} %maximum_multiply_fusion) | data formatting | bytes 1048576 | tf_op jit(solution)/shard_map/mul | solution.py:50
  (66 shorter events, 5.6 us)
Async XLA Ops:
  0.0 23.2 %copy-start = (f32[64,128]{1,0:T(8,128)S(1)}, f32[64,128]{1,0:T(8,128)}, u32[]{:S(2)}) copy-start(f32[64,128]{1,0:T(8,128)} %param.11) | copy-start | bytes 98308
  0.8 0.7 %copy-start.5 = (s32[1,8,16]{2,1,0:T(8,128)S(1)}, s32[1,8,16]{2,1,0:T(8,128)}, u32[]{:S(2)}) copy-start(s32[1,8,16]{2,1,0:T(8,128)} %param.7) | copy-start | bytes 1540
  1.6 0.8 %copy-start.2 = (s32[1,8,16,12]{2,1,3,0:T(8,128)S(1)}, s32[1,8,16,12]{2,1,3,0:T(8,128)}, u32[]{:S(2)}) copy-start(s32[1,8,16,12]{2,1,3,0:T(8,128)} %param.8) | copy-start | bytes 18436
  2.4 0.8 %copy-start.3 = (s32[1,8,16,12]{2,1,3,0:T(8,128)S(1)}, s32[1,8,16,12]{2,1,3,0:T(8,128)}, u32[]{:S(2)}) copy-start(s32[1,8,16,12]{2,1,3,0:T(8,128)} %param.9) | copy-start | bytes 18436
  3.2 0.8 %copy-start.4 = (s32[1,8,16,12]{2,1,3,0:T(8,128)S(1)}, s32[1,8,16,12]{2,1,3,0:T(8,128)}, u32[]{:S(2)}) copy-start(s32[1,8,16,12]{2,1,3,0:T(8,128)} %param.10) | copy-start | bytes 18436
  5.6 14.6 %all-to-all-start = ((f32[32,1,240]{2,1,0:T(1,128)}), f32[32,1,240]{2,1,0:T(1,128)S(1)}, u32[]{:S(2)}, u32[]{:S(2)}) async-start(f32[32,1,240]{2,1,0:T(1,128)} %reshape.128), calls=%async_computation | async-start | bytes 65536 | tf_op jit(solution)/shard_map/all_to_all | solution.py:183
  38.9 1.0 %copy-start.1 = (f32[2,128,512]{2,1,0:T(8,128)S(1)}, f32[2,128,512]{2,1,0:T(8,128)}, u32[]{:S(2)}) copy-start(f32[2,128,512]{2,1,0:T(8,128)} %shard_map.64) | copy-start | bytes 1572868
  40.0 1.6 %collective-permute-start = (f32[2,64,512]{2,1,0:T(8,128)S(1)}, f32[2,64,512]{2,1,0:T(8,128)S(1)}, u32[]{:S(2)}, u32[]{:S(2)}) collective-permute-start(f32[2,64,512]{2,1,0:T(8,128)S(1)} %get-tuple-element.11), channel_id=1, source_target_pairs={{0,1},{1,0},{2,3},{3,2},{4,5},{5,4},{6,7},{7,6},{8,9},{9,8},{10,11... | collective-permute-start | bytes 786440 | tf_op jit(solution)/shard_map/ppermute | solution.py:214

commit v5 on v4

--- a/solution.py
+++ b/solution.py
@@ -72,20 +72,58 @@
     return jnp.concatenate([part_re, part_im], axis=-1).astype(jnp.bfloat16)
 
 
-def grid_kernel(w_ref, vob_ref, uoa_ref, e_ref, out_ref, rep_ref, x_ref, r_ref):
+def split3(values):
+    high = lax.reduce_precision(values, exponent_bits=8, mantissa_bits=7)
+    rest = values - high
+    middle = lax.reduce_precision(rest, exponent_bits=8, mantissa_bits=7)
+    low = rest - middle
+    return high.astype(jnp.bfloat16), middle.astype(jnp.bfloat16), low.astype(jnp.bfloat16)
+
+
+def grid_kernel(fld_ref, eye_ref, kt_ref, xv_ref, xu_ref, e_ref, out_ref, rep_ref, x_ref, r_ref, tab_ref):
     chunk_step = pl.program_id(1)
-    chunk = w_ref.shape[1]
+    chunk = fld_ref.shape[2]
     rows = out_ref.shape[1]
     ngroups = chunk // GROUP
-    nblocks = w_ref.shape[2] // SUPPORT
+    width = 2 * SUPPORT * SUPPORT
+    nblocks = width // SUPPORT
     depth = nblocks * GROUP // 2
+    nplanes = kt_ref.shape[0]
 
     @pl.when(chunk_step == 0)
     def _():
         out_ref[...] = jnp.zeros_like(out_ref)
 
+    fld = fld_ref[0]
+    cols = lax.dot_general(
+        eye_ref[...], fld, (((1,), (1,)), ((), ())), preferred_element_type=jnp.float32
+    )
+    nf = fld.shape[0] // 3
+    cols = (cols[:, 0:nf] + cols[:, nf:2 * nf]) + cols[:, 2 * nf:3 * nf]
+    vis_re = cols[:, 0:1]
+    vis_im = cols[:, 1:2]
+    planes = cols[:, 2:3].astype(jnp.int32)
+    onehot = (planes == lax.broadcasted_iota(jnp.int32, (chunk, nplanes), 1)).astype(jnp.bfloat16)
+    parts = jnp.dot(onehot, kt_ref[...], preferred_element_type=jnp.float32)
+    kern_a = (parts[:, 0:width] + parts[:, width:2 * width]) + parts[:, 2 * width:3 * width]
+    kern_b = (parts[:, 3 * width:4 * width] + parts[:, 4 * width:5 * width]) + parts[:, 5 * width:6 * width]
+    lane = lax.broadcasted_iota(jnp.int32, (chunk, width), 1)
+    signed_im = jnp.where(lane < width // 2, -vis_im, vis_im)
+    weighted = (vis_re * kern_a + signed_im * kern_b).astype(jnp.bfloat16)
+
+    gmask = (
+        lax.broadcasted_iota(jnp.int32, (ngroups, chunk), 1) // GROUP
+        == lax.broadcasted_iota(jnp.int32, (ngroups, chunk), 0)
+    )
+    zero_row = jnp.zeros((ngroups, chunk), jnp.bfloat16)
+    vo_rows = jnp.where(gmask, fld[4:5, :], zero_row)
+    uo_rows = jnp.where(gmask, fld[3:4, :], zero_row)
+    tlane = lax.broadcasted_iota(jnp.int32, (ngroups, TILE), 1)
+    tab_ref[0] = jnp.dot(vo_rows, xv_ref[...], preferred_element_type=jnp.float32).astype(jnp.int32) + tlane % SUPPORT
+    tab_ref[1] = jnp.dot(uo_rows, xu_ref[...], preferred_element_type=jnp.float32).astype(jnp.int32) + tlane // GROUP
+
     rep_ref[...] = jnp.dot(
-        w_ref[0], e_ref[...], preferred_element_type=jnp.float32
+        weighted, e_ref[...], preferred_element_type=jnp.float32
     ).astype(jnp.bfloat16)
     lane = lax.broadcasted_iota(jnp.int32, (GROUP, TILE), 1)
     row = lax.broadcasted_iota(jnp.int32, (GROUP, TILE), 0)
@@ -101,7 +139,7 @@
             for i in range(nblocks)
         ]
         wbd = jnp.concatenate(blocks, axis=0)
-        vob = vob_ref[0, pl.ds(g, 1), :]
+        vob = tab_ref[0, pl.ds(g, 1), :]
         cst = (vrow == vob).astype(jnp.bfloat16)
         spread = lax.dot_general(
             wbd, cst, (((1,), (1,)), ((), ())), preferred_element_type=jnp.float32
@@ -109,7 +147,7 @@
         at = pl.multiple_of(g * depth, depth)
         x_ref[0, pl.ds(at, depth), :] = spread[:depth]
         x_ref[1, pl.ds(at, depth), :] = spread[depth:]
-        uoa = uoa_ref[0, pl.ds(g, 1), :]
+        uoa = tab_ref[1, pl.ds(g, 1), :]
         r_ref[:, pl.ds(at, TILE)] = (urow == uoa).astype(jnp.bfloat16)
         return carry
 
@@ -119,28 +157,44 @@
     out_ref[1] += jnp.dot(pick, x_ref[1], preferred_element_type=jnp.float32)
 
 
-def grid_rows(weighted, vob, uoa, rows):
-    dests, per_dest, width = weighted.shape
+def grid_rows(fld, kernels, rows):
+    dests, nf, per_dest = fld.shape
     chunk = per_dest
     for size in (384, 192, 96, 48, 16):
         if per_dest % size == 0 and size <= per_dest:
             chunk = size
             break
     steps = per_dest // chunk
+    ngroups = chunk // GROUP
+    width = kernels.shape[1]
+    half = width // 2
     nblocks = width // SUPPORT
     lanes_in = lax.broadcasted_iota(jnp.int32, (width, nblocks * TILE), 0)
     lanes_out = lax.broadcasted_iota(jnp.int32, (width, nblocks * TILE), 1)
     expand = (
         (lanes_in // SUPPORT == lanes_out // TILE) & (lanes_in % SUPPORT == lanes_out % SUPPORT)
     ).astype(jnp.bfloat16)
+    eye = (
+        lax.broadcasted_iota(jnp.int32, (chunk, chunk), 0)
+        == lax.broadcasted_iota(jnp.int32, (chunk, chunk), 1)
+    ).astype(jnp.bfloat16)
+    swapped = jnp.concatenate([kernels[:, half:], kernels[:, :half]], axis=1)
+    table = jnp.concatenate(split3(kernels) + split3(swapped), axis=1)
+    n_in = lax.broadcasted_iota(jnp.int32, (chunk, TILE), 0) % GROUP
+    lane_t = lax.broadcasted_iota(jnp.int32, (chunk, TILE), 1)
+    expand_v = (n_in == lane_t // SUPPORT).astype(jnp.bfloat16)
+    expand_u = (n_in == lane_t % GROUP).astype(jnp.bfloat16)
+    whole = lambda d, c: (0, 0)
     return pl.pallas_call(
         grid_kernel,
         grid=(dests, steps),
         in_specs=[
-            pl.BlockSpec((1, chunk, width), lambda d, c: (d, c, 0)),
-            pl.BlockSpec((1, chunk // GROUP, TILE), lambda d, c: (d, c, 0)),
-            pl.BlockSpec((1, chunk // GROUP, TILE), lambda d, c: (d, c, 0)),
-            pl.BlockSpec((width, nblocks * TILE), lambda d, c: (0, 0)),
+            pl.BlockSpec((1, nf, chunk), lambda d, c: (d, 0, c)),
+            pl.BlockSpec((chunk, chunk), whole),
+            pl.BlockSpec(table.shape, whole),
+            pl.BlockSpec((chunk, TILE), whole),
+            pl.BlockSpec((chunk, TILE), whole),
+            pl.BlockSpec((width, nblocks * TILE), whole),
         ],
         out_specs=pl.BlockSpec((2, rows, TILE), lambda d, c: (0, 0, d)),
         out_shape=jax.ShapeDtypeStruct((2, rows, dests * TILE), jnp.float32),
@@ -148,11 +202,12 @@
             pltpu.VMEM((chunk, nblocks * TILE), jnp.bfloat16),
             pltpu.VMEM((2, chunk * SUPPORT, TILE), jnp.bfloat16),
             pltpu.VMEM((rows, chunk * SUPPORT), jnp.bfloat16),
+            pltpu.VMEM((2, ngroups, TILE), jnp.int32),
         ],
         compiler_params=pltpu.CompilerParams(
             dimension_semantics=("arbitrary", "arbitrary")
         ),
-    )(weighted, vob, uoa, expand)
+    )(fld, eye, table, expand_v, expand_u, expand)
 
 
 def shards(visibilities, tile_counts, w_plane, u_offset, v_offset, kernels):
@@ -182,23 +237,9 @@
     send = send.reshape(ndev, FIELDS, own_dests, slots)
     got = lax.all_to_all(send, axes, split_axis=0, concat_axis=0, tiled=True)
     got = got.transpose(1, 2, 0, 3).reshape(FIELDS, own_dests, ndev * slots)
-    vis_re = got[0]
-    vis_im = got[1]
-    planes = got[2].astype(jnp.int32)
-    rows_first = got[3].astype(jnp.int32)
-    cols_first = got[4].astype(jnp.int32)
-    if vis_re.size <= 65536:
-        weighted = weigh(vis_re, vis_im, planes, kernels)
-    else:
-        weighted = lax.map(lambda x: weigh(x[0], x[1], x[2], kernels), (vis_re, vis_im, planes))
-    per_dest = ndev * slots
-    ngroups = per_dest // GROUP
-    taps = jnp.arange(SUPPORT, dtype=jnp.int32)
-    vob = (cols_first.reshape(own_dests, ngroups, GROUP, 1) + taps).reshape(own_dests, ngroups, TILE)
-    uoa = (rows_first.reshape(own_dests, ngroups, 1, GROUP) + taps[:, None]).reshape(
-        own_dests, ngroups, TILE
-    )
-    slab = grid_rows(weighted, vob, uoa, TILE)
+    got = jnp.pad(got.transpose(1, 0, 2), ((0, 0), (0, 8 - FIELDS), (0, 0)))
+    got = jnp.concatenate(split3(got), axis=1)
+    slab = grid_rows(got, kernels, TILE)
     width = own_dests * TILE
     mine = lax.dynamic_slice_in_dim(slab, member * rows, rows, axis=1)
     full = jnp.zeros((2, rows, dests * TILE), jnp.float32)

time: 47.7 us -> 46.2 us (0.969)
  waiting for transfers between devices: 7.31 us -> 4.66 us
  Pallas kernels: 12.5 us -> 15.1 us
  local copies, waits for them, and re-layouts: 11 us -> 10.1 us
  matrix products: 4.1 us -> 3.28 us
    all_to_all x1, waiting for transfers between devices: 5.94 us -> 3.27 us  [shards(): got = lax.all_to_all(send, axes, split_axis=0, concat_axis=0, tiled=True)]
    pallas_call x1, Pallas kernels: 12.5 us -> 15.1 us  [grid_rows(): pl.pallas_call(grid_kernel, grid=(dests, steps), in_specs=[pl.BlockSpec((...]
    convert_element_type x1 -> x3, other arithmetic: 0.03 us -> 1.66 us  [the longest x1 0.91 us: grid_rows(): expand_u = (n_in == lane_t % GROUP).astype(jnp.bfloat16)]
    dot_general x1 -> x0, matrix products: 0.81 us -> none  [weigh(): jnp.dot(onehot.reshape(-1, nplanes), kernels, precision=lax.Precision.HIG...]
    unnamed x19 -> x21, local copies, waits for them, and re-layouts: 4.79 us -> 5.51 us
    another operation x1 -> x0, other arithmetic: 0.68 us -> none
    convert_element_type x7 -> x0, local copies, waits for them, and re-layouts: 0.67 us -> none  [the longest x3 0.27 us: shards(): cols_first = got[4].astype(jnp.int32)]
    add x2 -> x1, other arithmetic: 0.64 us -> 0.01 us  [grid_rows(): expand_u = (n_in == lane_t % GROUP).astype(jnp.bfloat16)]
  transfers between devices with their start and end apart: 2 -> 2, of which waited for: 2 -> 2; matrix products, arithmetic and copies ran while one was open for 3% -> 7% of each run, Pallas kernels for 0% -> 0%
where the time goes in v5:
time: 46.2 us; the launch traced here: 45.7 us
  Pallas kernels  15.1 us (33%)
  local copies, waits for them, and re-layouts  10.1 us (22%)
  starting transfers between devices  7.46 us (16%)
  other arithmetic  4.69 us (10%)
  waiting for transfers between devices  4.66 us (10%)
  matrix products  3.28 us (7%)
    pallas_call x1, Pallas kernels, grid_rows(): pl.pallas_call(grid_kernel, grid=(dests, steps), in_specs=[pl.BlockSpec((...  15.1 us
    all_to_all x1, starting transfers between devices, shards(): got = lax.all_to_all(send, axes, split_axis=0, concat_axis=0, tiled=True)  7.3 us
    unnamed x21, local copies, waits for them, and re-layouts  5.51 us
    all_to_all x1, waiting for transfers between devices, shards(): got = lax.all_to_all(send, axes, split_axis=0, concat_axis=0, tiled=True)  3.27 us
    ppermute x1, waiting for transfers between devices, shards(): piece = lax.ppermute(piece, axes, pairs)  1.39 us
    mul x1, local copies, waits for them, and re-layouts, transform(): jnp.stack([final_re.reshape(nrows, total), final_im.reshape(nrows, total)...  1.2 us
    convert_element_type x1, other arithmetic, grid_rows(): expand = ((lanes_in // SUPPORT == lanes_out // TILE) & (lanes_in % SUPPOR...  1.05 us
  transfers between devices with their start and end apart: 2, of which 2 were waited for; matrix products, arithmetic and copies ran while one was open for 7% of the time, Pallas kernels for 0%

profile of v5, /device:TPU:0, one launch (start us, length us, event | category | flops | bytes accessed | tf_op | source)
XLA Modules:
  0.0 45.7 jit_solution(8864930649544457762)
XLA Ops:
  0.0 0.8 %fusion.101 = (f32[1,1,8,16,12]{3,2,4,1,0:T(8,128)S(1)}, f32[1,1,8,16,12]{3,2,4,1,0:T(8,128)S(1)}) fusion(f32[2,1,8,16,12]{3,2,4,1,0:T(8,128)} %param.6), kind=kLoop, calls=%fused_computation.161 | loop fusion | bytes 24576 | tf_op jit(solution)/shard_map/slice | solution.py:230
  1.0 0.5 %copy-done.6 = s32[1,8,16]{2,1,0:T(8,128)S(1)} copy-done((s32[1,8,16]{2,1,0:T(8,128)S(1)}, s32[1,8,16]{2,1,0:T(8,128)}, u32[]{:S(2)}) %copy-start.6) | copy-done | bytes 536
  1.7 0.7 %copy-done.3 = s32[1,8,16,12]{2,1,3,0:T(8,128)S(1)} copy-done((s32[1,8,16,12]{2,1,3,0:T(8,128)S(1)}, s32[1,8,16,12]{2,1,3,0:T(8,128)}, u32[]{:S(2)}) %copy-start.3) | copy-done | bytes 6168
  2.6 0.7 %copy-done.4 = s32[1,8,16,12]{2,1,3,0:T(8,128)S(1)} copy-done((s32[1,8,16,12]{2,1,3,0:T(8,128)S(1)}, s32[1,8,16,12]{2,1,3,0:T(8,128)}, u32[]{:S(2)}) %copy-start.4) | copy-done | bytes 6168
  3.4 0.7 %copy-done.5 = s32[1,8,16,12]{2,1,3,0:T(8,128)S(1)} copy-done((s32[1,8,16,12]{2,1,3,0:T(8,128)S(1)}, s32[1,8,16,12]{2,1,3,0:T(8,128)}, u32[]{:S(2)}) %copy-start.5) | copy-done | bytes 6168
  4.5 0.9 %reshape.82 = f32[32,1,240]{2,1,0:T(1,128)} reshape(f32[32,5,4,12]{3,2,1,0:T(4,128)S(1)} %bitcast.66) | data formatting | bytes 61440
  5.3 7.3 %all-to-all-start = ((f32[32,1,240]{2,1,0:T(1,128)}), f32[32,1,240]{2,1,0:T(1,128)S(1)}, u32[]{:S(2)}, u32[]{:S(2)}) async-start(f32[32,1,240]{2,1,0:T(1,128)} %reshape.82), calls=%async_computation | async-start | bytes 65536 | tf_op jit(solution)/shard_map/all_to_all | solution.py:238
  12.7 0.7 %copy-done.1 = f32[64,128]{1,0:T(8,128)S(1)} copy-done((f32[64,128]{1,0:T(8,128)S(1)}, f32[64,128]{1,0:T(8,128)}, u32[]{:S(2)}) %copy-start.1) | copy-done | bytes 32792
  13.6 0.7 %fusion.4.eye_ref = bf16[384,384]{1,0:T(8,128)(2,1)} fusion(), kind=kLoop, calls=%fused_computation.11 | loop fusion | flops 294912 | bytes 294912 | tf_op jit(solution)/shard_map/convert_element_type | solution.py:180
  14.6 0.9 %fusion.12 = (bf16[384,128]{1,0:T(8,128)(2,1)}, bf16[384,128]{1,0:T(8,128)(2,1)}) fusion(s32[128]{0:T(128)S(1)} %get-tuple-element.25, s32[128]{0:T(128)S(1)} %get-tuple-element.26, s32[384]{0:T(512)S(1)} %get-tuple-element.22, s32[384]{0:T(512)S(1)} %get-tuple-element.23, pred[384]{0:T(512)(128)(4,1)S(1)} %fusion.68, ...), kind=kLoop, calls=%fused_computation.27 | loop fusion | flops 344064 | bytes 202368 | tf_op jit(solution)/shard_map/convert_element_type | solution.py:186
  15.5 1.0 %fusion.3.e_ref = bf16[128,2048]{1,0:T(8,128)(2,1)} fusion(s32[2048]{0:T(1024)S(1)} %get-tuple-element.28, s32[2048]{0:T(1024)S(1)} %get-tuple-element.30, s32[128]{0:T(128)S(1)} %get-tuple-element.34, s32[128]{0:T(128)S(1)} %get-tuple-element.35, s32[2048]{0:T(1024)S(1)} %get-tuple-element.29, s32[2048]{0:T(1024)S(1)} %get-tuple-element.31, ...), kind=kLoop, calls=%fused_computation.9 | loop fusion | flops 2097152 | bytes 563456 | tf_op jit(solution)/shard_map/convert_element_type | solution.py:176
  16.6 3.3 %all-to-all-done = f32[32,1,240]{2,1,0:T(1,128)S(1)} async-done(((f32[32,1,240]{2,1,0:T(1,128)}), f32[32,1,240]{2,1,0:T(1,128)S(1)}, u32[]{:S(2)}, u32[]{:S(2)}) %all-to-all-start) | async-done | bytes 30752 | tf_op jit(solution)/shard_map/all_to_all | solution.py:238
  19.9 0.6 %broadcast.275 = f32[]{:T(128)} broadcast(f32[]{:T(128)} %constant.348), dimensions={} | broadcast | bytes 8 | tf_op jit(solution)/shard_map/all_to_all | solution.py:238
  20.5 0.7 %reduce = f32[32,240]{1,0:T(8,128)S(1)} reduce(f32[32,1,240]{2,1,0:T(1,128)S(1)} %all-to-all-done, f32[]{:T(128)} %broadcast.275), dimensions={1}, to_apply=%all_to_all.3.reduce_sub_computation | reduce | bytes 61444 | tf_op jit(solution)/shard_map/all_to_all | solution.py:238
  21.7 0.6 %pad_maximum_fusion.fld_ref = bf16[4,24,384]{2,1,0:T(8,128)(2,1)} fusion(bf16[4,8,384]{2,1,0:T(8,128)(2,1)S(1)} %get-tuple-element.14, bf16[4,8,384]{2,1,0:T(8,128)(2,1)S(1)} %get-tuple-element.15, bf16[4,8,384]{2,1,0:T(8,128)(2,1)S(1)} %get-tuple-element.13), kind=kLoop, calls=%fused_computation.31 | loop fusion | flops 221184 | bytes 147456 | tf_op jit(solution)/shard_map/concatenate | solution.py:241
  22.3 15.1 %shard_map.64 = f32[2,128,512]{2,1,0:T(8,128)} custom-call(bf16[4,24,384]{2,1,0:T(8,128)(2,1)} %pad_maximum_fusion.fld_ref, bf16[384,384]{1,0:T(8,128)(2,1)} %fusion.4.eye_ref, bf16[64,768]{1,0:T(8,128)(2,1)} %copy-done.2, bf16[384,128]{1,0:T(8,128)(2,1)} %get-tuple-element.19.xv_ref, bf16[384,128]{1,0:T(8,128)(2,1)} %get-tuple-element.18.xu_ref, ...), custom_call_target="tpu_custom_call" | custom-call | tf_op jit(solution)/shard_map/pallas_call | solution.py:188
  37.4 1.0 %copy-done = f32[2,128,512]{2,1,0:T(8,128)S(1)} copy-done((f32[2,128,512]{2,1,0:T(8,128)S(1)}, f32[2,128,512]{2,1,0:T(8,128)}, u32[]{:S(2)}) %copy-start) | copy-done | bytes 524312
  38.7 1.4 %collective-permute-done = f32[2,64,512]{2,1,0:T(8,128)S(1)} collective-permute-done((f32[2,64,512]{2,1,0:T(8,128)S(1)}, f32[2,64,512]{2,1,0:T(8,128)S(1)}, u32[]{:S(2)}, u32[]{:S(2)}) %collective-permute-start) | collective-permute-done | bytes 262176 | tf_op jit(solution)/shard_map/ppermute | solution.py:255
  41.2 0.3 add_bitcast_fusion
  41.5 0.5 %fusion.9 = f32[128,64,8]{0,1,2:T(8,128)S(1)} fusion(f32[64,8,128]{2,1,0:T(8,128)S(1)} %get-tuple-element.5), kind=kOutput, calls=%fused_computation.24 | convolution fusion | flops 50561024 | bytes 524288 | tf_op jit(solution)/shard_map/rkj,jm->rmk/dot_general | solution.py:42
  42.1 0.5 %fusion.5 = f32[128,64,8]{0,1,2:T(8,128)S(1)} fusion(f32[64,8,128]{2,1,0:T(8,128)S(1)} %get-tuple-element.6), kind=kOutput, calls=%fused_computation.20 | convolution fusion | flops 50561024 | bytes 524288 | tf_op jit(solution)/shard_map/rkj,jm->rmk/dot_general | solution.py:45
  42.6 0.5 %fusion.1 = f32[64,128,8]{1,0,2:T(8,128)S(1)} fusion(f32[128,64,8]{0,1,2:T(8,128)S(1)} %fusion.9, f32[64,8,128]{2,1,0:T(8,128)S(1)} %get-tuple-element.6), kind=kOutput, calls=%fused_computation.3 | convolution fusion | flops 50626560 | bytes 786432 | tf_op jit(solution)/shard_map/rkj,jm->rmk/dot_general | solution.py:42
  43.5 0.5 %fusion = f32[64,128,8]{1,0,2:T(8,128)S(1)} fusion(f32[128,64,8]{0,1,2:T(8,128)S(1)} %fusion.5, f32[64,8,128]{2,1,0:T(8,128)S(1)} %get-tuple-element.5), kind=kOutput, calls=%fused_computation.1 | convolution fusion | flops 50626560 | bytes 786432 | tf_op jit(solution)/shard_map/rkj,jm->rmk/dot_general | solution.py:45
  44.5 1.2 %copy.52 = f32[64,2,1024]{2,1,0:T(2,128)} copy(f32[64,2,1024]{2,0,1:T(8,128)S(1)} %maximum_multiply_fusion) | data formatting | bytes 1048576 | tf_op jit(solution)/shard_map/mul | solution.py:50
  (59 shorter events, 4.2 us)
Async XLA Ops:
  0.8 0.7 %copy-start.6 = (s32[1,8,16]{2,1,0:T(8,128)S(1)}, s32[1,8,16]{2,1,0:T(8,128)}, u32[]{:S(2)}) copy-start(s32[1,8,16]{2,1,0:T(8,128)} %param.7) | copy-start | bytes 1540
  1.6 0.8 %copy-start.3 = (s32[1,8,16,12]{2,1,3,0:T(8,128)S(1)}, s32[1,8,16,12]{2,1,3,0:T(8,128)}, u32[]{:S(2)}) copy-start(s32[1,8,16,12]{2,1,3,0:T(8,128)} %param.8) | copy-start | bytes 18436
  2.4 0.8 %copy-start.4 = (s32[1,8,16,12]{2,1,3,0:T(8,128)S(1)}, s32[1,8,16,12]{2,1,3,0:T(8,128)}, u32[]{:S(2)}) copy-start(s32[1,8,16,12]{2,1,3,0:T(8,128)} %param.9) | copy-start | bytes 18436
  3.2 0.8 %copy-start.5 = (s32[1,8,16,12]{2,1,3,0:T(8,128)S(1)}, s32[1,8,16,12]{2,1,3,0:T(8,128)}, u32[]{:S(2)}) copy-start(s32[1,8,16,12]{2,1,3,0:T(8,128)} %param.10) | copy-start | bytes 18436
  5.3 14.6 %all-to-all-start = ((f32[32,1,240]{2,1,0:T(1,128)}), f32[32,1,240]{2,1,0:T(1,128)S(1)}, u32[]{:S(2)}, u32[]{:S(2)}) async-start(f32[32,1,240]{2,1,0:T(1,128)} %reshape.82), calls=%async_computation | async-start | bytes 65536 | tf_op jit(solution)/shard_map/all_to_all | solution.py:238
  12.6 0.8 %copy-start.1 = (f32[64,128]{1,0:T(8,128)S(1)}, f32[64,128]{1,0:T(8,128)}, u32[]{:S(2)}) copy-start(f32[64,128]{1,0:T(8,128)} %param.11) | copy-start | bytes 98308
  16.6 4.8 %copy-start.2 = (bf16[64,768]{1,0:T(8,128)(2,1)}, bf16[64,768]{1,0:T(8,128)(2,1)S(1)}, u32[]{:S(2)}) copy-start(bf16[64,768]{1,0:T(8,128)(2,1)S(1)} %constant_dynamic-update-slice_fusion.3.kt_ref) | copy-start | bytes 294916
  37.4 1.0 %copy-start = (f32[2,128,512]{2,1,0:T(8,128)S(1)}, f32[2,128,512]{2,1,0:T(8,128)}, u32[]{:S(2)}) copy-start(f32[2,128,512]{2,1,0:T(8,128)} %shard_map.64) | copy-start | bytes 1572868
  38.5 1.6 %collective-permute-start = (f32[2,64,512]{2,1,0:T(8,128)S(1)}, f32[2,64,512]{2,1,0:T(8,128)S(1)}, u32[]{:S(2)}, u32[]{:S(2)}) collective-permute-start(f32[2,64,512]{2,1,0:T(8,128)S(1)} %get-tuple-element.9), channel_id=1, source_target_pairs={{0,1},{1,0},{2,3},{3,2},{4,5},{5,4},{6,7},{7,6},{8,9},{9,8},{10,11... | collective-permute-start | bytes 786440 | tf_op jit(solution)/shard_map/ppermute | solution.py:255

commit v6 on v5

--- a/solution.py
+++ b/solution.py
@@ -151,7 +151,7 @@
         r_ref[:, pl.ds(at, TILE)] = (urow == uoa).astype(jnp.bfloat16)
         return carry
 
-    lax.fori_loop(0, ngroups, body, 0, unroll=4)
+    lax.fori_loop(0, ngroups, body, 0, unroll=True)
     pick = r_ref[...]
     out_ref[0] += jnp.dot(pick, x_ref[0], preferred_element_type=jnp.float32)
     out_ref[1] += jnp.dot(pick, x_ref[1], preferred_element_type=jnp.float32)

time: 46.2 us -> 41.2 us (0.89)
  Pallas kernels: 15.1 us -> 10 us
    pallas_call x1, Pallas kernels: 15.1 us -> 10 us  [grid_rows(): pl.pallas_call(grid_kernel, grid=(dests, steps), in_specs=[pl.BlockSpec((...]
  transfers between devices with their start and end apart: 2 -> 2, of which waited for: 2 -> 2; matrix products, arithmetic and copies ran while one was open for 7% -> 8% of each run, Pallas kernels for 0% -> 0%
where the time goes in v6:
time: 41.2 us; the launch traced here: 40.7 us
  local copies, waits for them, and re-layouts  10.1 us (25%)
  Pallas kernels  10 us (24%)
  starting transfers between devices  7.48 us (18%)
  other arithmetic  4.69 us (11%)
  waiting for transfers between devices  4.64 us (11%)
  matrix products  3.28 us (8%)
    pallas_call x1, Pallas kernels, grid_rows(): pl.pallas_call(grid_kernel, grid=(dests, steps), in_specs=[pl.BlockSpec((...  10 us
    all_to_all x1, starting transfers between devices, shards(): got = lax.all_to_all(send, axes, split_axis=0, concat_axis=0, tiled=True)  7.3 us
    unnamed x21, local copies, waits for them, and re-layouts  5.51 us
    all_to_all x1, waiting for transfers between devices, shards(): got = lax.all_to_all(send, axes, split_axis=0, concat_axis=0, tiled=True)  3.27 us
    ppermute x1, waiting for transfers between devices, shards(): piece = lax.ppermute(piece, axes, pairs)  1.37 us
    mul x1, local copies, waits for them, and re-layouts, transform(): jnp.stack([final_re.reshape(nrows, total), final_im.reshape(nrows, total)...  1.2 us
    convert_element_type x1, other arithmetic, grid_rows(): expand = ((lanes_in // SUPPORT == lanes_out // TILE) & (lanes_in % SUPPOR...  1.05 us
    convert_element_type x1, other arithmetic, grid_rows(): expand_u = (n_in == lane_t % GROUP).astype(jnp.bfloat16)  0.91 us
  transfers between devices with their start and end apart: 2, of which 2 were waited for; matrix products, arithmetic and copies ran while one was open for 8% of the time, Pallas kernels for 0%

profile of v6, /device:TPU:0, one launch (start us, length us, event | category | flops | bytes accessed | tf_op | source)
XLA Modules:
  0.0 40.7 jit_solution(18291112126847651500)
XLA Ops:
  0.0 0.8 %fusion.101 = (f32[1,1,8,16,12]{3,2,4,1,0:T(8,128)S(1)}, f32[1,1,8,16,12]{3,2,4,1,0:T(8,128)S(1)}) fusion(f32[2,1,8,16,12]{3,2,4,1,0:T(8,128)} %param.6), kind=kLoop, calls=%fused_computation.161 | loop fusion | bytes 24576 | tf_op jit(solution)/shard_map/slice | solution.py:230
  1.0 0.5 %copy-done.6 = s32[1,8,16]{2,1,0:T(8,128)S(1)} copy-done((s32[1,8,16]{2,1,0:T(8,128)S(1)}, s32[1,8,16]{2,1,0:T(8,128)}, u32[]{:S(2)}) %copy-start.6) | copy-done | bytes 536
  1.7 0.7 %copy-done.3 = s32[1,8,16,12]{2,1,3,0:T(8,128)S(1)} copy-done((s32[1,8,16,12]{2,1,3,0:T(8,128)S(1)}, s32[1,8,16,12]{2,1,3,0:T(8,128)}, u32[]{:S(2)}) %copy-start.3) | copy-done | bytes 6168
  2.6 0.7 %copy-done.4 = s32[1,8,16,12]{2,1,3,0:T(8,128)S(1)} copy-done((s32[1,8,16,12]{2,1,3,0:T(8,128)S(1)}, s32[1,8,16,12]{2,1,3,0:T(8,128)}, u32[]{:S(2)}) %copy-start.4) | copy-done | bytes 6168
  3.4 0.7 %copy-done.5 = s32[1,8,16,12]{2,1,3,0:T(8,128)S(1)} copy-done((s32[1,8,16,12]{2,1,3,0:T(8,128)S(1)}, s32[1,8,16,12]{2,1,3,0:T(8,128)}, u32[]{:S(2)}) %copy-start.5) | copy-done | bytes 6168
  4.5 0.9 %reshape.82 = f32[32,1,240]{2,1,0:T(1,128)} reshape(f32[32,5,4,12]{3,2,1,0:T(4,128)S(1)} %bitcast.66) | data formatting | bytes 61440
  5.3 7.3 %all-to-all-start = ((f32[32,1,240]{2,1,0:T(1,128)}), f32[32,1,240]{2,1,0:T(1,128)S(1)}, u32[]{:S(2)}, u32[]{:S(2)}) async-start(f32[32,1,240]{2,1,0:T(1,128)} %reshape.82), calls=%async_computation | async-start | bytes 65536 | tf_op jit(solution)/shard_map/all_to_all | solution.py:238
  12.7 0.7 %copy-done.1 = f32[64,128]{1,0:T(8,128)S(1)} copy-done((f32[64,128]{1,0:T(8,128)S(1)}, f32[64,128]{1,0:T(8,128)}, u32[]{:S(2)}) %copy-start.1) | copy-done | bytes 32792
  13.6 0.7 %fusion.4.eye_ref = bf16[384,384]{1,0:T(8,128)(2,1)} fusion(), kind=kLoop, calls=%fused_computation.11 | loop fusion | flops 294912 | bytes 294912 | tf_op jit(solution)/shard_map/convert_element_type | solution.py:180
  14.6 0.9 %fusion.12 = (bf16[384,128]{1,0:T(8,128)(2,1)}, bf16[384,128]{1,0:T(8,128)(2,1)}) fusion(s32[128]{0:T(128)S(1)} %get-tuple-element.25, s32[128]{0:T(128)S(1)} %get-tuple-element.26, s32[384]{0:T(512)S(1)} %get-tuple-element.22, s32[384]{0:T(512)S(1)} %get-tuple-element.23, pred[384]{0:T(512)(128)(4,1)S(1)} %fusion.68, ...), kind=kLoop, calls=%fused_computation.27 | loop fusion | flops 344064 | bytes 202368 | tf_op jit(solution)/shard_map/convert_element_type | solution.py:186
  15.5 1.0 %fusion.3.e_ref = bf16[128,2048]{1,0:T(8,128)(2,1)} fusion(s32[2048]{0:T(1024)S(1)} %get-tuple-element.28, s32[2048]{0:T(1024)S(1)} %get-tuple-element.30, s32[128]{0:T(128)S(1)} %get-tuple-element.34, s32[128]{0:T(128)S(1)} %get-tuple-element.35, s32[2048]{0:T(1024)S(1)} %get-tuple-element.29, s32[2048]{0:T(1024)S(1)} %get-tuple-element.31, ...), kind=kLoop, calls=%fused_computation.9 | loop fusion | flops 2097152 | bytes 563456 | tf_op jit(solution)/shard_map/convert_element_type | solution.py:176
  16.6 3.3 %all-to-all-done = f32[32,1,240]{2,1,0:T(1,128)S(1)} async-done(((f32[32,1,240]{2,1,0:T(1,128)}), f32[32,1,240]{2,1,0:T(1,128)S(1)}, u32[]{:S(2)}, u32[]{:S(2)}) %all-to-all-start) | async-done | bytes 30752 | tf_op jit(solution)/shard_map/all_to_all | solution.py:238
  19.9 0.6 %broadcast.275 = f32[]{:T(128)} broadcast(f32[]{:T(128)} %constant.348), dimensions={} | broadcast | bytes 8 | tf_op jit(solution)/shard_map/all_to_all | solution.py:238
  20.5 0.7 %reduce = f32[32,240]{1,0:T(8,128)S(1)} reduce(f32[32,1,240]{2,1,0:T(1,128)S(1)} %all-to-all-done, f32[]{:T(128)} %broadcast.275), dimensions={1}, to_apply=%all_to_all.3.reduce_sub_computation | reduce | bytes 61444 | tf_op jit(solution)/shard_map/all_to_all | solution.py:238
  21.7 0.6 %pad_maximum_fusion.fld_ref = bf16[4,24,384]{2,1,0:T(8,128)(2,1)} fusion(bf16[4,8,384]{2,1,0:T(8,128)(2,1)S(1)} %get-tuple-element.14, bf16[4,8,384]{2,1,0:T(8,128)(2,1)S(1)} %get-tuple-element.15, bf16[4,8,384]{2,1,0:T(8,128)(2,1)S(1)} %get-tuple-element.13), kind=kLoop, calls=%fused_computation.31 | loop fusion | flops 221184 | bytes 147456 | tf_op jit(solution)/shard_map/concatenate | solution.py:241
  22.3 10.0 %shard_map.64 = f32[2,128,512]{2,1,0:T(8,128)} custom-call(bf16[4,24,384]{2,1,0:T(8,128)(2,1)} %pad_maximum_fusion.fld_ref, bf16[384,384]{1,0:T(8,128)(2,1)} %fusion.4.eye_ref, bf16[64,768]{1,0:T(8,128)(2,1)} %copy-done.2, bf16[384,128]{1,0:T(8,128)(2,1)} %get-tuple-element.19.xv_ref, bf16[384,128]{1,0:T(8,128)(2,1)} %get-tuple-element.18.xu_ref, ...), custom_call_target="tpu_custom_call" | custom-call | tf_op jit(solution)/shard_map/pallas_call | solution.py:188
  32.4 1.0 %copy-done = f32[2,128,512]{2,1,0:T(8,128)S(1)} copy-done((f32[2,128,512]{2,1,0:T(8,128)S(1)}, f32[2,128,512]{2,1,0:T(8,128)}, u32[]{:S(2)}) %copy-start) | copy-done | bytes 524312
  33.7 1.4 %collective-permute-done = f32[2,64,512]{2,1,0:T(8,128)S(1)} collective-permute-done((f32[2,64,512]{2,1,0:T(8,128)S(1)}, f32[2,64,512]{2,1,0:T(8,128)S(1)}, u32[]{:S(2)}, u32[]{:S(2)}) %collective-permute-start) | collective-permute-done | bytes 262176 | tf_op jit(solution)/shard_map/ppermute | solution.py:255
  36.2 0.3 add_bitcast_fusion
  36.5 0.5 %fusion.9 = f32[128,64,8]{0,1,2:T(8,128)S(1)} fusion(f32[64,8,128]{2,1,0:T(8,128)S(1)} %get-tuple-element.5), kind=kOutput, calls=%fused_computation.24 | convolution fusion | flops 50561024 | bytes 524288 | tf_op jit(solution)/shard_map/rkj,jm->rmk/dot_general | solution.py:42
  37.0 0.5 %fusion.5 = f32[128,64,8]{0,1,2:T(8,128)S(1)} fusion(f32[64,8,128]{2,1,0:T(8,128)S(1)} %get-tuple-element.6), kind=kOutput, calls=%fused_computation.20 | convolution fusion | flops 50561024 | bytes 524288 | tf_op jit(solution)/shard_map/rkj,jm->rmk/dot_general | solution.py:45
  37.5 0.5 %fusion.1 = f32[64,128,8]{1,0,2:T(8,128)S(1)} fusion(f32[128,64,8]{0,1,2:T(8,128)S(1)} %fusion.9, f32[64,8,128]{2,1,0:T(8,128)S(1)} %get-tuple-element.6), kind=kOutput, calls=%fused_computation.3 | convolution fusion | flops 50626560 | bytes 786432 | tf_op jit(solution)/shard_map/rkj,jm->rmk/dot_general | solution.py:42
  38.5 0.5 %fusion = f32[64,128,8]{1,0,2:T(8,128)S(1)} fusion(f32[128,64,8]{0,1,2:T(8,128)S(1)} %fusion.5, f32[64,8,128]{2,1,0:T(8,128)S(1)} %get-tuple-element.5), kind=kOutput, calls=%fused_computation.1 | convolution fusion | flops 50626560 | bytes 786432 | tf_op jit(solution)/shard_map/rkj,jm->rmk/dot_general | solution.py:45
  39.5 1.2 %copy.52 = f32[64,2,1024]{2,1,0:T(2,128)} copy(f32[64,2,1024]{2,0,1:T(8,128)S(1)} %maximum_multiply_fusion) | data formatting | bytes 1048576 | tf_op jit(solution)/shard_map/mul | solution.py:50
  (59 shorter events, 4.2 us)
Async XLA Ops:
  0.8 0.7 %copy-start.6 = (s32[1,8,16]{2,1,0:T(8,128)S(1)}, s32[1,8,16]{2,1,0:T(8,128)}, u32[]{:S(2)}) copy-start(s32[1,8,16]{2,1,0:T(8,128)} %param.7) | copy-start | bytes 1540
  1.6 0.8 %copy-start.3 = (s32[1,8,16,12]{2,1,3,0:T(8,128)S(1)}, s32[1,8,16,12]{2,1,3,0:T(8,128)}, u32[]{:S(2)}) copy-start(s32[1,8,16,12]{2,1,3,0:T(8,128)} %param.8) | copy-start | bytes 18436
  2.4 0.8 %copy-start.4 = (s32[1,8,16,12]{2,1,3,0:T(8,128)S(1)}, s32[1,8,16,12]{2,1,3,0:T(8,128)}, u32[]{:S(2)}) copy-start(s32[1,8,16,12]{2,1,3,0:T(8,128)} %param.9) | copy-start | bytes 18436
  3.2 0.8 %copy-start.5 = (s32[1,8,16,12]{2,1,3,0:T(8,128)S(1)}, s32[1,8,16,12]{2,1,3,0:T(8,128)}, u32[]{:S(2)}) copy-start(s32[1,8,16,12]{2,1,3,0:T(8,128)} %param.10) | copy-start | bytes 18436
  5.3 14.6 %all-to-all-start = ((f32[32,1,240]{2,1,0:T(1,128)}), f32[32,1,240]{2,1,0:T(1,128)S(1)}, u32[]{:S(2)}, u32[]{:S(2)}) async-start(f32[32,1,240]{2,1,0:T(1,128)} %reshape.82), calls=%async_computation | async-start | bytes 65536 | tf_op jit(solution)/shard_map/all_to_all | solution.py:238
  12.6 0.8 %copy-start.1 = (f32[64,128]{1,0:T(8,128)S(1)}, f32[64,128]{1,0:T(8,128)}, u32[]{:S(2)}) copy-start(f32[64,128]{1,0:T(8,128)} %param.11) | copy-start | bytes 98308
  16.6 4.8 %copy-start.2 = (bf16[64,768]{1,0:T(8,128)(2,1)}, bf16[64,768]{1,0:T(8,128)(2,1)S(1)}, u32[]{:S(2)}) copy-start(bf16[64,768]{1,0:T(8,128)(2,1)S(1)} %constant_dynamic-update-slice_fusion.3.kt_ref) | copy-start | bytes 294916
  32.3 1.0 %copy-start = (f32[2,128,512]{2,1,0:T(8,128)S(1)}, f32[2,128,512]{2,1,0:T(8,128)}, u32[]{:S(2)}) copy-start(f32[2,128,512]{2,1,0:T(8,128)} %shard_map.64) | copy-start | bytes 1572868
  33.4 1.6 %collective-permute-start = (f32[2,64,512]{2,1,0:T(8,128)S(1)}, f32[2,64,512]{2,1,0:T(8,128)S(1)}, u32[]{:S(2)}, u32[]{:S(2)}) collective-permute-start(f32[2,64,512]{2,1,0:T(8,128)S(1)} %get-tuple-element.9), channel_id=1, source_target_pairs={{0,1},{1,0},{2,3},{3,2},{4,5},{5,4},{6,7},{7,6},{8,9},{9,8},{10,11... | collective-permute-start | bytes 786440 | tf_op jit(solution)/shard_map/ppermute | solution.py:255

commit v7 on v6

--- a/solution.py
+++ b/solution.py
@@ -224,20 +224,22 @@
     live = (
         lax.broadcasted_iota(jnp.int32, (dests, ntiles, slots), 2) < tile_counts[0][:, :, None]
     ).astype(jnp.float32)
-    fields = jnp.stack(
+    fields = jnp.concatenate(
         [
             visibilities[0, 0] * live,
             visibilities[1, 0] * live,
             w_plane[0].astype(jnp.float32),
             u_offset[0].astype(jnp.float32),
             v_offset[0].astype(jnp.float32),
-        ]
-    )
-    send = fields.reshape(FIELDS, per_tile, own_dests, ntiles, slots).transpose(3, 1, 0, 2, 4)
-    send = send.reshape(ndev, FIELDS, own_dests, slots)
+        ],
+        axis=-1,
+    )
+    send = fields.reshape(per_tile, own_dests, ntiles, FIELDS * slots).transpose(2, 0, 1, 3)
+    send = send.reshape(ndev, own_dests * FIELDS * slots)
     got = lax.all_to_all(send, axes, split_axis=0, concat_axis=0, tiled=True)
-    got = got.transpose(1, 2, 0, 3).reshape(FIELDS, own_dests, ndev * slots)
-    got = jnp.pad(got.transpose(1, 0, 2), ((0, 0), (0, 8 - FIELDS), (0, 0)))
+    got = got.reshape(ndev, own_dests, FIELDS, slots).transpose(1, 2, 0, 3)
+    got = got.reshape(own_dests, FIELDS, ndev * slots)
+    got = jnp.pad(got, ((0, 0), (0, 8 - FIELDS), (0, 0)))
     got = jnp.concatenate(split3(got), axis=1)
     slab = grid_rows(got, kernels, TILE)
     width = own_dests * TILE

time: 41.2 us -> 39.3 us (0.954)
  local copies, waits for them, and re-layouts: 10.1 us -> 9.1 us
  other arithmetic: 4.69 us -> 3.92 us
    unnamed x21 -> x17, local copies, waits for them, and re-layouts: 5.51 us -> 3.77 us
    all_to_all x1 -> x0, other arithmetic: 0.7 us -> none  [shards(): got = lax.all_to_all(send, axes, split_axis=0, concat_axis=0, tiled=True)]
    another operation x4 -> x0, local copies, waits for them, and re-layouts: 0.42 us -> none  [shards(): jnp.stack([visibilities[0, 0] * live, visibilities[1, 0] * live, w_plane[...]
    all_to_all x1 -> x2, local copies, waits for them, and re-layouts: 0.57 us -> 0.85 us  [shards(): got = lax.all_to_all(send, axes, split_axis=0, concat_axis=0, tiled=True)]
where the time goes in v7:
time: 39.3 us; the launch traced here: 38.8 us
  Pallas kernels  10 us (25%)
  local copies, waits for them, and re-layouts  9.1 us (23%)
  starting transfers between devices  7.48 us (19%)
  waiting for transfers between devices  4.61 us (12%)
  other arithmetic  3.92 us (10%)
  matrix products  3.29 us (8%)
    pallas_call x1, Pallas kernels, grid_rows(): pl.pallas_call(grid_kernel, grid=(dests, steps), in_specs=[pl.BlockSpec((...  10 us
    all_to_all x1, starting transfers between devices, shards(): got = lax.all_to_all(send, axes, split_axis=0, concat_axis=0, tiled=True)  7.3 us
    unnamed x17, local copies, waits for them, and re-layouts  3.77 us
    all_to_all x1, waiting for transfers between devices, shards(): got = lax.all_to_all(send, axes, split_axis=0, concat_axis=0, tiled=True)  3.24 us
    ppermute x1, waiting for transfers between devices, shards(): piece = lax.ppermute(piece, axes, pairs)  1.37 us
    mul x1, local copies, waits for them, and re-layouts, transform(): jnp.stack([final_re.reshape(nrows, total), final_im.reshape(nrows, total)...  1.2 us
    convert_element_type x1, other arithmetic, grid_rows(): expand = ((lanes_in // SUPPORT == lanes_out // TILE) & (lanes_in % SUPPOR...  1.05 us
    convert_element_type x1, other arithmetic, grid_rows(): expand_u = (n_in == lane_t % GROUP).astype(jnp.bfloat16)  0.92 us
  transfers between devices with their start and end apart: 2, of which 2 were waited for; matrix products, arithmetic and copies ran while one was open for 8% of the time, Pallas kernels for 0%

profile of v7, /device:TPU:0, one launch (start us, length us, event | category | flops | bytes accessed | tf_op | source)
XLA Modules:
  0.0 38.8 jit_solution(6112674838410094333)
XLA Ops:
  0.0 0.8 %fusion.109 = (f32[1,1,8,16,12]{3,2,4,1,0:T(8,128)S(1)}, f32[1,1,8,16,12]{3,2,4,1,0:T(8,128)S(1)}) fusion(f32[2,1,8,16,12]{3,2,4,1,0:T(8,128)} %param.6), kind=kLoop, calls=%fused_computation.158 | loop fusion | bytes 24576 | tf_op jit(solution)/shard_map/slice | solution.py:230
  1.1 0.5 %copy-done.6 = s32[1,8,16]{2,1,0:T(8,128)S(1)} copy-done((s32[1,8,16]{2,1,0:T(8,128)S(1)}, s32[1,8,16]{2,1,0:T(8,128)}, u32[]{:S(2)}) %copy-start.6) | copy-done | bytes 536
  1.9 0.7 %copy-done.4 = s32[1,8,16,12]{2,1,3,0:T(8,128)S(1)} copy-done((s32[1,8,16,12]{2,1,3,0:T(8,128)S(1)}, s32[1,8,16,12]{2,1,3,0:T(8,128)}, u32[]{:S(2)}) %copy-start.4) | copy-done | bytes 6168
  2.7 0.7 %copy-done.5 = s32[1,8,16,12]{2,1,3,0:T(8,128)S(1)} copy-done((s32[1,8,16,12]{2,1,3,0:T(8,128)S(1)}, s32[1,8,16,12]{2,1,3,0:T(8,128)}, u32[]{:S(2)}) %copy-start.5) | copy-done | bytes 6168
  3.9 0.7 %all_to_all.8 = f32[32,1,240]{2,1,0:T(1,128)} reshape(f32[16,2,4,60]{3,2,1,0:T(4,128)S(1)} %bitcast.63) | data formatting | bytes 61440 | tf_op jit(solution)/shard_map/all_to_all | solution.py:239
  4.7 7.3 %all-to-all-start = ((f32[32,1,240]{2,1,0:T(1,128)}), f32[32,1,240]{2,1,0:T(1,128)S(1)}, u32[]{:S(2)}, u32[]{:S(2)}) async-start(f32[32,1,240]{2,1,0:T(1,128)} %all_to_all.8), calls=%async_computation | async-start | bytes 65536 | tf_op jit(solution)/shard_map/all_to_all | solution.py:239
  12.0 0.7 %copy-done.1 = f32[64,128]{1,0:T(8,128)S(1)} copy-done((f32[64,128]{1,0:T(8,128)S(1)}, f32[64,128]{1,0:T(8,128)}, u32[]{:S(2)}) %copy-start.1) | copy-done | bytes 32792
  12.9 0.8 %fusion.4.eye_ref = bf16[384,384]{1,0:T(8,128)(2,1)} fusion(), kind=kLoop, calls=%fused_computation.11 | loop fusion | flops 294912 | bytes 294912 | tf_op jit(solution)/shard_map/convert_element_type | solution.py:180
  13.9 0.9 %fusion.12 = (bf16[384,128]{1,0:T(8,128)(2,1)}, bf16[384,128]{1,0:T(8,128)(2,1)}) fusion(s32[128]{0:T(128)S(1)} %get-tuple-element.27, s32[128]{0:T(128)S(1)} %get-tuple-element.28, s32[384]{0:T(512)S(1)} %get-tuple-element.24, s32[384]{0:T(512)S(1)} %get-tuple-element.25, pred[384]{0:T(512)(128)(4,1)S(1)} %fusion.76, ...), kind=kLoop, calls=%fused_computation.27 | loop fusion | flops 344064 | bytes 202368 | tf_op jit(solution)/shard_map/convert_element_type | solution.py:186
  14.8 1.0 %fusion.3.e_ref = bf16[128,2048]{1,0:T(8,128)(2,1)} fusion(s32[2048]{0:T(1024)S(1)} %get-tuple-element.30, s32[2048]{0:T(1024)S(1)} %get-tuple-element.32, s32[128]{0:T(128)S(1)} %get-tuple-element.36, s32[128]{0:T(128)S(1)} %get-tuple-element.37, s32[2048]{0:T(1024)S(1)} %get-tuple-element.31, s32[2048]{0:T(1024)S(1)} %get-tuple-element.33, ...), kind=kLoop, calls=%fused_computation.9 | loop fusion | flops 2097152 | bytes 563456 | tf_op jit(solution)/shard_map/convert_element_type | solution.py:176
  16.0 3.2 %all-to-all-done = f32[32,1,240]{2,1,0:T(1,128)S(1)} async-done(((f32[32,1,240]{2,1,0:T(1,128)}), f32[32,1,240]{2,1,0:T(1,128)S(1)}, u32[]{:S(2)}, u32[]{:S(2)}) %all-to-all-start) | async-done | bytes 30752 | tf_op jit(solution)/shard_map/all_to_all | solution.py:239
  19.8 0.6 %pad_maximum_fusion.fld_ref = bf16[4,24,384]{2,1,0:T(8,128)(2,1)} fusion(bf16[4,8,384]{2,1,0:T(8,128)(2,1)S(1)} %get-tuple-element.14, bf16[4,8,384]{2,1,0:T(8,128)(2,1)S(1)} %get-tuple-element.15, bf16[4,8,384]{2,1,0:T(8,128)(2,1)S(1)} %get-tuple-element.13), kind=kLoop, calls=%fused_computation.31 | loop fusion | flops 221184 | bytes 147456 | tf_op jit(solution)/shard_map/concatenate | solution.py:243
  20.4 10.0 %shard_map.64 = f32[2,128,512]{2,1,0:T(8,128)} custom-call(bf16[4,24,384]{2,1,0:T(8,128)(2,1)} %pad_maximum_fusion.fld_ref, bf16[384,384]{1,0:T(8,128)(2,1)} %fusion.4.eye_ref, bf16[64,768]{1,0:T(8,128)(2,1)} %copy-done.2, bf16[384,128]{1,0:T(8,128)(2,1)} %get-tuple-element.21.xv_ref, bf16[384,128]{1,0:T(8,128)(2,1)} %get-tuple-element.20.xu_ref, ...), custom_call_target="tpu_custom_call" | custom-call | tf_op jit(solution)/shard_map/pallas_call | solution.py:188
  30.5 1.0 %copy-done = f32[2,128,512]{2,1,0:T(8,128)S(1)} copy-done((f32[2,128,512]{2,1,0:T(8,128)S(1)}, f32[2,128,512]{2,1,0:T(8,128)}, u32[]{:S(2)}) %copy-start) | copy-done | bytes 524312
  31.8 1.4 %collective-permute-done = f32[2,64,512]{2,1,0:T(8,128)S(1)} collective-permute-done((f32[2,64,512]{2,1,0:T(8,128)S(1)}, f32[2,64,512]{2,1,0:T(8,128)S(1)}, u32[]{:S(2)}, u32[]{:S(2)}) %collective-permute-start) | collective-permute-done | bytes 262176 | tf_op jit(solution)/shard_map/ppermute | solution.py:257
  33.3 0.3 fusion.55
  33.6 0.3 fusion.57
  34.0 0.3 convolution_subtract_fusion.1
  34.3 0.3 add_bitcast_fusion
  34.6 0.5 %fusion.9 = f32[128,64,8]{0,1,2:T(8,128)S(1)} fusion(f32[64,8,128]{2,1,0:T(8,128)S(1)} %get-tuple-element.5), kind=kOutput, calls=%fused_computation.24 | convolution fusion | flops 50561024 | bytes 524288 | tf_op jit(solution)/shard_map/rkj,jm->rmk/dot_general | solution.py:42
  35.1 0.5 %fusion.5 = f32[128,64,8]{0,1,2:T(8,128)S(1)} fusion(f32[64,8,128]{2,1,0:T(8,128)S(1)} %get-tuple-element.6), kind=kOutput, calls=%fused_computation.20 | convolution fusion | flops 50561024 | bytes 524288 | tf_op jit(solution)/shard_map/rkj,jm->rmk/dot_general | solution.py:45
  35.7 0.5 %fusion.1 = f32[64,128,8]{1,0,2:T(8,128)S(1)} fusion(f32[128,64,8]{0,1,2:T(8,128)S(1)} %fusion.9, f32[64,8,128]{2,1,0:T(8,128)S(1)} %get-tuple-element.6), kind=kOutput, calls=%fused_computation.3 | convolution fusion | flops 50626560 | bytes 786432 | tf_op jit(solution)/shard_map/rkj,jm->rmk/dot_general | solution.py:42
  36.6 0.5 %fusion = f32[64,128,8]{1,0,2:T(8,128)S(1)} fusion(f32[128,64,8]{0,1,2:T(8,128)S(1)} %fusion.5, f32[64,8,128]{2,1,0:T(8,128)S(1)} %get-tuple-element.5), kind=kOutput, calls=%fused_computation.1 | convolution fusion | flops 50626560 | bytes 786432 | tf_op jit(solution)/shard_map/rkj,jm->rmk/dot_general | solution.py:45
  37.6 1.2 %copy.62 = f32[64,2,1024]{2,1,0:T(2,128)} copy(f32[64,2,1024]{2,0,1:T(8,128)S(1)} %maximum_multiply_fusion) | data formatting | bytes 1048576 | tf_op jit(solution)/shard_map/mul | solution.py:50
  (55 shorter events, 3.5 us)
Async XLA Ops:
  1.0 0.7 %copy-start.6 = (s32[1,8,16]{2,1,0:T(8,128)S(1)}, s32[1,8,16]{2,1,0:T(8,128)}, u32[]{:S(2)}) copy-start(s32[1,8,16]{2,1,0:T(8,128)} %param.7) | copy-start | bytes 1540
  1.0 0.8 %copy-start.3 = (s32[1,8,16,12]{2,1,3,0:T(8,128)S(1)}, s32[1,8,16,12]{2,1,3,0:T(8,128)}, u32[]{:S(2)}) copy-start(s32[1,8,16,12]{2,1,3,0:T(8,128)} %param.8) | copy-start | bytes 18436
  1.8 0.8 %copy-start.4 = (s32[1,8,16,12]{2,1,3,0:T(8,128)S(1)}, s32[1,8,16,12]{2,1,3,0:T(8,128)}, u32[]{:S(2)}) copy-start(s32[1,8,16,12]{2,1,3,0:T(8,128)} %param.9) | copy-start | bytes 18436
  2.6 0.8 %copy-start.5 = (s32[1,8,16,12]{2,1,3,0:T(8,128)S(1)}, s32[1,8,16,12]{2,1,3,0:T(8,128)}, u32[]{:S(2)}) copy-start(s32[1,8,16,12]{2,1,3,0:T(8,128)} %param.10) | copy-start | bytes 18436
  4.7 14.6 %all-to-all-start = ((f32[32,1,240]{2,1,0:T(1,128)}), f32[32,1,240]{2,1,0:T(1,128)S(1)}, u32[]{:S(2)}, u32[]{:S(2)}) async-start(f32[32,1,240]{2,1,0:T(1,128)} %all_to_all.8), calls=%async_computation | async-start | bytes 65536 | tf_op jit(solution)/shard_map/all_to_all | solution.py:239
  12.0 0.8 %copy-start.1 = (f32[64,128]{1,0:T(8,128)S(1)}, f32[64,128]{1,0:T(8,128)}, u32[]{:S(2)}) copy-start(f32[64,128]{1,0:T(8,128)} %param.11) | copy-start | bytes 98308
  16.0 3.4 %copy-start.2 = (bf16[64,768]{1,0:T(8,128)(2,1)}, bf16[64,768]{1,0:T(8,128)(2,1)S(1)}, u32[]{:S(2)}) copy-start(bf16[64,768]{1,0:T(8,128)(2,1)S(1)} %fusion.34.kt_ref) | copy-start | bytes 294916
  30.5 1.0 %copy-start = (f32[2,128,512]{2,1,0:T(8,128)S(1)}, f32[2,128,512]{2,1,0:T(8,128)}, u32[]{:S(2)}) copy-start(f32[2,128,512]{2,1,0:T(8,128)} %shard_map.64) | copy-start | bytes 1572868
  31.5 1.6 %collective-permute-start = (f32[2,64,512]{2,1,0:T(8,128)S(1)}, f32[2,64,512]{2,1,0:T(8,128)S(1)}, u32[]{:S(2)}, u32[]{:S(2)}) collective-permute-start(f32[2,64,512]{2,1,0:T(8,128)S(1)} %get-tuple-element.9), channel_id=1, source_target_pairs={{0,1},{1,0},{2,3},{3,2},{4,5},{5,4},{6,7},{7,6},{8,9},{9,8},{10,11... | collective-permute-start | bytes 786440 | tf_op jit(solution)/shard_map/ppermute | solution.py:257

commit v8 on v7

--- a/solution.py
+++ b/solution.py
@@ -21,34 +21,29 @@
     return (jnp.cos(angle), jnp.sin(angle))
 
 
-def transform(real_in, imag_in, groups):
-    nrows = real_in.shape[0]
-    total = real_in.shape[1]
+def transform(field, groups):
+    nrows = field.shape[1]
+    total = field.shape[2]
     width = total // groups
-    highest = lax.Precision.HIGH
+    precision = lax.Precision.HIGH
     cos_a, sin_a = make_table(groups, groups, groups)
     cos_t, sin_t = make_table(groups, width, total)
     cos_b, sin_b = make_table(width, width, width)
-    real_in = real_in.reshape(nrows, groups, width)
-    imag_in = imag_in.reshape(nrows, groups, width)
-    first_re = jnp.einsum("rpj,pk->rkj", real_in, cos_a, precision=highest) + jnp.einsum(
-        "rpj,pk->rkj", imag_in, sin_a, precision=highest
-    )
-    first_im = jnp.einsum("rpj,pk->rkj", imag_in, cos_a, precision=highest) - jnp.einsum(
-        "rpj,pk->rkj", real_in, sin_a, precision=highest
-    )
-    turned_re = first_re * cos_t + first_im * sin_t
-    turned_im = first_im * cos_t - first_re * sin_t
-    final_re = jnp.einsum("rkj,jm->rmk", turned_re, cos_b, precision=highest) + jnp.einsum(
-        "rkj,jm->rmk", turned_im, sin_b, precision=highest
-    )
-    final_im = jnp.einsum("rkj,jm->rmk", turned_im, cos_b, precision=highest) - jnp.einsum(
-        "rkj,jm->rmk", turned_re, sin_b, precision=highest
+    first_matrix = jnp.stack(
+        [jnp.stack([cos_a, -sin_a], axis=1), jnp.stack([sin_a, cos_a], axis=1)]
     )
     scale = 1.0 / math.sqrt(total)
-    return (
-        jnp.stack([final_re.reshape(nrows, total), final_im.reshape(nrows, total)], axis=1) * scale
-    )
+    final_matrix = jnp.stack(
+        [jnp.stack([cos_b, -sin_b], axis=1), jnp.stack([sin_b, cos_b], axis=1)]
+    ) * scale
+    first = jnp.einsum(
+        "crpj,cpdk->drkj", field.reshape(2, nrows, groups, width), first_matrix, precision=precision
+    )
+    turned = jnp.stack(
+        [first[0] * cos_t + first[1] * sin_t, first[1] * cos_t - first[0] * sin_t]
+    )
+    final = jnp.einsum("drkj,djem->remk", turned, final_matrix, precision=precision)
+    return final.reshape(nrows, 2, total)
 
 
 def weigh(vis_re, vis_im, planes, kernels):
@@ -256,7 +251,7 @@
         piece = lax.dynamic_slice_in_dim(slab, target * rows, rows, axis=1)
         piece = lax.ppermute(piece, axes, pairs)
         full = lax.dynamic_update_slice_in_dim(full, piece, source * width, axis=2)
-    return transform(full[0], full[1], dests)
+    return transform(full, dests)
 
 
 def solution(mesh):

time: 39.3 us -> 36.8 us (0.936)
  matrix products: 3.29 us -> 0.82 us
  waiting for transfers between devices: 4.61 us -> 3.32 us
  other arithmetic: 3.92 us -> 4.64 us
  local copies, waits for them, and re-layouts: 9.1 us -> 9.61 us
    dot_general x8 -> x2, matrix products: 3.29 us -> 0.82 us  [the longest x1 0.42 us: transform(): jnp.einsum('crpj,cpdk->drkj', field.reshape(2, nrows, groups, width), fir...]
    reshape x0 -> x2, local copies, waits for them, and re-layouts: none -> 1.56 us  [the longest x1 1.14 us: transform(): return final.reshape(nrows, 2, total)]
    mul x1 -> x0, local copies, waits for them, and re-layouts: 1.2 us -> none  [transform(): jnp.stack([final_re.reshape(nrows, total), final_im.reshape(nrows, total)...]
    ppermute x1, waiting for transfers between devices: 1.37 us -> 0.48 us  [shards(): piece = lax.ppermute(piece, axes, pairs)]
    dynamic_update_slice x0 -> x1, local copies, waits for them, and re-layouts: none -> 0.41 us  [shards(): full = lax.dynamic_update_slice_in_dim(full, mine, member * width, axis=2)]
    all_to_all x1, waiting for transfers between devices: 3.24 us -> 2.84 us  [shards(): got = lax.all_to_all(send, axes, split_axis=0, concat_axis=0, tiled=True)]
    unnamed x17 -> x14, local copies, waits for them, and re-layouts: 3.77 us -> 3.63 us
  transfers between devices with their start and end apart: 2 -> 2, of which waited for: 2 -> 2; matrix products, arithmetic and copies ran while one was open for 8% -> 12% of each run, Pallas kernels for 0% -> 0%
where the time goes in v8:
time: 36.8 us; the launch traced here: 36.3 us
  Pallas kernels  10.1 us (27%)
  local copies, waits for them, and re-layouts  9.61 us (26%)
  starting transfers between devices  7.5 us (20%)
  other arithmetic  4.64 us (13%)
  waiting for transfers between devices  3.32 us (9%)
  matrix products  0.82 us (2%)
    pallas_call x1, Pallas kernels, grid_rows(): pl.pallas_call(grid_kernel, grid=(dests, steps), in_specs=[pl.BlockSpec((...  10.1 us
    all_to_all x1, starting transfers between devices, shards(): got = lax.all_to_all(send, axes, split_axis=0, concat_axis=0, tiled=True)  7.3 us
    unnamed x14, local copies, waits for them, and re-layouts  3.63 us
    all_to_all x1, waiting for transfers between devices, shards(): got = lax.all_to_all(send, axes, split_axis=0, concat_axis=0, tiled=True)  2.84 us
    reshape x1, local copies, waits for them, and re-layouts, transform(): return final.reshape(nrows, 2, total)  1.14 us
    convert_element_type x1, other arithmetic, grid_rows(): expand = ((lanes_in // SUPPORT == lanes_out // TILE) & (lanes_in % SUPPOR...  1.05 us
    convert_element_type x1, other arithmetic, grid_rows(): expand_u = (n_in == lane_t % GROUP).astype(jnp.bfloat16)  0.91 us
    all_to_all x2, local copies, waits for them, and re-layouts, shards(): got = lax.all_to_all(send, axes, split_axis=0, concat_axis=0, tiled=True)  0.83 us
  transfers between devices with their start and end apart: 2, of which 2 were waited for; matrix products, arithmetic and copies ran while one was open for 12% of the time, Pallas kernels for 0%

profile of v8, /device:TPU:0, one launch (start us, length us, event | category | flops | bytes accessed | tf_op | source)
XLA Modules:
  0.0 36.3 jit_solution(1828116167190478625)
XLA Ops:
  0.0 0.8 %fusion.65 = (f32[1,1,8,16,12]{3,2,4,1,0:T(8,128)S(1)}, f32[1,1,8,16,12]{3,2,4,1,0:T(8,128)S(1)}) fusion(f32[2,1,8,16,12]{3,2,4,1,0:T(8,128)} %param.6), kind=kLoop, calls=%fused_computation.123 | loop fusion | bytes 24576 | tf_op jit(solution)/shard_map/slice | solution.py:225
  1.1 0.5 %copy-done.6 = s32[1,8,16]{2,1,0:T(8,128)S(1)} copy-done((s32[1,8,16]{2,1,0:T(8,128)S(1)}, s32[1,8,16]{2,1,0:T(8,128)}, u32[]{:S(2)}) %copy-start.6) | copy-done | bytes 536
  1.9 0.7 %copy-done.4 = s32[1,8,16,12]{2,1,3,0:T(8,128)S(1)} copy-done((s32[1,8,16,12]{2,1,3,0:T(8,128)S(1)}, s32[1,8,16,12]{2,1,3,0:T(8,128)}, u32[]{:S(2)}) %copy-start.4) | copy-done | bytes 6168
  2.7 0.7 %copy-done.5 = s32[1,8,16,12]{2,1,3,0:T(8,128)S(1)} copy-done((s32[1,8,16,12]{2,1,3,0:T(8,128)S(1)}, s32[1,8,16,12]{2,1,3,0:T(8,128)}, u32[]{:S(2)}) %copy-start.5) | copy-done | bytes 6168
  3.6 0.3 concatenate.13
  3.9 0.7 %all_to_all.8 = f32[32,1,240]{2,1,0:T(1,128)} reshape(f32[16,2,4,60]{3,2,1,0:T(4,128)S(1)} %bitcast.51) | data formatting | bytes 61440 | tf_op jit(solution)/shard_map/all_to_all | solution.py:234
  4.6 7.3 %all-to-all-start = ((f32[32,1,240]{2,1,0:T(1,128)}), f32[32,1,240]{2,1,0:T(1,128)S(1)}, u32[]{:S(2)}, u32[]{:S(2)}) async-start(f32[32,1,240]{2,1,0:T(1,128)} %all_to_all.8), calls=%async_computation | async-start | bytes 65536 | tf_op jit(solution)/shard_map/all_to_all | solution.py:234
  12.0 0.7 %copy-done.1 = f32[64,128]{1,0:T(8,128)S(1)} copy-done((f32[64,128]{1,0:T(8,128)S(1)}, f32[64,128]{1,0:T(8,128)}, u32[]{:S(2)}) %copy-start.1) | copy-done | bytes 32792
  12.9 0.8 %fusion.2.eye_ref = bf16[384,384]{1,0:T(8,128)(2,1)} fusion(), kind=kLoop, calls=%fused_computation.7 | loop fusion | flops 294912 | bytes 294912 | tf_op jit(solution)/shard_map/convert_element_type | solution.py:175
  13.8 0.3 fusion.25
  14.4 0.9 %fusion.10 = (bf16[384,128]{1,0:T(8,128)(2,1)}, bf16[384,128]{1,0:T(8,128)(2,1)}) fusion(s32[128]{0:T(128)S(1)} %get-tuple-element.29, s32[128]{0:T(128)S(1)} %get-tuple-element.30, s32[384]{0:T(512)S(1)} %get-tuple-element.26, s32[384]{0:T(512)S(1)} %get-tuple-element.27, pred[384]{0:T(512)(128)(4,1)S(1)} %fusion.60, ...), kind=kLoop, calls=%fused_computation.22 | loop fusion | flops 344064 | bytes 202368 | tf_op jit(solution)/shard_map/convert_element_type | solution.py:181
  15.3 1.0 %fusion.1.e_ref = bf16[128,2048]{1,0:T(8,128)(2,1)} fusion(s32[2048]{0:T(1024)S(1)} %get-tuple-element.32, s32[2048]{0:T(1024)S(1)} %get-tuple-element.34, s32[128]{0:T(128)S(1)} %get-tuple-element.38, s32[128]{0:T(128)S(1)} %get-tuple-element.39, s32[2048]{0:T(1024)S(1)} %get-tuple-element.33, s32[2048]{0:T(1024)S(1)} %get-tuple-element.35, ...), kind=kLoop, calls=%fused_computation.5 | loop fusion | flops 2097152 | bytes 563456 | tf_op jit(solution)/shard_map/convert_element_type | solution.py:171
  16.4 2.8 %all-to-all-done = f32[32,1,240]{2,1,0:T(1,128)S(1)} async-done(((f32[32,1,240]{2,1,0:T(1,128)}), f32[32,1,240]{2,1,0:T(1,128)S(1)}, u32[]{:S(2)}, u32[]{:S(2)}) %all-to-all-start) | async-done | bytes 30752 | tf_op jit(solution)/shard_map/all_to_all | solution.py:234
  19.8 0.6 %pad_maximum_fusion.1.fld_ref = bf16[4,24,384]{2,1,0:T(8,128)(2,1)} fusion(bf16[4,8,384]{2,1,0:T(8,128)(2,1)S(1)} %get-tuple-element.14, bf16[4,8,384]{2,1,0:T(8,128)(2,1)S(1)} %get-tuple-element.15, bf16[4,8,384]{2,1,0:T(8,128)(2,1)S(1)} %get-tuple-element.13), kind=kLoop, calls=%fused_computation.29 | loop fusion | flops 221184 | bytes 147456 | tf_op jit(solution)/shard_map/concatenate | solution.py:238
  20.4 10.1 %shard_map.64 = f32[2,128,512]{2,1,0:T(8,128)} custom-call(bf16[4,24,384]{2,1,0:T(8,128)(2,1)} %pad_maximum_fusion.1.fld_ref, bf16[384,384]{1,0:T(8,128)(2,1)} %fusion.2.eye_ref, bf16[64,768]{1,0:T(8,128)(2,1)} %copy-done.2, bf16[384,128]{1,0:T(8,128)(2,1)} %get-tuple-element.21.xv_ref, bf16[384,128]{1,0:T(8,128)(2,1)} %get-tuple-element.20.xu_ref, ...), custom_call_target="tpu_custom_call" | custom-call | tf_op jit(solution)/shard_map/pallas_call | solution.py:183
  30.5 1.0 %copy-done = f32[2,128,512]{2,1,0:T(8,128)S(1)} copy-done((f32[2,128,512]{2,1,0:T(8,128)S(1)}, f32[2,128,512]{2,1,0:T(8,128)}, u32[]{:S(2)}) %copy-start) | copy-done | bytes 524312
  31.9 0.3 fusion.23
  32.3 0.4 %copy.43 = f32[2,64,1024]{2,0,1:T(2,128)S(1)} copy(f32[2,64,1024]{2,1,0:T(8,128)S(1)} %get-tuple-element.8) | data formatting | bytes 1048576 | tf_op jit(solution)/shard_map/dynamic_update_slice | solution.py:243
  32.7 0.5 %collective-permute-done = f32[2,64,512]{2,1,0:T(8,128)S(1)} collective-permute-done((f32[2,64,512]{2,1,0:T(8,128)S(1)}, f32[2,64,512]{2,1,0:T(8,128)S(1)}, u32[]{:S(2)}, u32[]{:S(2)}) %collective-permute-start) | collective-permute-done | bytes 262176 | tf_op jit(solution)/shard_map/ppermute | solution.py:252
  33.4 0.4 %reshape.195 = f32[2,64,8,128,1]{3,2,0,1,4:T(8,128)S(1)} reshape(f32[2,64,1024]{2,0,1:T(2,128)S(1)} %copy_dynamic-update-slice_fusion) | data formatting | bytes 1048576 | tf_op jit(solution)/shard_map/reshape | solution.py:40
  33.8 0.4 %convolution_bitcast_fusion.1 = f32[2,64,8,128]{3,2,1,0:T(8,128)S(1)} fusion(f32[2,64,8,128,1]{3,2,0,1,4:T(8,128)S(1)} %reshape.195, f32[1,8,2,8]{1,3,0,2:T(8,128)S(1)} %copy.32, f32[1,8,2,8]{1,3,0,2:T(8,128)S(1)} %copy.31), kind=kOutput, calls=%fused_computation.1 | convolution fusion | flops 12583168 | bytes 1049600 | tf_op jit(solution)/shard_map/crpj,cpdk->drkj/dot_general | solution.py:39
  34.3 0.4 %convolution_bitcast_fusion = f32[64,2,128,8]{2,0,3,1:T(8,128)S(1)} fusion(f32[2,64,8,128]{3,2,1,0:T(8,128)S(1)} %pad_maximum_fusion, f32[1,128,2,128]{3,1,0,2:T(8,128)S(1)} %get-tuple-element.12, f32[1,128,2,128]{3,1,0,2:T(8,128)S(1)} %get-tuple-element.11), kind=kOutput, calls=%fused_computation | convolution fusion | flops 201457664 | bytes 1310720 | tf_op jit(solution)/shard_map/drkj,djem->remk/dot_general | solution.py:45
  34.7 0.4 %copy.46 = f32[64,2,128,8]{0,3,2,1:T(8,128)S(1)} copy(f32[64,2,128,8]{2,0,3,1:T(8,128)S(1)} %convolution_bitcast_fusion) | data formatting | bytes 1048576 | tf_op jit(solution)/shard_map/drkj,djem->remk/transpose | solution.py:45
  35.1 1.1 %copy.47 = f32[64,2,1024]{2,1,0:T(2,128)} copy(f32[64,2,1024]{0,2,1:T(8,128)S(1)} %bitcast.49) | data formatting | bytes 1048576 | tf_op jit(solution)/shard_map/reshape | solution.py:46
  (54 shorter events, 2.8 us)
Async XLA Ops:
  1.0 0.7 %copy-start.6 = (s32[1,8,16]{2,1,0:T(8,128)S(1)}, s32[1,8,16]{2,1,0:T(8,128)}, u32[]{:S(2)}) copy-start(s32[1,8,16]{2,1,0:T(8,128)} %param.7) | copy-start | bytes 1540
  1.0 0.8 %copy-start.3 = (s32[1,8,16,12]{2,1,3,0:T(8,128)S(1)}, s32[1,8,16,12]{2,1,3,0:T(8,128)}, u32[]{:S(2)}) copy-start(s32[1,8,16,12]{2,1,3,0:T(8,128)} %param.8) | copy-start | bytes 18436
  1.8 0.8 %copy-start.4 = (s32[1,8,16,12]{2,1,3,0:T(8,128)S(1)}, s32[1,8,16,12]{2,1,3,0:T(8,128)}, u32[]{:S(2)}) copy-start(s32[1,8,16,12]{2,1,3,0:T(8,128)} %param.9) | copy-start | bytes 18436
  2.6 0.8 %copy-start.5 = (s32[1,8,16,12]{2,1,3,0:T(8,128)S(1)}, s32[1,8,16,12]{2,1,3,0:T(8,128)}, u32[]{:S(2)}) copy-start(s32[1,8,16,12]{2,1,3,0:T(8,128)} %param.10) | copy-start | bytes 18436
  4.6 14.6 %all-to-all-start = ((f32[32,1,240]{2,1,0:T(1,128)}), f32[32,1,240]{2,1,0:T(1,128)S(1)}, u32[]{:S(2)}, u32[]{:S(2)}) async-start(f32[32,1,240]{2,1,0:T(1,128)} %all_to_all.8), calls=%async_computation | async-start | bytes 65536 | tf_op jit(solution)/shard_map/all_to_all | solution.py:234
  12.0 0.8 %copy-start.1 = (f32[64,128]{1,0:T(8,128)S(1)}, f32[64,128]{1,0:T(8,128)}, u32[]{:S(2)}) copy-start(f32[64,128]{1,0:T(8,128)} %param.11) | copy-start | bytes 98308
  14.4 0.9 %copy-start.2 = (bf16[64,768]{1,0:T(8,128)(2,1)}, bf16[64,768]{1,0:T(8,128)(2,1)S(1)}, u32[]{:S(2)}) copy-start(bf16[64,768]{1,0:T(8,128)(2,1)S(1)} %fusion.26.kt_ref) | copy-start | bytes 294916
  30.5 1.0 %copy-start = (f32[2,128,512]{2,1,0:T(8,128)S(1)}, f32[2,128,512]{2,1,0:T(8,128)}, u32[]{:S(2)}) copy-start(f32[2,128,512]{2,1,0:T(8,128)} %shard_map.64) | copy-start | bytes 1572868
  31.5 1.6 %collective-permute-start = (f32[2,64,512]{2,1,0:T(8,128)S(1)}, f32[2,64,512]{2,1,0:T(8,128)S(1)}, u32[]{:S(2)}, u32[]{:S(2)}) collective-permute-start(f32[2,64,512]{2,1,0:T(8,128)S(1)} %get-tuple-element.7), channel_id=1, source_target_pairs={{0,1},{1,0},{2,3},{3,2},{4,5},{5,4},{6,7},{7,6},{8,9},{9,8},{10,11... | collective-permute-start | bytes 786440 | tf_op jit(solution)/shard_map/ppermute | solution.py:252

commit v9 on v8

--- a/solution.py
+++ b/solution.py
@@ -11,7 +11,7 @@
 TILE = 128
 SUPPORT = 8
 GROUP = 16
-FIELDS = 5
+FIELDS = 6
 
 
 def make_table(first, second, length):
@@ -75,8 +75,9 @@
     return high.astype(jnp.bfloat16), middle.astype(jnp.bfloat16), low.astype(jnp.bfloat16)
 
 
-def grid_kernel(fld_ref, eye_ref, kt_ref, xv_ref, xu_ref, e_ref, out_ref, rep_ref, x_ref, r_ref, tab_ref):
+def grid_kernel(flags_ref, fld_ref, eye_ref, kt_ref, xv_ref, xu_ref, e_ref, out_ref, rep_ref, x_ref, r_ref, tab_ref):
     chunk_step = pl.program_id(1)
+    base = (pl.program_id(0) * pl.num_programs(1) + chunk_step) * (fld_ref.shape[2] // GROUP)
     chunk = fld_ref.shape[2]
     rows = out_ref.shape[1]
     ngroups = chunk // GROUP
@@ -127,8 +128,8 @@
     urow = lax.broadcasted_iota(jnp.int32, (rows, TILE), 0)
     zero = jnp.zeros((GROUP, TILE), jnp.bfloat16)
 
-    def body(g, carry):
-        start = pl.multiple_of(g * GROUP, GROUP)
+    def body(g):
+        start = g * GROUP
         blocks = [
             jnp.where(keep, rep_ref[pl.ds(start, GROUP), pl.ds(i * TILE, TILE)], zero)
             for i in range(nblocks)
@@ -139,20 +140,27 @@
         spread = lax.dot_general(
             wbd, cst, (((1,), (1,)), ((), ())), preferred_element_type=jnp.float32
         ).astype(jnp.bfloat16)
-        at = pl.multiple_of(g * depth, depth)
+        at = g * depth
         x_ref[0, pl.ds(at, depth), :] = spread[:depth]
         x_ref[1, pl.ds(at, depth), :] = spread[depth:]
         uoa = tab_ref[1, pl.ds(g, 1), :]
         r_ref[:, pl.ds(at, TILE)] = (urow == uoa).astype(jnp.bfloat16)
-        return carry
-
-    lax.fori_loop(0, ngroups, body, 0, unroll=True)
+
+    def skip(g):
+        at = g * depth
+        x_ref[:, pl.ds(at, depth), :] = jnp.zeros((2, depth, TILE), jnp.bfloat16)
+        r_ref[:, pl.ds(at, TILE)] = jnp.zeros((rows, TILE), jnp.bfloat16)
+
+    for g in range(ngroups):
+        flag = flags_ref[base + g]
+        pl.when(flag > 0)(functools.partial(body, g))
+        pl.when(flag == 0)(functools.partial(skip, g))
     pick = r_ref[...]
     out_ref[0] += jnp.dot(pick, x_ref[0], preferred_element_type=jnp.float32)
     out_ref[1] += jnp.dot(pick, x_ref[1], preferred_element_type=jnp.float32)
 
 
-def grid_rows(fld, kernels, rows):
+def grid_rows(flags, fld, kernels, rows):
     dests, nf, per_dest = fld.shape
     chunk = per_dest
     for size in (384, 192, 96, 48, 16):
@@ -179,30 +187,34 @@
     lane_t = lax.broadcasted_iota(jnp.int32, (chunk, TILE), 1)
     expand_v = (n_in == lane_t // SUPPORT).astype(jnp.bfloat16)
     expand_u = (n_in == lane_t % GROUP).astype(jnp.bfloat16)
-    whole = lambda d, c: (0, 0)
-    return pl.pallas_call(
-        grid_kernel,
+    whole = lambda d, c, flags: (0, 0)
+    grid_spec = pltpu.PrefetchScalarGridSpec(
+        num_scalar_prefetch=1,
         grid=(dests, steps),
         in_specs=[
-            pl.BlockSpec((1, nf, chunk), lambda d, c: (d, 0, c)),
+            pl.BlockSpec((1, nf, chunk), lambda d, c, flags: (d, 0, c)),
             pl.BlockSpec((chunk, chunk), whole),
             pl.BlockSpec(table.shape, whole),
             pl.BlockSpec((chunk, TILE), whole),
             pl.BlockSpec((chunk, TILE), whole),
             pl.BlockSpec((width, nblocks * TILE), whole),
         ],
-        out_specs=pl.BlockSpec((2, rows, TILE), lambda d, c: (0, 0, d)),
-        out_shape=jax.ShapeDtypeStruct((2, rows, dests * TILE), jnp.float32),
+        out_specs=pl.BlockSpec((2, rows, TILE), lambda d, c, flags: (0, 0, d)),
         scratch_shapes=[
             pltpu.VMEM((chunk, nblocks * TILE), jnp.bfloat16),
             pltpu.VMEM((2, chunk * SUPPORT, TILE), jnp.bfloat16),
             pltpu.VMEM((rows, chunk * SUPPORT), jnp.bfloat16),
             pltpu.VMEM((2, ngroups, TILE), jnp.int32),
         ],
+    )
+    return pl.pallas_call(
+        grid_kernel,
+        grid_spec=grid_spec,
+        out_shape=jax.ShapeDtypeStruct((2, rows, dests * TILE), jnp.float32),
         compiler_params=pltpu.CompilerParams(
             dimension_semantics=("arbitrary", "arbitrary")
         ),
-    )(fld, eye, table, expand_v, expand_u, expand)
+    )(flags, fld, eye, table, expand_v, expand_u, expand)
 
 
 def shards(visibilities, tile_counts, w_plane, u_offset, v_offset, kernels):
@@ -226,17 +238,20 @@
             w_plane[0].astype(jnp.float32),
             u_offset[0].astype(jnp.float32),
             v_offset[0].astype(jnp.float32),
+            live,
         ],
         axis=-1,
     )
     send = fields.reshape(per_tile, own_dests, ntiles, FIELDS * slots).transpose(2, 0, 1, 3)
     send = send.reshape(ndev, own_dests * FIELDS * slots)
     got = lax.all_to_all(send, axes, split_axis=0, concat_axis=0, tiled=True)
-    got = got.reshape(ndev, own_dests, FIELDS, slots).transpose(1, 2, 0, 3)
+    got = got.reshape(ndev, own_dests, FIELDS, slots).transpose(1, 2, 3, 0)
     got = got.reshape(own_dests, FIELDS, ndev * slots)
+    flags = jnp.max(got[:, FIELDS - 1].reshape(own_dests, -1, GROUP), axis=2) > 0
+    flags = flags.astype(jnp.int32).reshape(-1)
     got = jnp.pad(got, ((0, 0), (0, 8 - FIELDS), (0, 0)))
     got = jnp.concatenate(split3(got), axis=1)
-    slab = grid_rows(got, kernels, TILE)
+    slab = grid_rows(flags, got, kernels, TILE)
     width = own_dests * TILE
     mine = lax.dynamic_slice_in_dim(slab, member * rows, rows, axis=1)
     full = jnp.zeros((2, rows, dests * TILE), jnp.float32)

time: 36.8 us -> 48.2 us (1.31)
  the two profiles are of different devices: /device:TPU:0 before, /device:TPU:9 now
where the time goes in v9:
time: 48.2 us; the launch traced here: 47.3 us
  Pallas kernels  22.2 us (46%)
  local copies, waits for them, and re-layouts  10.7 us (22%)
  starting transfers between devices  6.91 us (14%)
  other arithmetic  4.83 us (10%)
  waiting for transfers between devices  1.42 us (3%)
  matrix products  0.82 us (2%)
    pallas_call x1, Pallas kernels, grid_rows(): pl.pallas_call(grid_kernel, grid_spec=grid_spec, out_shape=jax.ShapeDtype...  22.2 us
    all_to_all x1, starting transfers between devices, shards(): got = lax.all_to_all(send, axes, split_axis=0, concat_axis=0, tiled=True)  6.36 us
    unnamed x15, local copies, waits for them, and re-layouts  4.2 us
    all_to_all x1, waiting for transfers between devices, shards(): got = lax.all_to_all(send, axes, split_axis=0, concat_axis=0, tiled=True)  1.18 us
    reshape x1, local copies, waits for them, and re-layouts, transform(): return final.reshape(nrows, 2, total)  1.14 us
    convert_element_type x1, other arithmetic, grid_rows(): expand = ((lanes_in // SUPPORT == lanes_out // TILE) & (lanes_in % SUPPOR...  1.05 us
  transfers between devices with their start and end apart: 2, of which 2 were waited for; matrix products, arithmetic and copies ran while one was open for 9% of the time, Pallas kernels for 0%

profile of v9, /device:TPU:9, one launch (start us, length us, event | category | flops | bytes accessed | tf_op | source)
XLA Modules:
  0.0 47.3 jit_solution(13835521815572455188)
XLA Ops:
  0.0 0.8 %fusion.66 = (f32[1,1,8,16,12]{3,2,4,1,0:T(8,128)S(1)}, f32[1,1,8,16,12]{3,2,4,1,0:T(8,128)S(1)}) fusion(f32[2,1,8,16,12]{3,2,4,1,0:T(8,128)} %param.6), kind=kLoop, calls=%fused_computation.125 | loop fusion | bytes 24576 | tf_op jit(solution)/shard_map/slice | solution.py:237
  1.1 0.5 %copy-done.6 = s32[1,8,16]{2,1,0:T(8,128)S(1)} copy-done((s32[1,8,16]{2,1,0:T(8,128)S(1)}, s32[1,8,16]{2,1,0:T(8,128)}, u32[]{:S(2)}) %copy-start.6) | copy-done | bytes 536
  1.9 0.6 %copy-done.3 = s32[1,8,16,12]{2,1,3,0:T(8,128)S(1)} copy-done((s32[1,8,16,12]{2,1,3,0:T(8,128)S(1)}, s32[1,8,16,12]{2,1,3,0:T(8,128)}, u32[]{:S(2)}) %copy-start.3) | copy-done | bytes 6168
  2.6 0.7 %copy-done.4 = s32[1,8,16,12]{2,1,3,0:T(8,128)S(1)} copy-done((s32[1,8,16,12]{2,1,3,0:T(8,128)S(1)}, s32[1,8,16,12]{2,1,3,0:T(8,128)}, u32[]{:S(2)}) %copy-start.4) | copy-done | bytes 6168
  3.4 0.7 %copy-done.5 = s32[1,8,16,12]{2,1,3,0:T(8,128)S(1)} copy-done((s32[1,8,16,12]{2,1,3,0:T(8,128)S(1)}, s32[1,8,16,12]{2,1,3,0:T(8,128)}, u32[]{:S(2)}) %copy-start.5) | copy-done | bytes 6168
  4.3 0.3 concatenate.13
  4.6 0.8 %all_to_all.8 = f32[32,1,288]{2,1,0:T(1,128)} reshape(f32[16,2,4,72]{3,2,1,0:T(4,128)S(1)} %bitcast.51) | data formatting | bytes 73728 | tf_op jit(solution)/shard_map/all_to_all | solution.py:247
  5.4 6.4 %all-to-all-start = ((f32[32,1,288]{2,1,0:T(1,128)}), f32[32,1,288]{2,1,0:T(1,128)S(1)}, u32[]{:S(2)}, u32[]{:S(2)}) async-start(f32[32,1,288]{2,1,0:T(1,128)} %all_to_all.8), calls=%async_computation | async-start | bytes 98304 | tf_op jit(solution)/shard_map/all_to_all | solution.py:247
  11.8 0.7 %copy-done.1 = f32[64,128]{1,0:T(8,128)S(1)} copy-done((f32[64,128]{1,0:T(8,128)S(1)}, f32[64,128]{1,0:T(8,128)}, u32[]{:S(2)}) %copy-start.1) | copy-done | bytes 32792
  12.7 0.7 %fusion.2.eye_ref = bf16[384,384]{1,0:T(8,128)(2,1)} fusion(), kind=kLoop, calls=%fused_computation.7 | loop fusion | flops 294912 | bytes 294912 | tf_op jit(solution)/shard_map/convert_element_type | solution.py:183
  14.2 0.9 %fusion.10 = (bf16[384,128]{1,0:T(8,128)(2,1)}, bf16[384,128]{1,0:T(8,128)(2,1)}) fusion(s32[128]{0:T(128)S(1)} %get-tuple-element.29, s32[128]{0:T(128)S(1)} %get-tuple-element.30, s32[384]{0:T(512)S(1)} %get-tuple-element.26, s32[384]{0:T(512)S(1)} %get-tuple-element.27, pred[384]{0:T(512)(128)(4,1)S(1)} %fusion.61, ...), kind=kLoop, calls=%fused_computation.22 | loop fusion | flops 344064 | bytes 202368 | tf_op jit(solution)/shard_map/convert_element_type | solution.py:189
  15.1 1.0 %fusion.1.e_ref = bf16[128,2048]{1,0:T(8,128)(2,1)} fusion(s32[2048]{0:T(1024)S(1)} %get-tuple-element.32, s32[2048]{0:T(1024)S(1)} %get-tuple-element.34, s32[128]{0:T(128)S(1)} %get-tuple-element.38, s32[128]{0:T(128)S(1)} %get-tuple-element.39, s32[2048]{0:T(1024)S(1)} %get-tuple-element.33, s32[2048]{0:T(1024)S(1)} %get-tuple-element.35, ...), kind=kLoop, calls=%fused_computation.5 | loop fusion | flops 2097152 | bytes 563456 | tf_op jit(solution)/shard_map/convert_element_type | solution.py:179
  16.2 1.2 %all-to-all-done = f32[32,1,288]{2,1,0:T(1,128)S(1)} async-done(((f32[32,1,288]{2,1,0:T(1,128)}), f32[32,1,288]{2,1,0:T(1,128)S(1)}, u32[]{:S(2)}, u32[]{:S(2)}) %all-to-all-start) | async-done | bytes 36896 | tf_op jit(solution)/shard_map/all_to_all | solution.py:247
  17.8 0.7 %reshape.204.flags_ref = s32[96]{0:T(128)} reshape(s32[4,24]{1,0:T(4,128)S(1)} %compare_convert_fusion) | data formatting | bytes 768 | tf_op jit(solution)/shard_map/convert_element_type | solution.py:251
  18.5 0.6 %pad_maximum_fusion.1.fld_ref = bf16[4,24,384]{2,1,0:T(8,128)(2,1)} fusion(bf16[4,8,384]{2,1,0:T(8,128)(2,1)S(1)} %get-tuple-element.14, bf16[4,8,384]{2,1,0:T(8,128)(2,1)S(1)} %get-tuple-element.15, bf16[4,8,384]{2,1,0:T(8,128)(2,1)S(1)} %get-tuple-element.13), kind=kLoop, calls=%fused_computation.29 | loop fusion | flops 221184 | bytes 147456 | tf_op jit(solution)/shard_map/concatenate | solution.py:253
  19.2 22.2 %shard_map.64 = f32[2,128,512]{2,1,0:T(8,128)} custom-call(s32[96]{0:T(128)} %reshape.204.flags_ref, bf16[4,24,384]{2,1,0:T(8,128)(2,1)} %pad_maximum_fusion.1.fld_ref, bf16[384,384]{1,0:T(8,128)(2,1)} %fusion.2.eye_ref, bf16[64,768]{1,0:T(8,128)(2,1)} %copy-done.2, bf16[384,128]{1,0:T(8,128)(2,1)} %get-tuple-element.21.xv_ref, ...), custom_call_target="tpu_custom_call" | custom-call | tf_op jit(solution)/shard_map/pallas_call | solution.py:210
  41.4 1.0 %copy-done = f32[2,128,512]{2,1,0:T(8,128)S(1)} copy-done((f32[2,128,512]{2,1,0:T(8,128)S(1)}, f32[2,128,512]{2,1,0:T(8,128)}, u32[]{:S(2)}) %copy-start) | copy-done | bytes 524312
  42.4 0.6 %collective-permute-start = (f32[2,64,512]{2,1,0:T(8,128)S(1)}, f32[2,64,512]{2,1,0:T(8,128)S(1)}, u32[]{:S(2)}, u32[]{:S(2)}) collective-permute-start(f32[2,64,512]{2,1,0:T(8,128)S(1)} %get-tuple-element.7), channel_id=1, source_target_pairs={{0,1},{1,0},{2,3},{3,2},{4,5},{5,4},{6,7},{7,6},{8,9},{9,8},{10,11... | collective-permute-start | bytes 786440 | tf_op jit(solution)/shard_map/ppermute | solution.py:267
  43.5 0.4 copy.43
  44.4 0.4 reshape.206
  44.8 0.4 convolution_bitcast_fusion.1
  45.3 0.4 convolution_bitcast_fusion
  45.8 0.4 copy.46
  46.1 1.1 %copy.47 = f32[64,2,1024]{2,1,0:T(2,128)} copy(f32[64,2,1024]{0,2,1:T(8,128)S(1)} %bitcast.49) | data formatting | bytes 1048576 | tf_op jit(solution)/shard_map/reshape | solution.py:46
  (60 shorter events, 3.3 us)
Async XLA Ops:
  1.0 0.7 %copy-start.6 = (s32[1,8,16]{2,1,0:T(8,128)S(1)}, s32[1,8,16]{2,1,0:T(8,128)}, u32[]{:S(2)}) copy-start(s32[1,8,16]{2,1,0:T(8,128)} %param.7) | copy-start | bytes 1540
  1.7 0.8 %copy-start.3 = (s32[1,8,16,12]{2,1,3,0:T(8,128)S(1)}, s32[1,8,16,12]{2,1,3,0:T(8,128)}, u32[]{:S(2)}) copy-start(s32[1,8,16,12]{2,1,3,0:T(8,128)} %param.8) | copy-start | bytes 18436
  2.5 0.8 %copy-start.4 = (s32[1,8,16,12]{2,1,3,0:T(8,128)S(1)}, s32[1,8,16,12]{2,1,3,0:T(8,128)}, u32[]{:S(2)}) copy-start(s32[1,8,16,12]{2,1,3,0:T(8,128)} %param.9) | copy-start | bytes 18436
  3.3 0.8 %copy-start.5 = (s32[1,8,16,12]{2,1,3,0:T(8,128)S(1)}, s32[1,8,16,12]{2,1,3,0:T(8,128)}, u32[]{:S(2)}) copy-start(s32[1,8,16,12]{2,1,3,0:T(8,128)} %param.10) | copy-start | bytes 18436
  5.4 11.9 %all-to-all-start = ((f32[32,1,288]{2,1,0:T(1,128)}), f32[32,1,288]{2,1,0:T(1,128)S(1)}, u32[]{:S(2)}, u32[]{:S(2)}) async-start(f32[32,1,288]{2,1,0:T(1,128)} %all_to_all.8), calls=%async_computation | async-start | bytes 98304 | tf_op jit(solution)/shard_map/all_to_all | solution.py:247
  11.8 0.8 %copy-start.1 = (f32[64,128]{1,0:T(8,128)S(1)}, f32[64,128]{1,0:T(8,128)}, u32[]{:S(2)}) copy-start(f32[64,128]{1,0:T(8,128)} %param.11) | copy-start | bytes 98308
  14.2 0.9 %copy-start.2 = (bf16[64,768]{1,0:T(8,128)(2,1)}, bf16[64,768]{1,0:T(8,128)(2,1)S(1)}, u32[]{:S(2)}) copy-start(bf16[64,768]{1,0:T(8,128)(2,1)S(1)} %fusion.27.kt_ref) | copy-start | bytes 294916
  41.4 1.0 %copy-start = (f32[2,128,512]{2,1,0:T(8,128)S(1)}, f32[2,128,512]{2,1,0:T(8,128)}, u32[]{:S(2)}) copy-start(f32[2,128,512]{2,1,0:T(8,128)} %shard_map.64) | copy-start | bytes 1572868
  42.4 1.7 %collective-permute-start = (f32[2,64,512]{2,1,0:T(8,128)S(1)}, f32[2,64,512]{2,1,0:T(8,128)S(1)}, u32[]{:S(2)}, u32[]{:S(2)}) collective-permute-start(f32[2,64,512]{2,1,0:T(8,128)S(1)} %get-tuple-element.7), channel_id=1, source_target_pairs={{0,1},{1,0},{2,3},{3,2},{4,5},{5,4},{6,7},{7,6},{8,9},{9,8},{10,11... | collective-permute-start | bytes 786440 | tf_op jit(solution)/shard_map/ppermute | solution.py:267

commit v10 on v8

--- a/solution.py
+++ b/solution.py
@@ -117,23 +117,28 @@
     tab_ref[0] = jnp.dot(vo_rows, xv_ref[...], preferred_element_type=jnp.float32).astype(jnp.int32) + tlane % SUPPORT
     tab_ref[1] = jnp.dot(uo_rows, xu_ref[...], preferred_element_type=jnp.float32).astype(jnp.int32) + tlane // GROUP
 
-    rep_ref[...] = jnp.dot(
-        weighted, e_ref[...], preferred_element_type=jnp.float32
-    ).astype(jnp.bfloat16)
+    rep_ref[...] = weighted.astype(jnp.float32)
     lane = lax.broadcasted_iota(jnp.int32, (GROUP, TILE), 1)
     row = lax.broadcasted_iota(jnp.int32, (GROUP, TILE), 0)
     keep = (lane // SUPPORT) == row
     vrow = lax.broadcasted_iota(jnp.int32, (TILE, TILE), 0)
     urow = lax.broadcasted_iota(jnp.int32, (rows, TILE), 0)
-    zero = jnp.zeros((GROUP, TILE), jnp.bfloat16)
+    zero = jnp.zeros((GROUP, TILE), jnp.float32)
 
     def body(g, carry):
         start = pl.multiple_of(g * GROUP, GROUP)
-        blocks = [
-            jnp.where(keep, rep_ref[pl.ds(start, GROUP), pl.ds(i * TILE, TILE)], zero)
-            for i in range(nblocks)
-        ]
-        wbd = jnp.concatenate(blocks, axis=0)
+        halves = [rep_ref[pl.ds(start + h * 8, 8), :] for h in range(GROUP // 8)]
+        pre = [pltpu.roll(v, TILE // 2, 1) for v in halves]
+        blocks = []
+        for i in range(nblocks):
+            for h in range(GROUP // 8):
+                shift = (h * 8 * SUPPORT - i * SUPPORT) % TILE
+                if shift + 7 * SUPPORT < TILE:
+                    moved = pltpu.roll(halves[h], shift, 1, stride=SUPPORT, stride_axis=0)
+                else:
+                    moved = pltpu.roll(pre[h], shift - TILE // 2, 1, stride=SUPPORT, stride_axis=0)
+                blocks.append(jnp.where(keep[h * 8:(h + 1) * 8], moved, zero[:8]))
+        wbd = jnp.concatenate(blocks, axis=0).astype(jnp.bfloat16)
         vob = tab_ref[0, pl.ds(g, 1), :]
         cst = (vrow == vob).astype(jnp.bfloat16)
         spread = lax.dot_general(
@@ -194,7 +199,7 @@
         out_specs=pl.BlockSpec((2, rows, TILE), lambda d, c: (0, 0, d)),
         out_shape=jax.ShapeDtypeStruct((2, rows, dests * TILE), jnp.float32),
         scratch_shapes=[
-            pltpu.VMEM((chunk, nblocks * TILE), jnp.bfloat16),
+            pltpu.VMEM((chunk, width), jnp.float32),
             pltpu.VMEM((2, chunk * SUPPORT, TILE), jnp.bfloat16),
             pltpu.VMEM((rows, chunk * SUPPORT), jnp.bfloat16),
             pltpu.VMEM((2, ngroups, TILE), jnp.int32),

time: 36.8 us -> 36.4 us (0.989)
  Pallas kernels: 10.1 us -> 9.7 us
where the time goes in v10:
time: 36.4 us; the launch traced here: 35.9 us
  Pallas kernels  9.7 us (27%)
  local copies, waits for them, and re-layouts  9.61 us (26%)
  starting transfers between devices  7.49 us (21%)
  other arithmetic  4.64 us (13%)
  waiting for transfers between devices  3.33 us (9%)
  matrix products  0.82 us (2%)
    pallas_call x1, Pallas kernels, grid_rows(): pl.pallas_call(grid_kernel, grid=(dests, steps), in_specs=[pl.BlockSpec((...  9.7 us
    all_to_all x1, starting transfers between devices, shards(): got = lax.all_to_all(send, axes, split_axis=0, concat_axis=0, tiled=True)  7.3 us
    unnamed x14, local copies, waits for them, and re-layouts  3.63 us
    all_to_all x1, waiting for transfers between devices, shards(): got = lax.all_to_all(send, axes, split_axis=0, concat_axis=0, tiled=True)  2.84 us
    reshape x1, local copies, waits for them, and re-layouts, transform(): return final.reshape(nrows, 2, total)  1.14 us
    convert_element_type x1, other arithmetic, grid_rows(): expand = ((lanes_in // SUPPORT == lanes_out // TILE) & (lanes_in % SUPPOR...  1.05 us
    convert_element_type x1, other arithmetic, grid_rows(): expand_u = (n_in == lane_t % GROUP).astype(jnp.bfloat16)  0.91 us
    all_to_all x2, local copies, waits for them, and re-layouts, shards(): got = lax.all_to_all(send, axes, split_axis=0, concat_axis=0, tiled=True)  0.83 us
  transfers between devices with their start and end apart: 2, of which 2 were waited for; matrix products, arithmetic and copies ran while one was open for 12% of the time, Pallas kernels for 0%

profile of v10, /device:TPU:0, one launch (start us, length us, event | category | flops | bytes accessed | tf_op | source)
XLA Modules:
  0.0 35.9 jit_solution(572338104526139301)
XLA Ops:
  0.0 0.8 %fusion.65 = (f32[1,1,8,16,12]{3,2,4,1,0:T(8,128)S(1)}, f32[1,1,8,16,12]{3,2,4,1,0:T(8,128)S(1)}) fusion(f32[2,1,8,16,12]{3,2,4,1,0:T(8,128)} %param.6), kind=kLoop, calls=%fused_computation.123 | loop fusion | bytes 24576 | tf_op jit(solution)/shard_map/slice | solution.py:230
  1.1 0.5 %copy-done.6 = s32[1,8,16]{2,1,0:T(8,128)S(1)} copy-done((s32[1,8,16]{2,1,0:T(8,128)S(1)}, s32[1,8,16]{2,1,0:T(8,128)}, u32[]{:S(2)}) %copy-start.6) | copy-done | bytes 536
  1.9 0.7 %copy-done.4 = s32[1,8,16,12]{2,1,3,0:T(8,128)S(1)} copy-done((s32[1,8,16,12]{2,1,3,0:T(8,128)S(1)}, s32[1,8,16,12]{2,1,3,0:T(8,128)}, u32[]{:S(2)}) %copy-start.4) | copy-done | bytes 6168
  2.7 0.7 %copy-done.5 = s32[1,8,16,12]{2,1,3,0:T(8,128)S(1)} copy-done((s32[1,8,16,12]{2,1,3,0:T(8,128)S(1)}, s32[1,8,16,12]{2,1,3,0:T(8,128)}, u32[]{:S(2)}) %copy-start.5) | copy-done | bytes 6168
  3.6 0.3 concatenate.13
  3.9 0.7 %all_to_all.8 = f32[32,1,240]{2,1,0:T(1,128)} reshape(f32[16,2,4,60]{3,2,1,0:T(4,128)S(1)} %bitcast.51) | data formatting | bytes 61440 | tf_op jit(solution)/shard_map/all_to_all | solution.py:239
  4.6 7.3 %all-to-all-start = ((f32[32,1,240]{2,1,0:T(1,128)}), f32[32,1,240]{2,1,0:T(1,128)S(1)}, u32[]{:S(2)}, u32[]{:S(2)}) async-start(f32[32,1,240]{2,1,0:T(1,128)} %all_to_all.8), calls=%async_computation | async-start | bytes 65536 | tf_op jit(solution)/shard_map/all_to_all | solution.py:239
  12.0 0.7 %copy-done.1 = f32[64,128]{1,0:T(8,128)S(1)} copy-done((f32[64,128]{1,0:T(8,128)S(1)}, f32[64,128]{1,0:T(8,128)}, u32[]{:S(2)}) %copy-start.1) | copy-done | bytes 32792
  12.9 0.8 %fusion.2.eye_ref = bf16[384,384]{1,0:T(8,128)(2,1)} fusion(), kind=kLoop, calls=%fused_computation.7 | loop fusion | flops 294912 | bytes 294912 | tf_op jit(solution)/shard_map/convert_element_type | solution.py:180
  13.8 0.3 fusion.25
  14.4 0.9 %fusion.10 = (bf16[384,128]{1,0:T(8,128)(2,1)}, bf16[384,128]{1,0:T(8,128)(2,1)}) fusion(s32[128]{0:T(128)S(1)} %get-tuple-element.29, s32[128]{0:T(128)S(1)} %get-tuple-element.30, s32[384]{0:T(512)S(1)} %get-tuple-element.26, s32[384]{0:T(512)S(1)} %get-tuple-element.27, pred[384]{0:T(512)(128)(4,1)S(1)} %fusion.60, ...), kind=kLoop, calls=%fused_computation.22 | loop fusion | flops 344064 | bytes 202368 | tf_op jit(solution)/shard_map/convert_element_type | solution.py:186
  15.3 1.0 %fusion.1.e_ref = bf16[128,2048]{1,0:T(8,128)(2,1)} fusion(s32[2048]{0:T(1024)S(1)} %get-tuple-element.32, s32[2048]{0:T(1024)S(1)} %get-tuple-element.34, s32[128]{0:T(128)S(1)} %get-tuple-element.38, s32[128]{0:T(128)S(1)} %get-tuple-element.39, s32[2048]{0:T(1024)S(1)} %get-tuple-element.33, s32[2048]{0:T(1024)S(1)} %get-tuple-element.35, ...), kind=kLoop, calls=%fused_computation.5 | loop fusion | flops 2097152 | bytes 563456 | tf_op jit(solution)/shard_map/convert_element_type | solution.py:176
  16.4 2.8 %all-to-all-done = f32[32,1,240]{2,1,0:T(1,128)S(1)} async-done(((f32[32,1,240]{2,1,0:T(1,128)}), f32[32,1,240]{2,1,0:T(1,128)S(1)}, u32[]{:S(2)}, u32[]{:S(2)}) %all-to-all-start) | async-done | bytes 30752 | tf_op jit(solution)/shard_map/all_to_all | solution.py:239
  19.8 0.6 %pad_maximum_fusion.1.fld_ref = bf16[4,24,384]{2,1,0:T(8,128)(2,1)} fusion(bf16[4,8,384]{2,1,0:T(8,128)(2,1)S(1)} %get-tuple-element.14, bf16[4,8,384]{2,1,0:T(8,128)(2,1)S(1)} %get-tuple-element.15, bf16[4,8,384]{2,1,0:T(8,128)(2,1)S(1)} %get-tuple-element.13), kind=kLoop, calls=%fused_computation.29 | loop fusion | flops 221184 | bytes 147456 | tf_op jit(solution)/shard_map/concatenate | solution.py:243
  20.4 9.7 %shard_map.64 = f32[2,128,512]{2,1,0:T(8,128)} custom-call(bf16[4,24,384]{2,1,0:T(8,128)(2,1)} %pad_maximum_fusion.1.fld_ref, bf16[384,384]{1,0:T(8,128)(2,1)} %fusion.2.eye_ref, bf16[64,768]{1,0:T(8,128)(2,1)} %copy-done.2, bf16[384,128]{1,0:T(8,128)(2,1)} %get-tuple-element.21.xv_ref, bf16[384,128]{1,0:T(8,128)(2,1)} %get-tuple-element.20.xu_ref, ...), custom_call_target="tpu_custom_call" | custom-call | tf_op jit(solution)/shard_map/pallas_call | solution.py:188
  30.1 1.0 %copy-done = f32[2,128,512]{2,1,0:T(8,128)S(1)} copy-done((f32[2,128,512]{2,1,0:T(8,128)S(1)}, f32[2,128,512]{2,1,0:T(8,128)}, u32[]{:S(2)}) %copy-start) | copy-done | bytes 524312
  31.6 0.3 fusion.23
  31.9 0.4 %copy.43 = f32[2,64,1024]{2,0,1:T(2,128)S(1)} copy(f32[2,64,1024]{2,1,0:T(8,128)S(1)} %get-tuple-element.8) | data formatting | bytes 1048576 | tf_op jit(solution)/shard_map/dynamic_update_slice | solution.py:248
  32.3 0.5 %collective-permute-done = f32[2,64,512]{2,1,0:T(8,128)S(1)} collective-permute-done((f32[2,64,512]{2,1,0:T(8,128)S(1)}, f32[2,64,512]{2,1,0:T(8,128)S(1)}, u32[]{:S(2)}, u32[]{:S(2)}) %collective-permute-start) | collective-permute-done | bytes 262176 | tf_op jit(solution)/shard_map/ppermute | solution.py:257
  33.0 0.4 %reshape.195 = f32[2,64,8,128,1]{3,2,0,1,4:T(8,128)S(1)} reshape(f32[2,64,1024]{2,0,1:T(2,128)S(1)} %copy_dynamic-update-slice_fusion) | data formatting | bytes 1048576 | tf_op jit(solution)/shard_map/reshape | solution.py:40
  33.4 0.4 %convolution_bitcast_fusion.1 = f32[2,64,8,128]{3,2,1,0:T(8,128)S(1)} fusion(f32[2,64,8,128,1]{3,2,0,1,4:T(8,128)S(1)} %reshape.195, f32[1,8,2,8]{1,3,0,2:T(8,128)S(1)} %copy.32, f32[1,8,2,8]{1,3,0,2:T(8,128)S(1)} %copy.31), kind=kOutput, calls=%fused_computation.1 | convolution fusion | flops 12583168 | bytes 1049600 | tf_op jit(solution)/shard_map/crpj,cpdk->drkj/dot_general | solution.py:39
  34.0 0.4 %convolution_bitcast_fusion = f32[64,2,128,8]{2,0,3,1:T(8,128)S(1)} fusion(f32[2,64,8,128]{3,2,1,0:T(8,128)S(1)} %pad_maximum_fusion, f32[1,128,2,128]{3,1,0,2:T(8,128)S(1)} %get-tuple-element.12, f32[1,128,2,128]{3,1,0,2:T(8,128)S(1)} %get-tuple-element.11), kind=kOutput, calls=%fused_computation | convolution fusion | flops 201457664 | bytes 1310720 | tf_op jit(solution)/shard_map/drkj,djem->remk/dot_general | solution.py:45
  34.4 0.4 %copy.46 = f32[64,2,128,8]{0,3,2,1:T(8,128)S(1)} copy(f32[64,2,128,8]{2,0,3,1:T(8,128)S(1)} %convolution_bitcast_fusion) | data formatting | bytes 1048576 | tf_op jit(solution)/shard_map/drkj,djem->remk/transpose | solution.py:45
  34.8 1.1 %copy.47 = f32[64,2,1024]{2,1,0:T(2,128)} copy(f32[64,2,1024]{0,2,1:T(8,128)S(1)} %bitcast.49) | data formatting | bytes 1048576 | tf_op jit(solution)/shard_map/reshape | solution.py:46
  (54 shorter events, 2.8 us)
Async XLA Ops:
  1.0 0.7 %copy-start.6 = (s32[1,8,16]{2,1,0:T(8,128)S(1)}, s32[1,8,16]{2,1,0:T(8,128)}, u32[]{:S(2)}) copy-start(s32[1,8,16]{2,1,0:T(8,128)} %param.7) | copy-start | bytes 1540
  1.0 0.8 %copy-start.3 = (s32[1,8,16,12]{2,1,3,0:T(8,128)S(1)}, s32[1,8,16,12]{2,1,3,0:T(8,128)}, u32[]{:S(2)}) copy-start(s32[1,8,16,12]{2,1,3,0:T(8,128)} %param.8) | copy-start | bytes 18436
  1.8 0.8 %copy-start.4 = (s32[1,8,16,12]{2,1,3,0:T(8,128)S(1)}, s32[1,8,16,12]{2,1,3,0:T(8,128)}, u32[]{:S(2)}) copy-start(s32[1,8,16,12]{2,1,3,0:T(8,128)} %param.9) | copy-start | bytes 18436
  2.6 0.8 %copy-start.5 = (s32[1,8,16,12]{2,1,3,0:T(8,128)S(1)}, s32[1,8,16,12]{2,1,3,0:T(8,128)}, u32[]{:S(2)}) copy-start(s32[1,8,16,12]{2,1,3,0:T(8,128)} %param.10) | copy-start | bytes 18436
  4.6 14.6 %all-to-all-start = ((f32[32,1,240]{2,1,0:T(1,128)}), f32[32,1,240]{2,1,0:T(1,128)S(1)}, u32[]{:S(2)}, u32[]{:S(2)}) async-start(f32[32,1,240]{2,1,0:T(1,128)} %all_to_all.8), calls=%async_computation | async-start | bytes 65536 | tf_op jit(solution)/shard_map/all_to_all | solution.py:239
  12.0 0.8 %copy-start.1 = (f32[64,128]{1,0:T(8,128)S(1)}, f32[64,128]{1,0:T(8,128)}, u32[]{:S(2)}) copy-start(f32[64,128]{1,0:T(8,128)} %param.11) | copy-start | bytes 98308
  14.4 0.9 %copy-start.2 = (bf16[64,768]{1,0:T(8,128)(2,1)}, bf16[64,768]{1,0:T(8,128)(2,1)S(1)}, u32[]{:S(2)}) copy-start(bf16[64,768]{1,0:T(8,128)(2,1)S(1)} %fusion.26.kt_ref) | copy-start | bytes 294916
  30.1 1.0 %copy-start = (f32[2,128,512]{2,1,0:T(8,128)S(1)}, f32[2,128,512]{2,1,0:T(8,128)}, u32[]{:S(2)}) copy-start(f32[2,128,512]{2,1,0:T(8,128)} %shard_map.64) | copy-start | bytes 1572868
  31.2 1.6 %collective-permute-start = (f32[2,64,512]{2,1,0:T(8,128)S(1)}, f32[2,64,512]{2,1,0:T(8,128)S(1)}, u32[]{:S(2)}, u32[]{:S(2)}) collective-permute-start(f32[2,64,512]{2,1,0:T(8,128)S(1)} %get-tuple-element.7), channel_id=1, source_target_pairs={{0,1},{1,0},{2,3},{3,2},{4,5},{5,4},{6,7},{7,6},{8,9},{9,8},{10,11... | collective-permute-start | bytes 786440 | tf_op jit(solution)/shard_map/ppermute | solution.py:257

commit v11 on v10

--- a/solution.py
+++ b/solution.py
@@ -46,27 +46,6 @@
     return final.reshape(nrows, 2, total)
 
 
-def weigh(vis_re, vis_im, planes, kernels):
-    nplanes = kernels.shape[0]
-    width = kernels.shape[1]
-    half = width // 2
-    onehot = (
-        planes[..., None] == lax.broadcasted_iota(jnp.int32, planes.shape + (nplanes,), planes.ndim)
-    ).astype(jnp.float32)
-    kern = jnp.dot(
-        onehot.reshape(-1, nplanes),
-        kernels,
-        precision=lax.Precision.HIGHEST,
-        preferred_element_type=jnp.float32,
-    )
-    kern = kern.reshape(planes.shape + (width,))
-    kern_re = kern[..., :half]
-    kern_im = kern[..., half:]
-    part_re = vis_re[..., None] * kern_re - vis_im[..., None] * kern_im
-    part_im = vis_re[..., None] * kern_im + vis_im[..., None] * kern_re
-    return jnp.concatenate([part_re, part_im], axis=-1).astype(jnp.bfloat16)
-
-
 def split3(values):
     high = lax.reduce_precision(values, exponent_bits=8, mantissa_bits=7)
     rest = values - high
@@ -75,7 +54,7 @@
     return high.astype(jnp.bfloat16), middle.astype(jnp.bfloat16), low.astype(jnp.bfloat16)
 
 
-def grid_kernel(fld_ref, eye_ref, kt_ref, xv_ref, xu_ref, e_ref, out_ref, rep_ref, x_ref, r_ref, tab_ref):
+def grid_kernel(fld_ref, eye_ref, kt_ref, xv_ref, xu_ref, out_ref, rep_ref, x_ref, r_ref, tab_ref):
     chunk_step = pl.program_id(1)
     chunk = fld_ref.shape[2]
     rows = out_ref.shape[1]
@@ -101,7 +80,7 @@
     onehot = (planes == lax.broadcasted_iota(jnp.int32, (chunk, nplanes), 1)).astype(jnp.bfloat16)
     parts = jnp.dot(onehot, kt_ref[...], preferred_element_type=jnp.float32)
     kern_a = (parts[:, 0:width] + parts[:, width:2 * width]) + parts[:, 2 * width:3 * width]
-    kern_b = (parts[:, 3 * width:4 * width] + parts[:, 4 * width:5 * width]) + parts[:, 5 * width:6 * width]
+    kern_b = pltpu.roll(kern_a, width // 2, 1)
     lane = lax.broadcasted_iota(jnp.int32, (chunk, width), 1)
     signed_im = jnp.where(lane < width // 2, -vis_im, vis_im)
     weighted = (vis_re * kern_a + signed_im * kern_b).astype(jnp.bfloat16)
@@ -169,17 +148,11 @@
     width = kernels.shape[1]
     half = width // 2
     nblocks = width // SUPPORT
-    lanes_in = lax.broadcasted_iota(jnp.int32, (width, nblocks * TILE), 0)
-    lanes_out = lax.broadcasted_iota(jnp.int32, (width, nblocks * TILE), 1)
-    expand = (
-        (lanes_in // SUPPORT == lanes_out // TILE) & (lanes_in % SUPPORT == lanes_out % SUPPORT)
-    ).astype(jnp.bfloat16)
     eye = (
         lax.broadcasted_iota(jnp.int32, (chunk, chunk), 0)
         == lax.broadcasted_iota(jnp.int32, (chunk, chunk), 1)
     ).astype(jnp.bfloat16)
-    swapped = jnp.concatenate([kernels[:, half:], kernels[:, :half]], axis=1)
-    table = jnp.concatenate(split3(kernels) + split3(swapped), axis=1)
+    table = jnp.concatenate(split3(kernels), axis=1)
     n_in = lax.broadcasted_iota(jnp.int32, (chunk, TILE), 0) % GROUP
     lane_t = lax.broadcasted_iota(jnp.int32, (chunk, TILE), 1)
     expand_v = (n_in == lane_t // SUPPORT).astype(jnp.bfloat16)
@@ -194,7 +167,6 @@
             pl.BlockSpec(table.shape, whole),
             pl.BlockSpec((chunk, TILE), whole),
             pl.BlockSpec((chunk, TILE), whole),
-            pl.BlockSpec((width, nblocks * TILE), whole),
         ],
         out_specs=pl.BlockSpec((2, rows, TILE), lambda d, c: (0, 0, d)),
         out_shape=jax.ShapeDtypeStruct((2, rows, dests * TILE), jnp.float32),
@@ -207,7 +179,7 @@
         compiler_params=pltpu.CompilerParams(
             dimension_semantics=("arbitrary", "arbitrary")
         ),
-    )(fld, eye, table, expand_v, expand_u, expand)
+    )(fld, eye, table, expand_v, expand_u)
 
 
 def shards(visibilities, tile_counts, w_plane, u_offset, v_offset, kernels):

time: 36.4 us -> 36.2 us (level)
  waiting for transfers between devices: 3.33 us -> 4.48 us
  other arithmetic: 4.64 us -> 3.88 us
    all_to_all x1, waiting for transfers between devices: 2.84 us -> 3.98 us  [shards(): got = lax.all_to_all(send, axes, split_axis=0, concat_axis=0, tiled=True)]
    convert_element_type x1 -> x0, other arithmetic: 1.05 us -> none  [grid_rows(): expand = ((lanes_in // SUPPORT == lanes_out // TILE) & (lanes_in % SUPPOR...]
    concatenate x1, other arithmetic: 0.09 us -> 0.63 us  [grid_rows(): table = jnp.concatenate(split3(kernels), axis=1)]
    unnamed x14 -> x12, local copies, waits for them, and re-layouts: 3.63 us -> 3.38 us
  transfers between devices with their start and end apart: 2 -> 2, of which waited for: 2 -> 2; matrix products, arithmetic and copies ran while one was open for 12% -> 10% of each run, Pallas kernels for 0% -> 0%
where the time goes in v11:
time: 36.2 us; the launch traced here: 35.7 us
  Pallas kernels  9.45 us (26%)
  local copies, waits for them, and re-layouts  9.3 us (26%)
  starting transfers between devices  7.48 us (21%)
  waiting for transfers between devices  4.48 us (12%)
  other arithmetic  3.88 us (11%)
  matrix products  0.82 us (2%)
    pallas_call x1, Pallas kernels, grid_rows(): pl.pallas_call(grid_kernel, grid=(dests, steps), in_specs=[pl.BlockSpec((...  9.45 us
    all_to_all x1, starting transfers between devices, shards(): got = lax.all_to_all(send, axes, split_axis=0, concat_axis=0, tiled=True)  7.3 us
    all_to_all x1, waiting for transfers between devices, shards(): got = lax.all_to_all(send, axes, split_axis=0, concat_axis=0, tiled=True)  3.98 us
    unnamed x12, local copies, waits for them, and re-layouts  3.38 us
    reshape x1, local copies, waits for them, and re-layouts, transform(): return final.reshape(nrows, 2, total)  1.14 us
    convert_element_type x1, other arithmetic, grid_rows(): expand_u = (n_in == lane_t % GROUP).astype(jnp.bfloat16)  0.9 us
    all_to_all x2, local copies, waits for them, and re-layouts, shards(): got = lax.all_to_all(send, axes, split_axis=0, concat_axis=0, tiled=True)  0.85 us
    slice x1, local copies, waits for them, and re-layouts, shards(): visibilities[1, 0] * live  0.83 us
  transfers between devices with their start and end apart: 2, of which 2 were waited for; matrix products, arithmetic and copies ran while one was open for 10% of the time, Pallas kernels for 0%

profile of v11, /device:TPU:0, one launch (start us, length us, event | category | flops | bytes accessed | tf_op | source)
XLA Modules:
  0.0 35.7 jit_solution(1031531988706775698)
XLA Ops:
  0.0 0.8 %fusion.49 = (f32[1,1,8,16,12]{3,2,4,1,0:T(8,128)S(1)}, f32[1,1,8,16,12]{3,2,4,1,0:T(8,128)S(1)}) fusion(f32[2,1,8,16,12]{3,2,4,1,0:T(8,128)} %param.6), kind=kLoop, calls=%fused_computation.94 | loop fusion | bytes 24576 | tf_op jit(solution)/shard_map/slice | solution.py:202
  1.1 0.5 %copy-done.5 = s32[1,8,16]{2,1,0:T(8,128)S(1)} copy-done((s32[1,8,16]{2,1,0:T(8,128)S(1)}, s32[1,8,16]{2,1,0:T(8,128)}, u32[]{:S(2)}) %copy-start.5) | copy-done | bytes 536
  1.9 0.7 %copy-done.2 = s32[1,8,16,12]{2,1,3,0:T(8,128)S(1)} copy-done((s32[1,8,16,12]{2,1,3,0:T(8,128)S(1)}, s32[1,8,16,12]{2,1,3,0:T(8,128)}, u32[]{:S(2)}) %copy-start.2) | copy-done | bytes 6168
  2.7 0.7 %copy-done.3 = s32[1,8,16,12]{2,1,3,0:T(8,128)S(1)} copy-done((s32[1,8,16,12]{2,1,3,0:T(8,128)S(1)}, s32[1,8,16,12]{2,1,3,0:T(8,128)}, u32[]{:S(2)}) %copy-start.3) | copy-done | bytes 6168
  3.6 0.3 concatenate.10
  3.9 0.7 %all_to_all.8 = f32[32,1,240]{2,1,0:T(1,128)} reshape(f32[16,2,4,60]{3,2,1,0:T(4,128)S(1)} %bitcast.51) | data formatting | bytes 61440 | tf_op jit(solution)/shard_map/all_to_all | solution.py:211
  4.7 7.3 %all-to-all-start = ((f32[32,1,240]{2,1,0:T(1,128)}), f32[32,1,240]{2,1,0:T(1,128)S(1)}, u32[]{:S(2)}, u32[]{:S(2)}) async-start(f32[32,1,240]{2,1,0:T(1,128)} %all_to_all.8), calls=%async_computation | async-start | bytes 65536 | tf_op jit(solution)/shard_map/all_to_all | solution.py:211
  12.1 0.7 %fusion.eye_ref = bf16[384,384]{1,0:T(8,128)(2,1)} fusion(), kind=kLoop, calls=%fused_computation.3 | loop fusion | flops 294912 | bytes 294912 | tf_op jit(solution)/shard_map/convert_element_type | solution.py:154
  12.9 0.3 fusion.22
  13.2 0.5 %copy-done.4 = f32[64,128]{1,0:T(8,128)S(1)} copy-done((f32[64,128]{1,0:T(8,128)S(1)}, f32[64,128]{1,0:T(8,128)}, u32[]{:S(2)}) %copy-start.4) | copy-done | bytes 32792
  13.7 0.6 %pad_maximum_fusion.2.kt_ref = bf16[64,384]{1,0:T(8,128)(2,1)} fusion(bf16[64,128]{1,0:T(8,128)(2,1)S(1)} %get-tuple-element.17, bf16[64,128]{1,0:T(8,128)(2,1)S(1)} %get-tuple-element.18, bf16[64,128]{1,0:T(8,128)(2,1)S(1)} %get-tuple-element.16), kind=kLoop, calls=%fused_computation.40 | loop fusion | flops 147456 | bytes 98304 | tf_op jit(solution)/shard_map/concatenate | solution.py:155
  14.3 0.9 %fusion.8 = (bf16[384,128]{1,0:T(8,128)(2,1)}, bf16[384,128]{1,0:T(8,128)(2,1)}) fusion(s32[128]{0:T(128)S(1)} %get-tuple-element.30, s32[128]{0:T(128)S(1)} %get-tuple-element.31, s32[384]{0:T(512)S(1)} %get-tuple-element.27, s32[384]{0:T(512)S(1)} %get-tuple-element.28, pred[384]{0:T(512)(128)(4,1)S(1)} %fusion.44, ...), kind=kLoop, calls=%fused_computation.18 | loop fusion | flops 344064 | bytes 202368 | tf_op jit(solution)/shard_map/convert_element_type | solution.py:159
  15.2 4.0 %all-to-all-done = f32[32,1,240]{2,1,0:T(1,128)S(1)} async-done(((f32[32,1,240]{2,1,0:T(1,128)}), f32[32,1,240]{2,1,0:T(1,128)S(1)}, u32[]{:S(2)}, u32[]{:S(2)}) %all-to-all-start) | async-done | bytes 30752 | tf_op jit(solution)/shard_map/all_to_all | solution.py:211
  19.8 0.6 %pad_maximum_fusion.1.fld_ref = bf16[4,24,384]{2,1,0:T(8,128)(2,1)} fusion(bf16[4,8,384]{2,1,0:T(8,128)(2,1)S(1)} %get-tuple-element.14, bf16[4,8,384]{2,1,0:T(8,128)(2,1)S(1)} %get-tuple-element.15, bf16[4,8,384]{2,1,0:T(8,128)(2,1)S(1)} %get-tuple-element.13), kind=kLoop, calls=%fused_computation.25 | loop fusion | flops 221184 | bytes 147456 | tf_op jit(solution)/shard_map/concatenate | solution.py:215
  20.4 9.5 %shard_map.64 = f32[2,128,512]{2,1,0:T(8,128)} custom-call(bf16[4,24,384]{2,1,0:T(8,128)(2,1)} %pad_maximum_fusion.1.fld_ref, bf16[384,384]{1,0:T(8,128)(2,1)} %fusion.eye_ref, bf16[64,384]{1,0:T(8,128)(2,1)} %pad_maximum_fusion.2.kt_ref, bf16[384,128]{1,0:T(8,128)(2,1)} %get-tuple-element.22.xv_ref, bf16[384,128]{1,0:T(8,128)(2,1)} %get-tuple-element.21.xu_ref), custom_call_target="tpu_custom_call" | custom-call | tf_op jit(solution)/shard_map/pallas_call | solution.py:161
  29.9 1.0 %copy-done = f32[2,128,512]{2,1,0:T(8,128)S(1)} copy-done((f32[2,128,512]{2,1,0:T(8,128)S(1)}, f32[2,128,512]{2,1,0:T(8,128)}, u32[]{:S(2)}) %copy-start) | copy-done | bytes 524312
  31.3 0.3 fusion.20
  31.6 0.4 %copy.43 = f32[2,64,1024]{2,0,1:T(2,128)S(1)} copy(f32[2,64,1024]{2,1,0:T(8,128)S(1)} %get-tuple-element.8) | data formatting | bytes 1048576 | tf_op jit(solution)/shard_map/dynamic_update_slice | solution.py:220
  32.0 0.5 %collective-permute-done = f32[2,64,512]{2,1,0:T(8,128)S(1)} collective-permute-done((f32[2,64,512]{2,1,0:T(8,128)S(1)}, f32[2,64,512]{2,1,0:T(8,128)S(1)}, u32[]{:S(2)}, u32[]{:S(2)}) %collective-permute-start) | collective-permute-done | bytes 262176 | tf_op jit(solution)/shard_map/ppermute | solution.py:229
  32.8 0.4 %reshape.195 = f32[2,64,8,128,1]{3,2,0,1,4:T(8,128)S(1)} reshape(f32[2,64,1024]{2,0,1:T(2,128)S(1)} %copy_dynamic-update-slice_fusion) | data formatting | bytes 1048576 | tf_op jit(solution)/shard_map/reshape | solution.py:40
  33.2 0.4 %convolution_bitcast_fusion.1 = f32[2,64,8,128]{3,2,1,0:T(8,128)S(1)} fusion(f32[2,64,8,128,1]{3,2,0,1,4:T(8,128)S(1)} %reshape.195, f32[1,8,2,8]{1,3,0,2:T(8,128)S(1)} %copy.32, f32[1,8,2,8]{1,3,0,2:T(8,128)S(1)} %copy.31), kind=kOutput, calls=%fused_computation.1 | convolution fusion | flops 12583168 | bytes 1049600 | tf_op jit(solution)/shard_map/crpj,cpdk->drkj/dot_general | solution.py:39
  33.7 0.4 %convolution_bitcast_fusion = f32[64,2,128,8]{2,0,3,1:T(8,128)S(1)} fusion(f32[2,64,8,128]{3,2,1,0:T(8,128)S(1)} %pad_maximum_fusion, f32[1,128,2,128]{3,1,0,2:T(8,128)S(1)} %get-tuple-element.12, f32[1,128,2,128]{3,1,0,2:T(8,128)S(1)} %get-tuple-element.11), kind=kOutput, calls=%fused_computation | convolution fusion | flops 201457664 | bytes 1310720 | tf_op jit(solution)/shard_map/drkj,djem->remk/dot_general | solution.py:45
  34.1 0.4 %copy.46 = f32[64,2,128,8]{0,3,2,1:T(8,128)S(1)} copy(f32[64,2,128,8]{2,0,3,1:T(8,128)S(1)} %convolution_bitcast_fusion) | data formatting | bytes 1048576 | tf_op jit(solution)/shard_map/drkj,djem->remk/transpose | solution.py:45
  34.5 1.1 %copy.47 = f32[64,2,1024]{2,1,0:T(2,128)} copy(f32[64,2,1024]{0,2,1:T(8,128)S(1)} %bitcast.49) | data formatting | bytes 1048576 | tf_op jit(solution)/shard_map/reshape | solution.py:46
  (41 shorter events, 2.4 us)
Async XLA Ops:
  1.0 0.7 %copy-start.5 = (s32[1,8,16]{2,1,0:T(8,128)S(1)}, s32[1,8,16]{2,1,0:T(8,128)}, u32[]{:S(2)}) copy-start(s32[1,8,16]{2,1,0:T(8,128)} %param.7) | copy-start | bytes 1540
  1.0 0.8 %copy-start.1 = (s32[1,8,16,12]{2,1,3,0:T(8,128)S(1)}, s32[1,8,16,12]{2,1,3,0:T(8,128)}, u32[]{:S(2)}) copy-start(s32[1,8,16,12]{2,1,3,0:T(8,128)} %param.8) | copy-start | bytes 18436
  1.8 0.8 %copy-start.2 = (s32[1,8,16,12]{2,1,3,0:T(8,128)S(1)}, s32[1,8,16,12]{2,1,3,0:T(8,128)}, u32[]{:S(2)}) copy-start(s32[1,8,16,12]{2,1,3,0:T(8,128)} %param.9) | copy-start | bytes 18436
  2.6 0.8 %copy-start.3 = (s32[1,8,16,12]{2,1,3,0:T(8,128)S(1)}, s32[1,8,16,12]{2,1,3,0:T(8,128)}, u32[]{:S(2)}) copy-start(s32[1,8,16,12]{2,1,3,0:T(8,128)} %param.10) | copy-start | bytes 18436
  4.7 14.6 %all-to-all-start = ((f32[32,1,240]{2,1,0:T(1,128)}), f32[32,1,240]{2,1,0:T(1,128)S(1)}, u32[]{:S(2)}, u32[]{:S(2)}) async-start(f32[32,1,240]{2,1,0:T(1,128)} %all_to_all.8), calls=%async_computation | async-start | bytes 65536 | tf_op jit(solution)/shard_map/all_to_all | solution.py:211
  12.9 0.8 %copy-start.4 = (f32[64,128]{1,0:T(8,128)S(1)}, f32[64,128]{1,0:T(8,128)}, u32[]{:S(2)}) copy-start(f32[64,128]{1,0:T(8,128)} %param.11) | copy-start | bytes 98308
  29.9 1.0 %copy-start = (f32[2,128,512]{2,1,0:T(8,128)S(1)}, f32[2,128,512]{2,1,0:T(8,128)}, u32[]{:S(2)}) copy-start(f32[2,128,512]{2,1,0:T(8,128)} %shard_map.64) | copy-start | bytes 1572868
  30.9 1.6 %collective-permute-start = (f32[2,64,512]{2,1,0:T(8,128)S(1)}, f32[2,64,512]{2,1,0:T(8,128)S(1)}, u32[]{:S(2)}, u32[]{:S(2)}) collective-permute-start(f32[2,64,512]{2,1,0:T(8,128)S(1)} %get-tuple-element.7), channel_id=1, source_target_pairs={{0,1},{1,0},{2,3},{3,2},{4,5},{5,4},{6,7},{7,6},{8,9},{9,8},{10,11... | collective-permute-start | bytes 786440 | tf_op jit(solution)/shard_map/ppermute | solution.py:229

commit v12 on v11

--- a/solution.py
+++ b/solution.py
@@ -54,10 +54,14 @@
     return high.astype(jnp.bfloat16), middle.astype(jnp.bfloat16), low.astype(jnp.bfloat16)
 
 
-def grid_kernel(fld_ref, eye_ref, kt_ref, xv_ref, xu_ref, out_ref, rep_ref, x_ref, r_ref, tab_ref):
+def grid_kernel(*refs):
+    if len(refs) == 11:
+        member_ref, fld_ref, eye_ref, kt_ref, xv_ref, xu_ref, out_ref, other_ref, rep_ref, x_ref, r_ref, tab_ref = (None,) + refs
+    else:
+        member_ref, fld_ref, eye_ref, kt_ref, xv_ref, xu_ref, out_ref, other_ref, rep_ref, x_ref, r_ref, tab_ref = refs
     chunk_step = pl.program_id(1)
     chunk = fld_ref.shape[2]
-    rows = out_ref.shape[1]
+    rows = r_ref.shape[0]
     ngroups = chunk // GROUP
     width = 2 * SUPPORT * SUPPORT
     nblocks = width // SUPPORT
@@ -67,6 +71,7 @@
     @pl.when(chunk_step == 0)
     def _():
         out_ref[...] = jnp.zeros_like(out_ref)
+        other_ref[...] = jnp.zeros_like(other_ref)
 
     fld = fld_ref[0]
     cols = lax.dot_general(
@@ -131,12 +136,20 @@
         return carry
 
     lax.fori_loop(0, ngroups, body, 0, unroll=True)
-    pick = r_ref[...]
-    out_ref[0] += jnp.dot(pick, x_ref[0], preferred_element_type=jnp.float32)
-    out_ref[1] += jnp.dot(pick, x_ref[1], preferred_element_type=jnp.float32)
-
-
-def grid_rows(fld, kernels, rows):
+    if member_ref is None:
+        pick = r_ref[...]
+        out_ref[0] += jnp.dot(pick, x_ref[0], preferred_element_type=jnp.float32)
+        out_ref[1] += jnp.dot(pick, x_ref[1], preferred_element_type=jnp.float32)
+    else:
+        part = out_ref.shape[1]
+        member = member_ref[0]
+        for target, sel in ((out_ref, member), (other_ref, 1 - member)):
+            pick = r_ref[pl.ds(pl.multiple_of(sel * part, part), part), :]
+            target[0] += jnp.dot(pick, x_ref[0], preferred_element_type=jnp.float32)
+            target[1] += jnp.dot(pick, x_ref[1], preferred_element_type=jnp.float32)
+
+
+def grid_rows(fld, kernels, rows, member=None, full_dests=None):
     dests, nf, per_dest = fld.shape
     chunk = per_dest
     for size in (384, 192, 96, 48, 16):
@@ -158,28 +171,64 @@
     expand_v = (n_in == lane_t // SUPPORT).astype(jnp.bfloat16)
     expand_u = (n_in == lane_t % GROUP).astype(jnp.bfloat16)
     whole = lambda d, c: (0, 0)
-    return pl.pallas_call(
-        grid_kernel,
+    scratch = [
+        pltpu.VMEM((chunk, width), jnp.float32),
+        pltpu.VMEM((2, chunk * SUPPORT, TILE), jnp.bfloat16),
+        pltpu.VMEM((rows, chunk * SUPPORT), jnp.bfloat16),
+        pltpu.VMEM((2, ngroups, TILE), jnp.int32),
+    ]
+    params = pltpu.CompilerParams(dimension_semantics=("arbitrary", "arbitrary"))
+    operands = (fld, eye, table, expand_v, expand_u)
+    if member is None:
+        whole = lambda d, c: (0, 0)
+        return pl.pallas_call(
+            grid_kernel,
+            grid=(dests, steps),
+            in_specs=[
+                pl.BlockSpec((1, nf, chunk), lambda d, c: (d, 0, c)),
+                pl.BlockSpec((chunk, chunk), whole),
+                pl.BlockSpec(table.shape, whole),
+                pl.BlockSpec((chunk, TILE), whole),
+                pl.BlockSpec((chunk, TILE), whole),
+            ],
+            out_specs=[
+                pl.BlockSpec((2, rows, TILE), lambda d, c: (0, 0, d)),
+                pl.BlockSpec((2, SUPPORT, TILE), lambda d, c: (0, 0, 0)),
+            ],
+            out_shape=[
+                jax.ShapeDtypeStruct((2, rows, dests * TILE), jnp.float32),
+                jax.ShapeDtypeStruct((2, SUPPORT, TILE), jnp.float32),
+            ],
+            scratch_shapes=scratch,
+            compiler_params=params,
+        )(*operands)[0]
+    part = rows // 2
+    whole = lambda d, c, m: (0, 0)
+    grid_spec = pltpu.PrefetchScalarGridSpec(
+        num_scalar_prefetch=1,
         grid=(dests, steps),
         in_specs=[
-            pl.BlockSpec((1, nf, chunk), lambda d, c: (d, 0, c)),
+            pl.BlockSpec((1, nf, chunk), lambda d, c, m: (d, 0, c)),
             pl.BlockSpec((chunk, chunk), whole),
             pl.BlockSpec(table.shape, whole),
             pl.BlockSpec((chunk, TILE), whole),
             pl.BlockSpec((chunk, TILE), whole),
         ],
-        out_specs=pl.BlockSpec((2, rows, TILE), lambda d, c: (0, 0, d)),
-        out_shape=jax.ShapeDtypeStruct((2, rows, dests * TILE), jnp.float32),
-        scratch_shapes=[
-            pltpu.VMEM((chunk, width), jnp.float32),
-            pltpu.VMEM((2, chunk * SUPPORT, TILE), jnp.bfloat16),
-            pltpu.VMEM((rows, chunk * SUPPORT), jnp.bfloat16),
-            pltpu.VMEM((2, ngroups, TILE), jnp.int32),
-        ],
-        compiler_params=pltpu.CompilerParams(
-            dimension_semantics=("arbitrary", "arbitrary")
-        ),
-    )(fld, eye, table, expand_v, expand_u)
+        out_specs=[
+            pl.BlockSpec((2, part, TILE), lambda d, c, m: (0, 0, m[0] * dests + d)),
+            pl.BlockSpec((2, part, TILE), lambda d, c, m: (0, 0, d)),
+        ],
+        scratch_shapes=scratch,
+    )
+    return pl.pallas_call(
+        grid_kernel,
+        grid_spec=grid_spec,
+        out_shape=[
+            jax.ShapeDtypeStruct((2, part, full_dests * TILE), jnp.float32),
+            jax.ShapeDtypeStruct((2, part, dests * TILE), jnp.float32),
+        ],
+        compiler_params=params,
+    )(member.reshape(1), *operands)
 
 
 def shards(visibilities, tile_counts, w_plane, u_offset, v_offset, kernels):
@@ -213,8 +262,13 @@
     got = got.reshape(own_dests, FIELDS, ndev * slots)
     got = jnp.pad(got, ((0, 0), (0, 8 - FIELDS), (0, 0)))
     got = jnp.concatenate(split3(got), axis=1)
+    width = own_dests * TILE
+    if per_tile == 2:
+        full, other = grid_rows(got, kernels, TILE, member.astype(jnp.int32), dests)
+        other = lax.ppermute(other, axes, [(k, k ^ 1) for k in range(ndev)])
+        full = lax.dynamic_update_slice_in_dim(full, other, (1 - member) * width, axis=2)
+        return transform(full, dests)
     slab = grid_rows(got, kernels, TILE)
-    width = own_dests * TILE
     mine = lax.dynamic_slice_in_dim(slab, member * rows, rows, axis=1)
     full = jnp.zeros((2, rows, dests * TILE), jnp.float32)
     full = lax.dynamic_update_slice_in_dim(full, mine, member * width, axis=2)

time: 36.2 us -> 35.5 us (0.981)
  local copies, waits for them, and re-layouts: 9.3 us -> 7.31 us
  Pallas kernels: 9.45 us -> 10.2 us
  waiting for transfers between devices: 4.48 us -> 5.14 us
    unnamed x12 -> x13, local copies, waits for them, and re-layouts: 3.38 us -> 2.49 us
    pallas_call x1, Pallas kernels: 9.45 us -> 10.2 us  [grid_rows(): pl.pallas_call(grid_kernel, grid_spec=grid_spec, out_shape=[jax.ShapeDtyp...]
    ppermute x1, waiting for transfers between devices: 0.5 us -> 1.12 us  [shards(): other = lax.ppermute(other, axes, [(k, k ^ 1) for k in range(ndev)])]
    dynamic_update_slice x2 -> x1, local copies, waits for them, and re-layouts: 0.62 us -> 0.02 us  [shards(): lax.dynamic_update_slice_in_dim(full, other, (1 - member) * width, axis=2)]
    reshape x1 -> x0, local copies, waits for them, and re-layouts: 0.42 us -> none  [transform(): field.reshape(2, nrows, groups, width)]
  transfers between devices with their start and end apart: 2 -> 2, of which waited for: 2 -> 2; matrix products, arithmetic and copies ran while one was open for 10% -> 9% of each run, Pallas kernels for 0% -> 0%
where the time goes in v12:
time: 35.5 us; the launch traced here: 35 us
  Pallas kernels  10.2 us (29%)
  starting transfers between devices  7.41 us (21%)
  local copies, waits for them, and re-layouts  7.31 us (21%)
  waiting for transfers between devices  5.14 us (14%)
  other arithmetic  3.89 us (11%)
  matrix products  0.82 us (2%)
    pallas_call x1, Pallas kernels, grid_rows(): pl.pallas_call(grid_kernel, grid_spec=grid_spec, out_shape=[jax.ShapeDtyp...  10.2 us
    all_to_all x1, starting transfers between devices, shards(): got = lax.all_to_all(send, axes, split_axis=0, concat_axis=0, tiled=True)  7.3 us
    all_to_all x1, waiting for transfers between devices, shards(): got = lax.all_to_all(send, axes, split_axis=0, concat_axis=0, tiled=True)  4.01 us
    unnamed x13, local copies, waits for them, and re-layouts  2.49 us
    reshape x1, local copies, waits for them, and re-layouts, transform(): return final.reshape(nrows, 2, total)  1.14 us
    ppermute x1, waiting for transfers between devices, shards(): other = lax.ppermute(other, axes, [(k, k ^ 1) for k in range(ndev)])  1.12 us
    convert_element_type x1, other arithmetic, grid_rows(): expand_u = (n_in == lane_t % GROUP).astype(jnp.bfloat16)  0.9 us
    all_to_all x2, local copies, waits for them, and re-layouts, shards(): got = lax.all_to_all(send, axes, split_axis=0, concat_axis=0, tiled=True)  0.85 us
  transfers between devices with their start and end apart: 2, of which 2 were waited for; matrix products, arithmetic and copies ran while one was open for 9% of the time, Pallas kernels for 0%

profile of v12, /device:TPU:0, one launch (start us, length us, event | category | flops | bytes accessed | tf_op | source)
XLA Modules:
  0.0 35.0 jit_solution(8192120280453840509)
XLA Ops:
  0.0 0.8 %fusion.51 = (f32[1,1,8,16,12]{3,2,4,1,0:T(8,128)S(1)}, f32[1,1,8,16,12]{3,2,4,1,0:T(8,128)S(1)}) fusion(f32[2,1,8,16,12]{3,2,4,1,0:T(8,128)} %param.6), kind=kLoop, calls=%fused_computation.94 | loop fusion | bytes 24576 | tf_op jit(solution)/shard_map/slice | solution.py:251
  1.1 0.5 %copy-done.5 = s32[1,8,16]{2,1,0:T(8,128)S(1)} copy-done((s32[1,8,16]{2,1,0:T(8,128)S(1)}, s32[1,8,16]{2,1,0:T(8,128)}, u32[]{:S(2)}) %copy-start.5) | copy-done | bytes 536
  1.9 0.7 %copy-done.2 = s32[1,8,16,12]{2,1,3,0:T(8,128)S(1)} copy-done((s32[1,8,16,12]{2,1,3,0:T(8,128)S(1)}, s32[1,8,16,12]{2,1,3,0:T(8,128)}, u32[]{:S(2)}) %copy-start.2) | copy-done | bytes 6168
  2.7 0.7 %copy-done.3 = s32[1,8,16,12]{2,1,3,0:T(8,128)S(1)} copy-done((s32[1,8,16,12]{2,1,3,0:T(8,128)S(1)}, s32[1,8,16,12]{2,1,3,0:T(8,128)}, u32[]{:S(2)}) %copy-start.3) | copy-done | bytes 6168
  3.4 0.1 copy.36
  3.6 0.3 concatenate.10
  3.9 0.7 %all_to_all.8 = f32[32,1,240]{2,1,0:T(1,128)} reshape(f32[16,2,4,60]{3,2,1,0:T(4,128)S(1)} %bitcast.64) | data formatting | bytes 61440 | tf_op jit(solution)/shard_map/all_to_all | solution.py:260
  4.7 7.3 %all-to-all-start = ((f32[32,1,240]{2,1,0:T(1,128)}), f32[32,1,240]{2,1,0:T(1,128)S(1)}, u32[]{:S(2)}, u32[]{:S(2)}) async-start(f32[32,1,240]{2,1,0:T(1,128)} %all_to_all.8), calls=%async_computation | async-start | bytes 65536 | tf_op jit(solution)/shard_map/all_to_all | solution.py:260
  12.0 0.7 %fusion.refs_2_ = bf16[384,384]{1,0:T(8,128)(2,1)} fusion(), kind=kLoop, calls=%fused_computation.3 | loop fusion | flops 294912 | bytes 294912 | tf_op jit(solution)/shard_map/convert_element_type | solution.py:167
  12.9 0.3 fusion.24
  13.2 0.5 %copy-done.4 = f32[64,128]{1,0:T(8,128)S(1)} copy-done((f32[64,128]{1,0:T(8,128)S(1)}, f32[64,128]{1,0:T(8,128)}, u32[]{:S(2)}) %copy-start.4) | copy-done | bytes 32792
  13.7 0.6 %pad_maximum_fusion.2.refs_3_ = bf16[64,384]{1,0:T(8,128)(2,1)} fusion(bf16[64,128]{1,0:T(8,128)(2,1)S(1)} %get-tuple-element.19, bf16[64,128]{1,0:T(8,128)(2,1)S(1)} %get-tuple-element.20, bf16[64,128]{1,0:T(8,128)(2,1)S(1)} %get-tuple-element.18), kind=kLoop, calls=%fused_computation.40 | loop fusion | flops 147456 | bytes 98304 | tf_op jit(solution)/shard_map/concatenate | solution.py:168
  14.3 0.9 %fusion.10 = (bf16[384,128]{1,0:T(8,128)(2,1)}, bf16[384,128]{1,0:T(8,128)(2,1)}) fusion(s32[128]{0:T(128)S(1)} %get-tuple-element.32, s32[128]{0:T(128)S(1)} %get-tuple-element.33, s32[384]{0:T(512)S(1)} %get-tuple-element.27, s32[384]{0:T(512)S(1)} %get-tuple-element.28, pred[384]{0:T(512)(128)(4,1)S(1)} %fusion.46, ...), kind=kLoop, calls=%fused_computation.18 | loop fusion | flops 344064 | bytes 202368 | tf_op jit(solution)/shard_map/convert_element_type | solution.py:172
  15.2 4.0 %all-to-all-done = f32[32,1,240]{2,1,0:T(1,128)S(1)} async-done(((f32[32,1,240]{2,1,0:T(1,128)}), f32[32,1,240]{2,1,0:T(1,128)S(1)}, u32[]{:S(2)}, u32[]{:S(2)}) %all-to-all-start) | async-done | bytes 30752 | tf_op jit(solution)/shard_map/all_to_all | solution.py:260
  19.3 0.2 copy.49
  19.5 0.2 reshape.204
  19.8 0.6 %pad_maximum_fusion.1.refs_1_ = bf16[4,24,384]{2,1,0:T(8,128)(2,1)} fusion(bf16[4,8,384]{2,1,0:T(8,128)(2,1)S(1)} %get-tuple-element.16, bf16[4,8,384]{2,1,0:T(8,128)(2,1)S(1)} %get-tuple-element.17, bf16[4,8,384]{2,1,0:T(8,128)(2,1)S(1)} %get-tuple-element.15), kind=kLoop, calls=%fused_computation.25 | loop fusion | flops 221184 | bytes 147456 | tf_op jit(solution)/shard_map/concatenate | solution.py:264
  20.4 10.2 %shard_map.64 = (f32[2,64,1024]{2,1,0:T(8,128)}, f32[2,64,512]{2,1,0:T(8,128)}) custom-call(s32[1]{0:T(128)} %bitcast.9.refs_0_, bf16[4,24,384]{2,1,0:T(8,128)(2,1)} %pad_maximum_fusion.1.refs_1_, bf16[384,384]{1,0:T(8,128)(2,1)} %fusion.refs_2_, bf16[64,384]{1,0:T(8,128)(2,1)} %pad_maximum_fusion.2.refs_3_, bf16[384,128]{1,0:T(8,128)(2,1)} %get-tuple-element.24.refs_4_, ...), custom_call_target="tpu_custom_call" | custom-call | tf_op jit(solution)/shard_map/pallas_call | solution.py:223
  31.0 0.3 fusion.22
  31.3 1.1 %collective-permute-done = f32[2,64,512]{2,1,0:T(8,128)S(1)} collective-permute-done((f32[2,64,512]{2,1,0:T(8,128)}, f32[2,64,512]{2,1,0:T(8,128)S(1)}, u32[]{:S(2)}, u32[]{:S(2)}) %collective-permute-start) | collective-permute-done | bytes 262176 | tf_op jit(solution)/shard_map/ppermute | solution.py:268
  32.5 0.4 %convolution_bitcast_fusion.1 = f32[2,64,8,128]{3,2,1,0:T(8,128)S(1)} fusion(f32[1,8,2,8]{1,3,0,2:T(8,128)S(1)} %copy.30, f32[1,8,2,8]{1,3,0,2:T(8,128)S(1)} %copy.29, f32[2,64,8,128]{3,2,1,0:T(8,128)S(1)} %bitcast.61), kind=kOutput, calls=%fused_computation.1 | convolution fusion | flops 12583168 | bytes 1049600 | tf_op jit(solution)/shard_map/crpj,cpdk->drkj/dot_general | solution.py:39
  33.1 0.4 %convolution_bitcast_fusion = f32[64,2,128,8]{2,0,3,1:T(8,128)S(1)} fusion(f32[2,64,8,128]{3,2,1,0:T(8,128)S(1)} %pad_maximum_fusion, f32[1,128,2,128]{3,1,0,2:T(8,128)S(1)} %get-tuple-element.14, f32[1,128,2,128]{3,1,0,2:T(8,128)S(1)} %get-tuple-element.13), kind=kOutput, calls=%fused_computation | convolution fusion | flops 201457664 | bytes 1310720 | tf_op jit(solution)/shard_map/drkj,djem->remk/dot_general | solution.py:45
  33.5 0.4 %copy.43 = f32[64,2,128,8]{0,3,2,1:T(8,128)S(1)} copy(f32[64,2,128,8]{2,0,3,1:T(8,128)S(1)} %convolution_bitcast_fusion) | data formatting | bytes 1048576 | tf_op jit(solution)/shard_map/drkj,djem->remk/transpose | solution.py:45
  33.9 1.1 %copy.44 = f32[64,2,1024]{2,1,0:T(2,128)} copy(f32[64,2,1024]{0,2,1:T(8,128)S(1)} %bitcast.60) | data formatting | bytes 1048576 | tf_op jit(solution)/shard_map/reshape | solution.py:46
  (38 shorter events, 1.6 us)
Async XLA Ops:
  1.0 0.7 %copy-start.5 = (s32[1,8,16]{2,1,0:T(8,128)S(1)}, s32[1,8,16]{2,1,0:T(8,128)}, u32[]{:S(2)}) copy-start(s32[1,8,16]{2,1,0:T(8,128)} %param.7) | copy-start | bytes 1540
  1.0 0.8 %copy-start.1 = (s32[1,8,16,12]{2,1,3,0:T(8,128)S(1)}, s32[1,8,16,12]{2,1,3,0:T(8,128)}, u32[]{:S(2)}) copy-start(s32[1,8,16,12]{2,1,3,0:T(8,128)} %param.8) | copy-start | bytes 18436
  1.8 0.8 %copy-start.2 = (s32[1,8,16,12]{2,1,3,0:T(8,128)S(1)}, s32[1,8,16,12]{2,1,3,0:T(8,128)}, u32[]{:S(2)}) copy-start(s32[1,8,16,12]{2,1,3,0:T(8,128)} %param.9) | copy-start | bytes 18436
  2.6 0.8 %copy-start.3 = (s32[1,8,16,12]{2,1,3,0:T(8,128)S(1)}, s32[1,8,16,12]{2,1,3,0:T(8,128)}, u32[]{:S(2)}) copy-start(s32[1,8,16,12]{2,1,3,0:T(8,128)} %param.10) | copy-start | bytes 18436
  4.7 14.6 %all-to-all-start = ((f32[32,1,240]{2,1,0:T(1,128)}), f32[32,1,240]{2,1,0:T(1,128)S(1)}, u32[]{:S(2)}, u32[]{:S(2)}) async-start(f32[32,1,240]{2,1,0:T(1,128)} %all_to_all.8), calls=%async_computation | async-start | bytes 65536 | tf_op jit(solution)/shard_map/all_to_all | solution.py:260
  12.9 0.8 %copy-start.4 = (f32[64,128]{1,0:T(8,128)S(1)}, f32[64,128]{1,0:T(8,128)}, u32[]{:S(2)}) copy-start(f32[64,128]{1,0:T(8,128)} %param.11) | copy-start | bytes 98308
  30.6 1.8 %copy-start = (f32[2,64,1024]{2,1,0:T(8,128)S(1)}, f32[2,64,1024]{2,1,0:T(8,128)}, u32[]{:S(2)}) copy-start(f32[2,64,1024]{2,1,0:T(8,128)} %get-tuple-element.7) | copy-start | bytes 1572868
  30.6 1.7 %collective-permute-start = (f32[2,64,512]{2,1,0:T(8,128)}, f32[2,64,512]{2,1,0:T(8,128)S(1)}, u32[]{:S(2)}, u32[]{:S(2)}) collective-permute-start(f32[2,64,512]{2,1,0:T(8,128)} %get-tuple-element.8), channel_id=1, source_target_pairs={{0,1},{1,0},{2,3},{3,2},{4,5},{5,4},{6,7},{7,6},{8,9},{9,8},{10,11... | collective-permute-start | bytes 786440 | tf_op jit(solution)/shard_map/ppermute | solution.py:268
